TPU v7x, 128 devices: a whole 4x4x4 slice. The times are simulated.
128 devices in a mesh: sample: 8 (over x, y_hi), landmark: 16 (over z, y_lo, core).
Axes of the slice: x: 4, y: 4 (y_hi: 2, y_lo: 2; y = y_hi * 2 + y_lo), z: 4, core: 2. Of those that a mesh axis runs over, the one named last changes fastest.
Arguments:
- summaries: bfloat16 [16384, 1024], P('sample', 'landmark'), may hold values from -12 to 12
- row_level: int32 [16384], P('sample'), may hold values from 0 to 3
- pool: bfloat16 [32768, 1024], P('landmark'), may hold values from -6 to 6
- pool_level: int32 [32768], P('landmark'), may hold values from 0 to 3
- landmark_index: int32 [16384], P('landmark'), may hold values from 0 to 2047, as said below
- level_scale: float32 [4], replicated, may hold values from 1.2 to 2.4
- targets: bfloat16 [16384, 256], P('sample'), may hold values from -6 to 6
Outputs:
- weights: float32 [16384, 256], P('landmark')
- residual: float32 [16384, 256], P('landmark')
Inputs may be any that keep to these rules, and one draw needn't show every extreme that they name: Landmark j is pool row (j // 1024) * 2048 + landmark_index[j], a row of the pool block of its own landmark group; indices may repeat.
All inputs are finite; a program needn't handle non-finite values.
Results may differ from a plain program's by a relative error of at most 0.012.
Values may be sent and summed in bfloat16 or wider, within the bound.
No kernel may reach another device: no remote copies, remote signals or barrier semaphores. Data moves between devices by JAX's collectives and lax.ppermute only.
A program may use at most 64 MiB of HBM per device.

v0:
```python
import math

import jax
import jax.numpy as jnp
from jax import lax
from jax.sharding import PartitionSpec as P

ITERS = 2
GROUPS = 2


ridge = 0.5


def level_values(level_ids, level_table):
    onehot = level_ids[:, None] == jnp.arange(level_table.shape[0], dtype=jnp.int32)[None, :]
    return jnp.sum(
        jnp.where(onehot, level_table[None, :], jnp.zeros_like(level_table)[None, :]), axis=1
    )


def raw_block(summary_rows, row_factor, anchors, anchor_factor):
    scores = jnp.dot(summary_rows, anchors.T, preferred_element_type=jnp.float32)
    return jnp.exp(scores * row_factor[:, None] * anchor_factor[None, :])


def partner_bits(size, order):
    bits = [b for b in order if b < size]
    assert sorted(bits) == [1 << i for i in range(size.bit_length() - 1)]
    return bits


def butterfly_sum(x, axis, bits):
    size = lax.axis_size(axis)
    for k in bits:
        perm = [(i, i ^ k) for i in range(size)]
        x = x + lax.ppermute(x, axis, perm)
    return x


def pack_rows(extra, columns, wire_dtype):
    rows = extra.reshape(-1, columns)
    if wire_dtype == jnp.float32:
        parts = [rows]
    else:
        parts = []
        rest = rows
        for _ in range(3):
            term = rest.astype(wire_dtype)
            parts.append(term)
            rest = rest - term.astype(jnp.float32)
    return jnp.concatenate(parts, axis=0).astype(wire_dtype)


def unpack_rows(packed, count, wire_dtype):
    terms = 1 if wire_dtype == jnp.float32 else 3
    packed = packed.astype(jnp.float32).reshape(terms, count, -1)
    total = packed[0]
    for t in range(1, terms):
        total = total + packed[t]
    return total.reshape(-1)


def halving_sum(x, extra, axis, bits, gather_dtype, wire_dtype=jnp.bfloat16):
    size = lax.axis_size(axis)
    index = lax.axis_index(axis)
    columns = x.shape[1]
    for k in bits:
        perm = [(i, i ^ k) for i in range(size)]
        half = x.shape[0] // 2
        mine = (index // k) % 2
        keep = lax.dynamic_slice_in_dim(x, mine * half, half, axis=0)
        send = lax.dynamic_slice_in_dim(x, (1 - mine) * half, half, axis=0).astype(wire_dtype)
        if extra is not None:
            send = jnp.concatenate([send, pack_rows(extra, columns, wire_dtype)], axis=0)
        got = lax.ppermute(send, axis, perm)
        x = keep + got[:half].astype(jnp.float32)
        if extra is not None:
            extra = extra + unpack_rows(got[half:], extra.shape[0] // columns, wire_dtype)
    x = x.astype(gather_dtype)
    for k in reversed(bits):
        perm = [(i, i ^ k) for i in range(size)]
        part = x.shape[0]
        mine = (index // k) % 2
        got = lax.ppermute(x, axis, perm)
        whole = jnp.zeros((2 * part,) + x.shape[1:], x.dtype)
        whole = lax.dynamic_update_slice_in_dim(whole, x, mine * part, axis=0)
        x = lax.dynamic_update_slice_in_dim(whole, got, (1 - mine) * part, axis=0)
    return x, extra


def conjugate_gradients(kernel, targets, n_rows, sample_bits, landmark_bits):
    rhs_part = jnp.dot(kernel.T, targets, preferred_element_type=jnp.float32)
    rhs_total, _ = halving_sum(
        rhs_part, None, "sample", sample_bits, jnp.float32, jnp.float32
    )
    rhs = rhs_total / math.sqrt(n_rows)
    weights = jnp.zeros_like(rhs)
    residual = rhs
    direction = rhs
    norm_now = None
    for iteration in range(ITERS):
        direction_half = direction.astype(jnp.bfloat16)
        row_part = jnp.dot(kernel, direction_half, preferred_element_type=jnp.float32)
        sums = [jnp.sum(direction * direction, axis=0)]
        if norm_now is None:
            sums.append(jnp.sum(residual * residual, axis=0))
        row_half, landmark_sums = halving_sum(
            row_part, jnp.concatenate(sums), "landmark", landmark_bits, jnp.bfloat16
        )
        column_count = direction.shape[1]
        direction_square = landmark_sums[:column_count]
        if norm_now is None:
            norm_now = landmark_sums[column_count:]
        row_square = jnp.sum(jnp.square(row_half.astype(jnp.float32)), axis=0)
        column_part = jnp.dot(kernel.T, row_half, preferred_element_type=jnp.float32)
        column_total, row_square_total = halving_sum(
            column_part, row_square, "sample", sample_bits, jnp.float32, jnp.float32
        )
        image = column_total / n_rows + ridge * direction
        curvature = row_square_total / n_rows + ridge * direction_square
        step_size = norm_now / curvature
        weights = weights + step_size * direction
        residual = residual - step_size * image
        norm_next = butterfly_sum(jnp.sum(residual * residual, axis=0), "landmark", landmark_bits)
        direction = residual + norm_next / norm_now * direction
        norm_now = norm_next
    return weights, residual


def on_device(summaries, row_level, pool, pool_level, landmark_index, level_scale, targets):
    sample_bits = partner_bits(lax.axis_size("sample"), (2, 1, 4, 8, 16, 32, 64))
    landmark_bits = partner_bits(lax.axis_size("landmark"), (1, 2, 4, 8, 16, 32, 64))
    row_count = summaries.shape[0]
    n_rows = row_count * lax.axis_size("sample")
    gathered = lax.all_gather(summaries, "landmark", axis=1, tiled=True)
    feature_count = gathered.shape[1]
    anchors = jnp.take(pool, landmark_index, axis=0)
    anchor_level = jnp.take(pool_level, landmark_index, axis=0)
    row_factor = 1.0 / math.sqrt(feature_count) / level_values(row_level, level_scale)
    anchor_factor = 1.0 / level_values(anchor_level, level_scale)
    raw = raw_block(gathered, row_factor, anchors, anchor_factor)
    column_mean = butterfly_sum(jnp.sum(raw, axis=0), "sample", sample_bits) / n_rows
    kernel = (raw - column_mean[None, :]).astype(jnp.bfloat16)
    column_count = targets.shape[1]
    group_width = column_count // GROUPS
    results = [
        conjugate_gradients(
            kernel, targets[:, g * group_width:(g + 1) * group_width], n_rows, sample_bits, landmark_bits
        )
        for g in range(GROUPS)
    ]
    weights = jnp.concatenate([r[0] for r in results], axis=1)
    residual = jnp.concatenate([r[1] for r in results], axis=1)
    return (weights, residual)


def solution(mesh):
    return jax.shard_map(
        on_device,
        mesh=mesh,
        in_specs=(
            P("sample", "landmark"),
            P("sample"),
            P("landmark", None),
            P("landmark"),
            P("landmark"),
            P(),
            P("sample", None),
        ),
        out_specs=(P("landmark", None), P("landmark", None)),
        check_vma=False,
    )
```

profile of v0, /device:TPU:0, one launch (start us, length us, event | category | flops | bytes accessed | tf_op | source)
XLA Modules:
  0.0 334.3 jit_solution(3671340445035670978)
XLA Ops:
  8.6 6.1 %gather_fusion.1 = s32[1024]{0:T(1024)S(1)} fusion(s32[2048]{0:T(1024)S(1)} %copy-done, s32[1024]{0:T(1024)S(1)} %fusion.17), kind=kCustom, calls=%fused_computation.1 | custom fusion | bytes 12288 | tf_op jit(solution)/shard_map/jit(_take)/gather | solution.py:139
  14.8 7.7 %gather_fusion = bf16[1024,1024]{1,0:T(8,128)(2,1)S(1)} fusion(bf16[2048,1024]{1,0:T(8,128)(2,1)} %param.9, s32[1024]{0:T(1024)S(1)} %fusion.17), kind=kCustom, calls=%fused_computation | custom fusion | bytes 4198400 | tf_op jit(solution)/shard_map/jit(_take)/gather | solution.py:138
  22.8 26.9 %all-gather.2.cloned.1.call-done = bf16[2048,1024]{0,1:T(8,128)(2,1)} async-done(((bf16[2048,64]{0,1:T(8,128)(2,1)}), bf16[2048,1024]{0,1:T(8,128)(2,1)}) %all-gather.2.cloned.1.call-update) | async-done | bytes 4194320 | tf_op jit(solution)/shard_map/all_gather | solution.py:136
  49.7 9.7 %fusion = (f32[1024]{0:T(1024)S(1)}, f32[1024,2048]{1,0:T(8,128)}) fusion(f32[1024]{0:T(1024)S(1)} %broadcast_divide_fusion.1, f32[2048]{0:T(1024)S(1)} %broadcast_divide_fusion, bf16[2048,1024]{0,1:T(8,128)(2,1)} %all-gather.2.cloned.1.call-done, bf16[1024,1024]{1,0:T(8,128)(2,1)S(1)} %gather_fusion, pred[1024]{0:T(1024)(128)(4,1)S(1)} %get-tuple-element.59), kind=kOutput, calls=%fused_computation.4 | convolution fusion | flops 4302306304 | bytes 14697472 | tf_op jit(solution)/shard_map/dot_general | solution.py:23
  60.7 2.3 collective-permute-done
  63.0 2.5 collective-permute-start.1
  65.5 2.6 collective-permute-done.1
  68.1 2.9 collective-permute-start.2
  71.0 2.3 collective-permute-done.2
  73.2 4.4 %subtract_convert_fusion = bf16[1024,2048]{1,0:T(8,128)(2,1)S(1)} fusion(f32[1024,2048]{1,0:T(8,128)} %get-tuple-element.97, f32[1024]{0:T(1024)S(1)} %add_multiply_fusion, f32[1024]{0:T(1024)S(1)} %broadcast_divide_fusion.1, f32[2048]{0:T(1024)S(1)} %broadcast_divide_fusion), kind=kLoop, calls=%fused_computation.2 | loop fusion | flops 8388608 | bytes 12599296 | tf_op jit(solution)/shard_map/convert
  82.4 4.4 %collective-permute-done.3 = f32[512,128]{1,0:T(8,128)S(1)} collective-permute-done((f32[512,128]{1,0:T(8,128)S(1)}, f32[512,128]{1,0:T(8,128)S(1)}, u32[]{:S(2)}, u32[]{:S(2)}) %collective-permute-start.3) | collective-permute-done | bytes 262176 | tf_op jit(solution)/shard_map/ppermute | solution.py:76
  86.9 2.6 collective-permute-start.4
  89.7 2.6 collective-permute-start.39
  93.5 2.9 collective-permute-start.5
  96.5 2.9 collective-permute-start.40
  99.4 2.9 collective-permute-start.6
  102.3 2.9 collective-permute-start.41
  105.3 2.9 collective-permute-start.7
  108.3 3.4 %collective-permute-start.42 = (f32[256,128]{1,0:T(8,128)S(1)}, f32[256,128]{1,0:T(8,128)S(1)}, u32[]{:S(2)}, u32[]{:S(2)}) collective-permute-start(f32[256,128]{1,0:T(8,128)S(1)} %constant_dynamic-update-slice_fusion.38), channel_id=1, source_target_pairs={{0,16},{16,0},{32,48},{48,32},{64,80},{80,64},{96,112},{112,96},{1... | collective-permute-start | bytes 393224 | tf_op jit(solution)/shard_map/ppermute | solution.py:85
  114.9 2.1 collective-permute-start.43
  119.8 1.8 collective-permute-done.43
  128.1 1.9 collective-permute-start.10
  130.5 4.2 %collective-permute-done.10 = bf16[518,128]{1,0:T(8,128)(2,1)S(1)} collective-permute-done((bf16[518,128]{1,0:T(8,128)(2,1)S(1)}, bf16[518,128]{1,0:T(8,128)(2,1)S(1)}, u32[]{:S(2)}, u32[]{:S(2)}) %collective-permute-start.10) | collective-permute-done | bytes 132640 | tf_op jit(solution)/shard_map/ppermute | solution.py:76
  139.5 2.2 collective-permute-start.12
  141.8 2.1 collective-permute-start.47
  145.0 2.2 collective-permute-start.13
  147.3 2.1 collective-permute-start.48
  155.1 1.9 collective-permute-start.15
  157.4 1.9 collective-permute-start.50
  160.3 2.2 collective-permute-done.50
  164.5 2.2 collective-permute-start.17
  168.4 5.5 %collective-permute-done.17 = f32[513,128]{1,0:T(8,128)S(1)} collective-permute-done((f32[513,128]{1,0:T(8,128)S(1)}, f32[513,128]{1,0:T(8,128)S(1)}, u32[]{:S(2)}, u32[]{:S(2)}) %collective-permute-start.17) | collective-permute-done | bytes 262688 | tf_op jit(solution)/shard_map/ppermute | solution.py:76
  174.0 12.3 %collective-permute-start.18 = (f32[257,128]{1,0:T(8,128)S(1)}, f32[257,128]{1,0:T(8,128)S(1)}, u32[]{:S(2)}, u32[]{:S(2)}) collective-permute-start(f32[257,128]{1,0:T(8,128)S(1)} %pad_maximum_fusion.6), channel_id=1, source_target_pairs={{0,16},{16,0},{32,48},{48,32},{64,80},{80,64},{96,112},{112,96},{1... | collective-permute-start | bytes 394760 | tf_op jit(solution)/shard_map/ppermute | solution.py:76
  186.6 3.3 collective-permute-done.18
  190.0 3.5 %collective-permute-start.19 = (f32[129,128]{1,0:T(8,128)S(1)}, f32[129,128]{1,0:T(8,128)S(1)}, u32[]{:S(2)}, u32[]{:S(2)}) collective-permute-start(f32[129,128]{1,0:T(8,128)S(1)} %pad_maximum_fusion.14), channel_id=1, source_target_pairs={{0,64},{16,80},{32,96},{48,112},{64,0},{80,16},{96,32},{112,48},{1... | collective-permute-start | bytes 198152 | tf_op jit(solution)/shard_map/ppermute | solution.py:76
  193.6 2.4 collective-permute-start.54
  196.2 3.8 %collective-permute-start.20 = (f32[128,128]{1,0:T(8,128)S(1)}, f32[128,128]{1,0:T(8,128)S(1)}, u32[]{:S(2)}, u32[]{:S(2)}) collective-permute-start(f32[128,128]{1,0:T(8,128)S(1)} %get-tuple-element.21), channel_id=1, source_target_pairs={{0,64},{16,80},{32,96},{48,112},{64,0},{80,16},{96,32},{112,48},{1... | collective-permute-start | bytes 196616 | tf_op jit(solution)/shard_map/ppermute | solution.py:85
  200.1 1.8 collective-permute-start.55
  202.3 3.5 %collective-permute-start.21 = (f32[256,128]{1,0:T(8,128)S(1)}, f32[256,128]{1,0:T(8,128)S(1)}, u32[]{:S(2)}, u32[]{:S(2)}) collective-permute-start(f32[256,128]{1,0:T(8,128)S(1)} %constant_dynamic-update-slice_fusion.52), channel_id=1, source_target_pairs={{0,16},{16,0},{32,48},{48,32},{64,80},{80,64},{96,112},{112,96},{1... | collective-permute-start | bytes 393224 | tf_op jit(solution)/shard_map/ppermute | solution.py:85
  206.0 3.4 %collective-permute-start.56 = (f32[256,128]{1,0:T(8,128)S(1)}, f32[256,128]{1,0:T(8,128)S(1)}, u32[]{:S(2)}, u32[]{:S(2)}) collective-permute-start(f32[256,128]{1,0:T(8,128)S(1)} %constant_dynamic-update-slice_fusion.24), channel_id=1, source_target_pairs={{0,16},{16,0},{32,48},{48,32},{64,80},{80,64},{96,112},{112,96},{1... | collective-permute-start | bytes 393224 | tf_op jit(solution)/shard_map/ppermute | solution.py:85
  209.4 2.0 collective-permute-start.22
  213.9 3.0 collective-permute-done.22
  217.2 2.5 collective-permute-done.57
  228.8 1.9 collective-permute-start.61
  243.0 4.2 %collective-permute-done.28 = bf16[515,128]{1,0:T(8,128)(2,1)S(1)} collective-permute-done((bf16[515,128]{1,0:T(8,128)(2,1)S(1)}, bf16[515,128]{1,0:T(8,128)(2,1)S(1)}, u32[]{:S(2)}, u32[]{:S(2)}) %collective-permute-start.28) | collective-permute-done | bytes 131872 | tf_op jit(solution)/shard_map/ppermute | solution.py:76
  250.3 1.8 collective-permute-done.29
  252.2 2.0 collective-permute-start.30
  254.3 1.8 collective-permute-start.65
  257.8 2.2 collective-permute-start.31
  261.8 1.8 collective-permute-done.31
  273.0 2.2 collective-permute-done.68
  281.1 5.5 %collective-permute-done.35 = f32[513,128]{1,0:T(8,128)S(1)} collective-permute-done((f32[513,128]{1,0:T(8,128)S(1)}, f32[513,128]{1,0:T(8,128)S(1)}, u32[]{:S(2)}, u32[]{:S(2)}) %collective-permute-start.35) | collective-permute-done | bytes 262688 | tf_op jit(solution)/shard_map/ppermute | solution.py:76
  286.7 2.6 collective-permute-start.36
  289.2 2.6 collective-permute-done.70
  291.9 2.6 collective-permute-start.71
  294.5 2.5 collective-permute-start.37
  298.7 2.3 collective-permute-start.72
  301.0 1.9 collective-permute-start.73
  302.9 2.2 collective-permute-done.72
  307.3 2.9 collective-permute-start.74
  311.0 2.7 collective-permute-start.77
  315.8 1.8 collective-permute-done.77
  318.7 3.9 %collective-permute-done.75 = f32[512,128]{1,0:T(8,128)S(1)} collective-permute-done((f32[512,128]{1,0:T(8,128)S(1)}, f32[512,128]{1,0:T(8,128)S(1)}, u32[]{:S(2)}, u32[]{:S(2)}) %collective-permute-start.75) | collective-permute-done | bytes 262176 | tf_op jit(solution)/shard_map/ppermute | solution.py:85
  322.9 2.5 collective-permute-done.78
  (411 shorter events, 96.2 us)
Async XLA Ops:
  7.2 42.5 %all-gather.2.cloned.1.call-start = ((), (), s32[]{:S(2)}) async-start(), calls=%async_computation | async-start | bytes 4456448 | tf_op jit(solution)/shard_map/all_gather | solution.py:136
  63.0 5.1 %collective-permute-start.1 = (f32[1024]{0:T(1024)S(1)}, f32[1024]{0:T(1024)S(1)}, u32[]{:S(2)}, u32[]{:S(2)}) collective-permute-start(f32[1024]{0:T(1024)S(1)} %add.823), channel_id=1, source_target_pairs={{0,16},{16,0},{32,48},{48,32},{64,80},{80,64},{96,112},{112,96},{1... | collective-permute-start | bytes 12296 | tf_op jit(solution)/shard_map/ppermute | solution.py:37
  68.1 5.1 %collective-permute-start.2 = (f32[1024]{0:T(1024)S(1)}, f32[1024]{0:T(1024)S(1)}, u32[]{:S(2)}, u32[]{:S(2)}) collective-permute-start(f32[1024]{0:T(1024)S(1)} %add.824), channel_id=1, source_target_pairs={{0,64},{16,80},{32,96},{48,112},{64,0},{80,16},{96,32},{112,48},{1... | collective-permute-start | bytes 12296 | tf_op jit(solution)/shard_map/ppermute | solution.py:37
  78.9 7.9 %collective-permute-start.3 = (f32[512,128]{1,0:T(8,128)S(1)}, f32[512,128]{1,0:T(8,128)S(1)}, u32[]{:S(2)}, u32[]{:S(2)}) collective-permute-start(f32[512,128]{1,0:T(8,128)S(1)} %constant_dynamic-slice_fusion.17), channel_id=1, source_target_pairs={{0,32},{16,48},{32,0},{48,16},{64,96},{80,112},{96,64},{112,80},{1... | collective-permute-start | bytes 786440 | tf_op jit(solution)/shard_map/ppermute | solution.py:76
  81.7 8.0 %collective-permute-start.38 = (f32[512,128]{1,0:T(8,128)S(1)}, f32[512,128]{1,0:T(8,128)S(1)}, u32[]{:S(2)}, u32[]{:S(2)}) collective-permute-start(f32[512,128]{1,0:T(8,128)S(1)} %constant_dynamic-slice_fusion.8), channel_id=1, source_target_pairs={{0,32},{16,48},{32,0},{48,16},{64,96},{80,112},{96,64},{112,80},{1... | collective-permute-start | bytes 786440 | tf_op jit(solution)/shard_map/ppermute | solution.py:76
  86.9 6.6 %collective-permute-start.4 = (f32[256,128]{1,0:T(8,128)S(1)}, f32[256,128]{1,0:T(8,128)S(1)}, u32[]{:S(2)}, u32[]{:S(2)}) collective-permute-start(f32[256,128]{1,0:T(8,128)S(1)} %constant_dynamic-slice_fusion.16), channel_id=1, source_target_pairs={{0,16},{16,0},{32,48},{48,32},{64,80},{80,64},{96,112},{112,96},{1... | collective-permute-start | bytes 393224 | tf_op jit(solution)/shard_map/ppermute | solution.py:76
  89.7 6.7 %collective-permute-start.39 = (f32[256,128]{1,0:T(8,128)S(1)}, f32[256,128]{1,0:T(8,128)S(1)}, u32[]{:S(2)}, u32[]{:S(2)}) collective-permute-start(f32[256,128]{1,0:T(8,128)S(1)} %constant_dynamic-slice_fusion.7), channel_id=1, source_target_pairs={{0,16},{16,0},{32,48},{48,32},{64,80},{80,64},{96,112},{112,96},{1... | collective-permute-start | bytes 393224 | tf_op jit(solution)/shard_map/ppermute | solution.py:76
  93.5 5.9 %collective-permute-start.5 = (f32[128,128]{1,0:T(8,128)S(1)}, f32[128,128]{1,0:T(8,128)S(1)}, u32[]{:S(2)}, u32[]{:S(2)}) collective-permute-start(f32[128,128]{1,0:T(8,128)S(1)} %constant_dynamic-slice_fusion.15), channel_id=1, source_target_pairs={{0,64},{16,80},{32,96},{48,112},{64,0},{80,16},{96,32},{112,48},{1... | collective-permute-start | bytes 196616 | tf_op jit(solution)/shard_map/ppermute | solution.py:76
  96.5 5.8 %collective-permute-start.40 = (f32[128,128]{1,0:T(8,128)S(1)}, f32[128,128]{1,0:T(8,128)S(1)}, u32[]{:S(2)}, u32[]{:S(2)}) collective-permute-start(f32[128,128]{1,0:T(8,128)S(1)} %constant_dynamic-slice_fusion.6), channel_id=1, source_target_pairs={{0,64},{16,80},{32,96},{48,112},{64,0},{80,16},{96,32},{112,48},{1... | collective-permute-start | bytes 196616 | tf_op jit(solution)/shard_map/ppermute | solution.py:76
  99.4 5.8 %collective-permute-start.6 = (f32[128,128]{1,0:T(8,128)S(1)}, f32[128,128]{1,0:T(8,128)S(1)}, u32[]{:S(2)}, u32[]{:S(2)}) collective-permute-start(f32[128,128]{1,0:T(8,128)S(1)} %get-tuple-element.31), channel_id=1, source_target_pairs={{0,64},{16,80},{32,96},{48,112},{64,0},{80,16},{96,32},{112,48},{1... | collective-permute-start | bytes 196616 | tf_op jit(solution)/shard_map/ppermute | solution.py:85
  102.3 6.0 %collective-permute-start.41 = (f32[128,128]{1,0:T(8,128)S(1)}, f32[128,128]{1,0:T(8,128)S(1)}, u32[]{:S(2)}, u32[]{:S(2)}) collective-permute-start(f32[128,128]{1,0:T(8,128)S(1)} %get-tuple-element.57), channel_id=1, source_target_pairs={{0,64},{16,80},{32,96},{48,112},{64,0},{80,16},{96,32},{112,48},{1... | collective-permute-start | bytes 196616 | tf_op jit(solution)/shard_map/ppermute | solution.py:85
  105.3 6.6 %collective-permute-start.7 = (f32[256,128]{1,0:T(8,128)S(1)}, f32[256,128]{1,0:T(8,128)S(1)}, u32[]{:S(2)}, u32[]{:S(2)}) collective-permute-start(f32[256,128]{1,0:T(8,128)S(1)} %constant_dynamic-update-slice_fusion.66), channel_id=1, source_target_pairs={{0,16},{16,0},{32,48},{48,32},{64,80},{80,64},{96,112},{112,96},{1... | collective-permute-start | bytes 393224 | tf_op jit(solution)/shard_map/ppermute | solution.py:85
  108.3 6.6 %collective-permute-start.42 = (f32[256,128]{1,0:T(8,128)S(1)}, f32[256,128]{1,0:T(8,128)S(1)}, u32[]{:S(2)}, u32[]{:S(2)}) collective-permute-start(f32[256,128]{1,0:T(8,128)S(1)} %constant_dynamic-update-slice_fusion.38), channel_id=1, source_target_pairs={{0,16},{16,0},{32,48},{48,32},{64,80},{80,64},{96,112},{112,96},{1... | collective-permute-start | bytes 393224 | tf_op jit(solution)/shard_map/ppermute | solution.py:85
  111.8 6.5 %collective-permute-start.8 = (f32[512,128]{1,0:T(8,128)S(1)}, f32[512,128]{1,0:T(8,128)S(1)}, u32[]{:S(2)}, u32[]{:S(2)}) collective-permute-start(f32[512,128]{1,0:T(8,128)S(1)} %constant_dynamic-update-slice_fusion.64), channel_id=1, source_target_pairs={{0,32},{16,48},{32,0},{48,16},{64,96},{80,112},{96,64},{112,80},{1... | collective-permute-start | bytes 786440 | tf_op jit(solution)/shard_map/ppermute | solution.py:85
  114.9 6.7 %collective-permute-start.43 = (f32[512,128]{1,0:T(8,128)S(1)}, f32[512,128]{1,0:T(8,128)S(1)}, u32[]{:S(2)}, u32[]{:S(2)}) collective-permute-start(f32[512,128]{1,0:T(8,128)S(1)} %constant_dynamic-update-slice_fusion.36), channel_id=1, source_target_pairs={{0,32},{16,48},{32,0},{48,16},{64,96},{80,112},{96,64},{112,80},{1... | collective-permute-start | bytes 786440 | tf_op jit(solution)/shard_map/ppermute | solution.py:85
  128.1 6.5 %collective-permute-start.10 = (bf16[518,128]{1,0:T(8,128)(2,1)S(1)}, bf16[518,128]{1,0:T(8,128)(2,1)S(1)}, u32[]{:S(2)}, u32[]{:S(2)}) collective-permute-start(bf16[518,128]{1,0:T(8,128)(2,1)S(1)} %pad_maximum_fusion.10), channel_id=1, source_target_pairs={{0,2},{1,3},{2,0},{3,1},{4,6},{5,7},{6,4},{7,5},{8,10},{9,11},{10,... | collective-permute-start | bytes 397832 | tf_op jit(solution)/shard_map/ppermute | solution.py:76
  130.2 6.5 %collective-permute-start.45 = (bf16[518,128]{1,0:T(8,128)(2,1)S(1)}, bf16[518,128]{1,0:T(8,128)(2,1)S(1)}, u32[]{:S(2)}, u32[]{:S(2)}) collective-permute-start(bf16[518,128]{1,0:T(8,128)(2,1)S(1)} %pad_maximum_fusion.12), channel_id=1, source_target_pairs={{0,2},{1,3},{2,0},{3,1},{4,6},{5,7},{6,4},{7,5},{8,10},{9,11},{10,... | collective-permute-start | bytes 397832 | tf_op jit(solution)/shard_map/ppermute | solution.py:76
  134.8 4.6 %collective-permute-start.11 = (bf16[262,128]{1,0:T(8,128)(2,1)S(1)}, bf16[262,128]{1,0:T(8,128)(2,1)S(1)}, u32[]{:S(2)}, u32[]{:S(2)}) collective-permute-start(bf16[262,128]{1,0:T(8,128)(2,1)S(1)} %pad_maximum_fusion.18), channel_id=1, source_target_pairs={{0,4},{1,5},{2,6},{3,7},{4,0},{5,1},{6,2},{7,3},{8,12},{9,13},{10,... | collective-permute-start | bytes 201224 | tf_op jit(solution)/shard_map/ppermute | solution.py:76
  136.8 4.8 %collective-permute-start.46 = (bf16[262,128]{1,0:T(8,128)(2,1)S(1)}, bf16[262,128]{1,0:T(8,128)(2,1)S(1)}, u32[]{:S(2)}, u32[]{:S(2)}) collective-permute-start(bf16[262,128]{1,0:T(8,128)(2,1)S(1)} %pad_maximum_fusion.20), channel_id=1, source_target_pairs={{0,4},{1,5},{2,6},{3,7},{4,0},{5,1},{6,2},{7,3},{8,12},{9,13},{10,... | collective-permute-start | bytes 201224 | tf_op jit(solution)/shard_map/ppermute | solution.py:76
  139.5 5.5 %collective-permute-start.12 = (bf16[134,128]{1,0:T(8,128)(2,1)S(1)}, bf16[134,128]{1,0:T(8,128)(2,1)S(1)}, u32[]{:S(2)}, u32[]{:S(2)}) collective-permute-start(bf16[134,128]{1,0:T(8,128)(2,1)S(1)} %pad_maximum_fusion.22), channel_id=1, source_target_pairs={{0,8},{1,9},{2,10},{3,11},{4,12},{5,13},{6,14},{7,15},{8,0},{9,1},... | collective-permute-start | bytes 102920 | tf_op jit(solution)/shard_map/ppermute | solution.py:76
  141.8 5.5 %collective-permute-start.47 = (bf16[134,128]{1,0:T(8,128)(2,1)S(1)}, bf16[134,128]{1,0:T(8,128)(2,1)S(1)}, u32[]{:S(2)}, u32[]{:S(2)}) collective-permute-start(bf16[134,128]{1,0:T(8,128)(2,1)S(1)} %pad_maximum_fusion.24), channel_id=1, source_target_pairs={{0,8},{1,9},{2,10},{3,11},{4,12},{5,13},{6,14},{7,15},{8,0},{9,1},... | collective-permute-start | bytes 102920 | tf_op jit(solution)/shard_map/ppermute | solution.py:76
  145.0 5.8 %collective-permute-start.13 = (bf16[128,128]{1,0:T(8,128)(2,1)S(1)}, bf16[128,128]{1,0:T(8,128)(2,1)S(1)}, u32[]{:S(2)}, u32[]{:S(2)}) collective-permute-start(bf16[128,128]{1,0:T(8,128)(2,1)S(1)} %get-tuple-element.23), channel_id=1, source_target_pairs={{0,8},{1,9},{2,10},{3,11},{4,12},{5,13},{6,14},{7,15},{8,0},{9,1},... | collective-permute-start | bytes 98312 | tf_op jit(solution)/shard_map/ppermute | solution.py:85
  147.3 5.8 %collective-permute-start.48 = (bf16[128,128]{1,0:T(8,128)(2,1)S(1)}, bf16[128,128]{1,0:T(8,128)(2,1)S(1)}, u32[]{:S(2)}, u32[]{:S(2)}) collective-permute-start(bf16[128,128]{1,0:T(8,128)(2,1)S(1)} %get-tuple-element.49), channel_id=1, source_target_pairs={{0,8},{1,9},{2,10},{3,11},{4,12},{5,13},{6,14},{7,15},{8,0},{9,1},... | collective-permute-start | bytes 98312 | tf_op jit(solution)/shard_map/ppermute | solution.py:85
  150.9 4.3 %collective-permute-start.14 = (bf16[256,128]{1,0:T(8,128)(2,1)S(1)}, bf16[256,128]{1,0:T(8,128)(2,1)S(1)}, u32[]{:S(2)}, u32[]{:S(2)}) collective-permute-start(bf16[256,128]{1,0:T(8,128)(2,1)S(1)} %constant_dynamic-update-slice_fusion.60), channel_id=1, source_target_pairs={{0,4},{1,5},{2,6},{3,7},{4,0},{5,1},{6,2},{7,3},{8,12},{9,13},{10,... | collective-permute-start | bytes 196616 | tf_op jit(solution)/shard_map/ppermute | solution.py:85
  153.1 4.3 %collective-permute-start.49 = (bf16[256,128]{1,0:T(8,128)(2,1)S(1)}, bf16[256,128]{1,0:T(8,128)(2,1)S(1)}, u32[]{:S(2)}, u32[]{:S(2)}) collective-permute-start(bf16[256,128]{1,0:T(8,128)(2,1)S(1)} %constant_dynamic-update-slice_fusion.32), channel_id=1, source_target_pairs={{0,4},{1,5},{2,6},{3,7},{4,0},{5,1},{6,2},{7,3},{8,12},{9,13},{10,... | collective-permute-start | bytes 196616 | tf_op jit(solution)/shard_map/ppermute | solution.py:85
  155.1 5.0 %collective-permute-start.15 = (bf16[512,128]{1,0:T(8,128)(2,1)S(1)}, bf16[512,128]{1,0:T(8,128)(2,1)S(1)}, u32[]{:S(2)}, u32[]{:S(2)}) collective-permute-start(bf16[512,128]{1,0:T(8,128)(2,1)S(1)} %constant_dynamic-update-slice_fusion.58), channel_id=1, source_target_pairs={{0,2},{1,3},{2,0},{3,1},{4,6},{5,7},{6,4},{7,5},{8,10},{9,11},{10,... | collective-permute-start | bytes 393224 | tf_op jit(solution)/shard_map/ppermute | solution.py:85
  157.4 5.0 %collective-permute-start.50 = (bf16[512,128]{1,0:T(8,128)(2,1)S(1)}, bf16[512,128]{1,0:T(8,128)(2,1)S(1)}, u32[]{:S(2)}, u32[]{:S(2)}) collective-permute-start(bf16[512,128]{1,0:T(8,128)(2,1)S(1)} %constant_dynamic-update-slice_fusion.30), channel_id=1, source_target_pairs={{0,2},{1,3},{2,0},{3,1},{4,6},{5,7},{6,4},{7,5},{8,10},{9,11},{10,... | collective-permute-start | bytes 393224 | tf_op jit(solution)/shard_map/ppermute | solution.py:85
  164.5 9.4 %collective-permute-start.17 = (f32[513,128]{1,0:T(8,128)S(1)}, f32[513,128]{1,0:T(8,128)S(1)}, u32[]{:S(2)}, u32[]{:S(2)}) collective-permute-start(f32[513,128]{1,0:T(8,128)S(1)} %pad_maximum_fusion.2), channel_id=1, source_target_pairs={{0,32},{16,48},{32,0},{48,16},{64,96},{80,112},{96,64},{112,80},{1... | collective-permute-start | bytes 787976 | tf_op jit(solution)/shard_map/ppermute | solution.py:76
  168.3 18.0 %collective-permute-start.52 = (f32[513,128]{1,0:T(8,128)S(1)}, f32[513,128]{1,0:T(8,128)S(1)}, u32[]{:S(2)}, u32[]{:S(2)}) collective-permute-start(f32[513,128]{1,0:T(8,128)S(1)} %pad_maximum_fusion.4), channel_id=1, source_target_pairs={{0,32},{16,48},{32,0},{48,16},{64,96},{80,112},{96,64},{112,80},{1... | collective-permute-start | bytes 787976 | tf_op jit(solution)/shard_map/ppermute | solution.py:76
  174.0 15.9 %collective-permute-start.18 = (f32[257,128]{1,0:T(8,128)S(1)}, f32[257,128]{1,0:T(8,128)S(1)}, u32[]{:S(2)}, u32[]{:S(2)}) collective-permute-start(f32[257,128]{1,0:T(8,128)S(1)} %pad_maximum_fusion.6), channel_id=1, source_target_pairs={{0,16},{16,0},{32,48},{48,32},{64,80},{80,64},{96,112},{112,96},{1... | collective-permute-start | bytes 394760 | tf_op jit(solution)/shard_map/ppermute | solution.py:76
  186.4 7.1 %collective-permute-start.53 = (f32[257,128]{1,0:T(8,128)S(1)}, f32[257,128]{1,0:T(8,128)S(1)}, u32[]{:S(2)}, u32[]{:S(2)}) collective-permute-start(f32[257,128]{1,0:T(8,128)S(1)} %pad_maximum_fusion.8), channel_id=1, source_target_pairs={{0,16},{16,0},{32,48},{48,32},{64,80},{80,64},{96,112},{112,96},{1... | collective-permute-start | bytes 394760 | tf_op jit(solution)/shard_map/ppermute | solution.py:76
  190.0 6.2 %collective-permute-start.19 = (f32[129,128]{1,0:T(8,128)S(1)}, f32[129,128]{1,0:T(8,128)S(1)}, u32[]{:S(2)}, u32[]{:S(2)}) collective-permute-start(f32[129,128]{1,0:T(8,128)S(1)} %pad_maximum_fusion.14), channel_id=1, source_target_pairs={{0,64},{16,80},{32,96},{48,112},{64,0},{80,16},{96,32},{112,48},{1... | collective-permute-start | bytes 198152 | tf_op jit(solution)/shard_map/ppermute | solution.py:76
  193.6 6.5 %collective-permute-start.54 = (f32[129,128]{1,0:T(8,128)S(1)}, f32[129,128]{1,0:T(8,128)S(1)}, u32[]{:S(2)}, u32[]{:S(2)}) collective-permute-start(f32[129,128]{1,0:T(8,128)S(1)} %pad_maximum_fusion.16), channel_id=1, source_target_pairs={{0,64},{16,80},{32,96},{48,112},{64,0},{80,16},{96,32},{112,48},{1... | collective-permute-start | bytes 198152 | tf_op jit(solution)/shard_map/ppermute | solution.py:76
  196.2 6.1 %collective-permute-start.20 = (f32[128,128]{1,0:T(8,128)S(1)}, f32[128,128]{1,0:T(8,128)S(1)}, u32[]{:S(2)}, u32[]{:S(2)}) collective-permute-start(f32[128,128]{1,0:T(8,128)S(1)} %get-tuple-element.21), channel_id=1, source_target_pairs={{0,64},{16,80},{32,96},{48,112},{64,0},{80,16},{96,32},{112,48},{1... | collective-permute-start | bytes 196616 | tf_op jit(solution)/shard_map/ppermute | solution.py:85
  200.1 5.8 %collective-permute-start.55 = (f32[128,128]{1,0:T(8,128)S(1)}, f32[128,128]{1,0:T(8,128)S(1)}, u32[]{:S(2)}, u32[]{:S(2)}) collective-permute-start(f32[128,128]{1,0:T(8,128)S(1)} %get-tuple-element.47), channel_id=1, source_target_pairs={{0,64},{16,80},{32,96},{48,112},{64,0},{80,16},{96,32},{112,48},{1... | collective-permute-start | bytes 196616 | tf_op jit(solution)/shard_map/ppermute | solution.py:85
  202.3 7.0 %collective-permute-start.21 = (f32[256,128]{1,0:T(8,128)S(1)}, f32[256,128]{1,0:T(8,128)S(1)}, u32[]{:S(2)}, u32[]{:S(2)}) collective-permute-start(f32[256,128]{1,0:T(8,128)S(1)} %constant_dynamic-update-slice_fusion.52), channel_id=1, source_target_pairs={{0,16},{16,0},{32,48},{48,32},{64,80},{80,64},{96,112},{112,96},{1... | collective-permute-start | bytes 393224 | tf_op jit(solution)/shard_map/ppermute | solution.py:85
  206.0 6.6 %collective-permute-start.56 = (f32[256,128]{1,0:T(8,128)S(1)}, f32[256,128]{1,0:T(8,128)S(1)}, u32[]{:S(2)}, u32[]{:S(2)}) collective-permute-start(f32[256,128]{1,0:T(8,128)S(1)} %constant_dynamic-update-slice_fusion.24), channel_id=1, source_target_pairs={{0,16},{16,0},{32,48},{48,32},{64,80},{80,64},{96,112},{112,96},{1... | collective-permute-start | bytes 393224 | tf_op jit(solution)/shard_map/ppermute | solution.py:85
  209.4 7.5 %collective-permute-start.22 = (f32[512,128]{1,0:T(8,128)S(1)}, f32[512,128]{1,0:T(8,128)S(1)}, u32[]{:S(2)}, u32[]{:S(2)}) collective-permute-start(f32[512,128]{1,0:T(8,128)S(1)} %constant_dynamic-update-slice_fusion.50), channel_id=1, source_target_pairs={{0,32},{16,48},{32,0},{48,16},{64,96},{80,112},{96,64},{112,80},{1... | collective-permute-start | bytes 786440 | tf_op jit(solution)/shard_map/ppermute | solution.py:85
  212.6 7.1 %collective-permute-start.57 = (f32[512,128]{1,0:T(8,128)S(1)}, f32[512,128]{1,0:T(8,128)S(1)}, u32[]{:S(2)}, u32[]{:S(2)}) collective-permute-start(f32[512,128]{1,0:T(8,128)S(1)} %constant_dynamic-update-slice_fusion.22), channel_id=1, source_target_pairs={{0,32},{16,48},{32,0},{48,16},{64,96},{80,112},{96,64},{112,80},{1... | collective-permute-start | bytes 786440 | tf_op jit(solution)/shard_map/ppermute | solution.py:85
  227.2 5.1 %collective-permute-start.26 = (f32[128]{0:T(128)S(1)}, f32[128]{0:T(128)S(1)}, u32[]{:S(2)}, u32[]{:S(2)}) collective-permute-start(f32[128]{0:T(128)S(1)} %add.885), channel_id=1, source_target_pairs={{0,8},{1,9},{2,10},{3,11},{4,12},{5,13},{6,14},{7,15},{8,0},{9,1},... | collective-permute-start | bytes 1544 | tf_op jit(solution)/shard_map/ppermute | solution.py:37
  228.8 5.1 %collective-permute-start.61 = (f32[128]{0:T(128)S(1)}, f32[128]{0:T(128)S(1)}, u32[]{:S(2)}, u32[]{:S(2)}) collective-permute-start(f32[128]{0:T(128)S(1)} %add.954), channel_id=1, source_target_pairs={{0,8},{1,9},{2,10},{3,11},{4,12},{5,13},{6,14},{7,15},{8,0},{9,1},... | collective-permute-start | bytes 1544 | tf_op jit(solution)/shard_map/ppermute | solution.py:37
  240.7 6.5 %collective-permute-start.28 = (bf16[515,128]{1,0:T(8,128)(2,1)S(1)}, bf16[515,128]{1,0:T(8,128)(2,1)S(1)}, u32[]{:S(2)}, u32[]{:S(2)}) collective-permute-start(bf16[515,128]{1,0:T(8,128)(2,1)S(1)} %pad_maximum_fusion.11), channel_id=1, source_target_pairs={{0,2},{1,3},{2,0},{3,1},{4,6},{5,7},{6,4},{7,5},{8,10},{9,11},{10,... | collective-permute-start | bytes 395528 | tf_op jit(solution)/shard_map/ppermute | solution.py:76
  242.3 6.9 %collective-permute-start.63 = (bf16[515,128]{1,0:T(8,128)(2,1)S(1)}, bf16[515,128]{1,0:T(8,128)(2,1)S(1)}, u32[]{:S(2)}, u32[]{:S(2)}) collective-permute-start(bf16[515,128]{1,0:T(8,128)(2,1)S(1)} %pad_maximum_fusion.13), channel_id=1, source_target_pairs={{0,2},{1,3},{2,0},{3,1},{4,6},{5,7},{6,4},{7,5},{8,10},{9,11},{10,... | collective-permute-start | bytes 395528 | tf_op jit(solution)/shard_map/ppermute | solution.py:76
  247.3 4.8 %collective-permute-start.29 = (bf16[259,128]{1,0:T(8,128)(2,1)S(1)}, bf16[259,128]{1,0:T(8,128)(2,1)S(1)}, u32[]{:S(2)}, u32[]{:S(2)}) collective-permute-start(bf16[259,128]{1,0:T(8,128)(2,1)S(1)} %pad_maximum_fusion.19), channel_id=1, source_target_pairs={{0,4},{1,5},{2,6},{3,7},{4,0},{5,1},{6,2},{7,3},{8,12},{9,13},{10,... | collective-permute-start | bytes 198920 | tf_op jit(solution)/shard_map/ppermute | solution.py:76
  249.3 4.9 %collective-permute-start.64 = (bf16[259,128]{1,0:T(8,128)(2,1)S(1)}, bf16[259,128]{1,0:T(8,128)(2,1)S(1)}, u32[]{:S(2)}, u32[]{:S(2)}) collective-permute-start(bf16[259,128]{1,0:T(8,128)(2,1)S(1)} %pad_maximum_fusion.21), channel_id=1, source_target_pairs={{0,4},{1,5},{2,6},{3,7},{4,0},{5,1},{6,2},{7,3},{8,12},{9,13},{10,... | collective-permute-start | bytes 198920 | tf_op jit(solution)/shard_map/ppermute | solution.py:76
  252.2 5.5 %collective-permute-start.30 = (bf16[131,128]{1,0:T(8,128)(2,1)S(1)}, bf16[131,128]{1,0:T(8,128)(2,1)S(1)}, u32[]{:S(2)}, u32[]{:S(2)}) collective-permute-start(bf16[131,128]{1,0:T(8,128)(2,1)S(1)} %pad_maximum_fusion.23), channel_id=1, source_target_pairs={{0,8},{1,9},{2,10},{3,11},{4,12},{5,13},{6,14},{7,15},{8,0},{9,1},... | collective-permute-start | bytes 100616 | tf_op jit(solution)/shard_map/ppermute | solution.py:76
  254.3 5.7 %collective-permute-start.65 = (bf16[131,128]{1,0:T(8,128)(2,1)S(1)}, bf16[131,128]{1,0:T(8,128)(2,1)S(1)}, u32[]{:S(2)}, u32[]{:S(2)}) collective-permute-start(bf16[131,128]{1,0:T(8,128)(2,1)S(1)} %pad_maximum_fusion.25), channel_id=1, source_target_pairs={{0,8},{1,9},{2,10},{3,11},{4,12},{5,13},{6,14},{7,15},{8,0},{9,1},... | collective-permute-start | bytes 100616 | tf_op jit(solution)/shard_map/ppermute | solution.py:76
  257.8 5.7 %collective-permute-start.31 = (bf16[128,128]{1,0:T(8,128)(2,1)S(1)}, bf16[128,128]{1,0:T(8,128)(2,1)S(1)}, u32[]{:S(2)}, u32[]{:S(2)}) collective-permute-start(bf16[128,128]{1,0:T(8,128)(2,1)S(1)} %get-tuple-element.9), channel_id=1, source_target_pairs={{0,8},{1,9},{2,10},{3,11},{4,12},{5,13},{6,14},{7,15},{8,0},{9,1},... | collective-permute-start | bytes 98312 | tf_op jit(solution)/shard_map/ppermute | solution.py:85
  260.1 5.8 %collective-permute-start.66 = (bf16[128,128]{1,0:T(8,128)(2,1)S(1)}, bf16[128,128]{1,0:T(8,128)(2,1)S(1)}, u32[]{:S(2)}, u32[]{:S(2)}) collective-permute-start(bf16[128,128]{1,0:T(8,128)(2,1)S(1)} %get-tuple-element.35), channel_id=1, source_target_pairs={{0,8},{1,9},{2,10},{3,11},{4,12},{5,13},{6,14},{7,15},{8,0},{9,1},... | collective-permute-start | bytes 98312 | tf_op jit(solution)/shard_map/ppermute | solution.py:85
  263.5 4.3 %collective-permute-start.32 = (bf16[256,128]{1,0:T(8,128)(2,1)S(1)}, bf16[256,128]{1,0:T(8,128)(2,1)S(1)}, u32[]{:S(2)}, u32[]{:S(2)}) collective-permute-start(bf16[256,128]{1,0:T(8,128)(2,1)S(1)} %constant_dynamic-update-slice_fusion.46), channel_id=1, source_target_pairs={{0,4},{1,5},{2,6},{3,7},{4,0},{5,1},{6,2},{7,3},{8,12},{9,13},{10,... | collective-permute-start | bytes 196616 | tf_op jit(solution)/shard_map/ppermute | solution.py:85
  267.8 5.0 %collective-permute-start.33 = (bf16[512,128]{1,0:T(8,128)(2,1)S(1)}, bf16[512,128]{1,0:T(8,128)(2,1)S(1)}, u32[]{:S(2)}, u32[]{:S(2)}) collective-permute-start(bf16[512,128]{1,0:T(8,128)(2,1)S(1)} %constant_dynamic-update-slice_fusion.44), channel_id=1, source_target_pairs={{0,2},{1,3},{2,0},{3,1},{4,6},{5,7},{6,4},{7,5},{8,10},{9,11},{10,... | collective-permute-start | bytes 393224 | tf_op jit(solution)/shard_map/ppermute | solution.py:85
  270.1 5.0 %collective-permute-start.68 = (bf16[512,128]{1,0:T(8,128)(2,1)S(1)}, bf16[512,128]{1,0:T(8,128)(2,1)S(1)}, u32[]{:S(2)}, u32[]{:S(2)}) collective-permute-start(bf16[512,128]{1,0:T(8,128)(2,1)S(1)} %constant_dynamic-update-slice_fusion.16), channel_id=1, source_target_pairs={{0,2},{1,3},{2,0},{3,1},{4,6},{5,7},{6,4},{7,5},{8,10},{9,11},{10,... | collective-permute-start | bytes 393224 | tf_op jit(solution)/shard_map/ppermute | solution.py:85
  277.2 9.3 %collective-permute-start.35 = (f32[513,128]{1,0:T(8,128)S(1)}, f32[513,128]{1,0:T(8,128)S(1)}, u32[]{:S(2)}, u32[]{:S(2)}) collective-permute-start(f32[513,128]{1,0:T(8,128)S(1)} %pad_maximum_fusion.3), channel_id=1, source_target_pairs={{0,32},{16,48},{32,0},{48,16},{64,96},{80,112},{96,64},{112,80},{1... | collective-permute-start | bytes 787976 | tf_op jit(solution)/shard_map/ppermute | solution.py:76
  279.7 12.1 %collective-permute-start.70 = (f32[513,128]{1,0:T(8,128)S(1)}, f32[513,128]{1,0:T(8,128)S(1)}, u32[]{:S(2)}, u32[]{:S(2)}) collective-permute-start(f32[513,128]{1,0:T(8,128)S(1)} %pad_maximum_fusion.5), channel_id=1, source_target_pairs={{0,32},{16,48},{32,0},{48,16},{64,96},{80,112},{96,64},{112,80},{1... | collective-permute-start | bytes 787976 | tf_op jit(solution)/shard_map/ppermute | solution.py:76
  286.7 7.8 %collective-permute-start.36 = (f32[257,128]{1,0:T(8,128)S(1)}, f32[257,128]{1,0:T(8,128)S(1)}, u32[]{:S(2)}, u32[]{:S(2)}) collective-permute-start(f32[257,128]{1,0:T(8,128)S(1)} %pad_maximum_fusion.7), channel_id=1, source_target_pairs={{0,16},{16,0},{32,48},{48,32},{64,80},{80,64},{96,112},{112,96},{1... | collective-permute-start | bytes 394760 | tf_op jit(solution)/shard_map/ppermute | solution.py:76
  291.9 6.7 %collective-permute-start.71 = (f32[257,128]{1,0:T(8,128)S(1)}, f32[257,128]{1,0:T(8,128)S(1)}, u32[]{:S(2)}, u32[]{:S(2)}) collective-permute-start(f32[257,128]{1,0:T(8,128)S(1)} %pad_maximum_fusion.9), channel_id=1, source_target_pairs={{0,16},{16,0},{32,48},{48,32},{64,80},{80,64},{96,112},{112,96},{1... | collective-permute-start | bytes 394760 | tf_op jit(solution)/shard_map/ppermute | solution.py:76
  294.5 6.4 %collective-permute-start.37 = (f32[129,128]{1,0:T(8,128)S(1)}, f32[129,128]{1,0:T(8,128)S(1)}, u32[]{:S(2)}, u32[]{:S(2)}) collective-permute-start(f32[129,128]{1,0:T(8,128)S(1)} %pad_maximum_fusion.15), channel_id=1, source_target_pairs={{0,64},{16,80},{32,96},{48,112},{64,0},{80,16},{96,32},{112,48},{1... | collective-permute-start | bytes 198152 | tf_op jit(solution)/shard_map/ppermute | solution.py:76
  298.7 6.5 %collective-permute-start.72 = (f32[129,128]{1,0:T(8,128)S(1)}, f32[129,128]{1,0:T(8,128)S(1)}, u32[]{:S(2)}, u32[]{:S(2)}) collective-permute-start(f32[129,128]{1,0:T(8,128)S(1)} %pad_maximum_fusion.17), channel_id=1, source_target_pairs={{0,64},{16,80},{32,96},{48,112},{64,0},{80,16},{96,32},{112,48},{1... | collective-permute-start | bytes 198152 | tf_op jit(solution)/shard_map/ppermute | solution.py:76
  301.0 6.3 %collective-permute-start.73 = (f32[128,128]{1,0:T(8,128)S(1)}, f32[128,128]{1,0:T(8,128)S(1)}, u32[]{:S(2)}, u32[]{:S(2)}) collective-permute-start(f32[128,128]{1,0:T(8,128)S(1)} %get-tuple-element.3), channel_id=1, source_target_pairs={{0,64},{16,80},{32,96},{48,112},{64,0},{80,16},{96,32},{112,48},{1... | collective-permute-start | bytes 196616 | tf_op jit(solution)/shard_map/ppermute | solution.py:85
  305.2 5.8 %collective-permute-start.76 = (f32[128,128]{1,0:T(8,128)S(1)}, f32[128,128]{1,0:T(8,128)S(1)}, u32[]{:S(2)}, u32[]{:S(2)}) collective-permute-start(f32[128,128]{1,0:T(8,128)S(1)} %get-tuple-element.5), channel_id=1, source_target_pairs={{0,64},{16,80},{32,96},{48,112},{64,0},{80,16},{96,32},{112,48},{1... | collective-permute-start | bytes 196616 | tf_op jit(solution)/shard_map/ppermute | solution.py:85
  307.3 7.4 %collective-permute-start.74 = (f32[256,128]{1,0:T(8,128)S(1)}, f32[256,128]{1,0:T(8,128)S(1)}, u32[]{:S(2)}, u32[]{:S(2)}) collective-permute-start(f32[256,128]{1,0:T(8,128)S(1)} %constant_dynamic-update-slice_fusion.10), channel_id=1, source_target_pairs={{0,16},{16,0},{32,48},{48,32},{64,80},{80,64},{96,112},{112,96},{1... | collective-permute-start | bytes 393224 | tf_op jit(solution)/shard_map/ppermute | solution.py:85
  311.0 6.6 %collective-permute-start.77 = (f32[256,128]{1,0:T(8,128)S(1)}, f32[256,128]{1,0:T(8,128)S(1)}, u32[]{:S(2)}, u32[]{:S(2)}) collective-permute-start(f32[256,128]{1,0:T(8,128)S(1)} %constant_dynamic-update-slice_fusion.4), channel_id=1, source_target_pairs={{0,16},{16,0},{32,48},{48,32},{64,80},{80,64},{96,112},{112,96},{1... | collective-permute-start | bytes 393224 | tf_op jit(solution)/shard_map/ppermute | solution.py:85
  314.7 7.9 %collective-permute-start.75 = (f32[512,128]{1,0:T(8,128)S(1)}, f32[512,128]{1,0:T(8,128)S(1)}, u32[]{:S(2)}, u32[]{:S(2)}) collective-permute-start(f32[512,128]{1,0:T(8,128)S(1)} %constant_dynamic-update-slice_fusion.8), channel_id=1, source_target_pairs={{0,32},{16,48},{32,0},{48,16},{64,96},{80,112},{96,64},{112,80},{1... | collective-permute-start | bytes 786440 | tf_op jit(solution)/shard_map/ppermute | solution.py:85
  317.6 7.8 %collective-permute-start.78 = (f32[512,128]{1,0:T(8,128)S(1)}, f32[512,128]{1,0:T(8,128)S(1)}, u32[]{:S(2)}, u32[]{:S(2)}) collective-permute-start(f32[512,128]{1,0:T(8,128)S(1)} %constant_dynamic-update-slice_fusion.2), channel_id=1, source_target_pairs={{0,32},{16,48},{32,0},{48,16},{64,96},{80,112},{96,64},{112,80},{1... | collective-permute-start | bytes 786440 | tf_op jit(solution)/shard_map/ppermute | solution.py:85
  (26 other events, 187.5 us)
Sparse Core Ops, SparseCore 0:
  9.7 39.9 all-gather.1
where the time goes:
time: 340 us; the launch traced here: 334 us
  starting transfers between devices  138 us (41%)
  waiting for transfers between devices  121 us (36%)
  matrix products  22.5 us (7%)
  local copies, waits for them, and re-layouts  22.1 us (6%)
  between operations  15.9 us (5%)
  other arithmetic  14.6 us (4%)
    ppermute x34, starting transfers between devices, halving_sum(): got = lax.ppermute(send, axis, perm)  64.1 us
    ppermute x34, starting transfers between devices, halving_sum(): got = lax.ppermute(x, axis, perm)  60.4 us
    ppermute x34, waiting for transfers between devices, halving_sum(): got = lax.ppermute(send, axis, perm)  42.5 us
    ppermute x34, waiting for transfers between devices, halving_sum(): got = lax.ppermute(x, axis, perm)  38.3 us
    all_gather x1, waiting for transfers between devices, on_device(): gathered = lax.all_gather(summaries, 'landmark', axis=1, tiled=True)  26.9 us
    ppermute x11, starting transfers between devices, butterfly_sum(): x = x + lax.ppermute(x, axis, perm)  13.9 us
    ppermute x11, waiting for transfers between devices, butterfly_sum(): x = x + lax.ppermute(x, axis, perm)  12.4 us
    dot_general x1, matrix products, raw_block(): jnp.dot(summary_rows, anchors.T, preferred_element_type=jnp.float32)  9.71 us
  transfers between devices with their start and end apart: 80, of which 55 were waited for; matrix products, arithmetic and copies ran while one was open for 11% of the time, Pallas kernels for 0%

commit v1 on v0

--- a/solution.py
+++ b/solution.py
@@ -46,9 +46,9 @@
         parts = []
         rest = rows
         for _ in range(3):
-            term = rest.astype(wire_dtype)
+            term = lax.reduce_precision(rest, exponent_bits=8, mantissa_bits=7)
             parts.append(term)
-            rest = rest - term.astype(jnp.float32)
+            rest = rest - term
     return jnp.concatenate(parts, axis=0).astype(wire_dtype)
 
 

time: 340 us -> 340 us (level)
    ppermute x34, waiting for transfers between devices: 38.3 us -> 34.7 us  [halving_sum(): got = lax.ppermute(x, axis, perm)]
  transfers between devices with their start and end apart: 80 -> 80, of which waited for: 55 -> 57; matrix products, arithmetic and copies ran while one was open for 11% -> 12% of each run, Pallas kernels for 0% -> 0%
where the time goes in v1:
time: 340 us; the launch traced here: 335 us
  starting transfers between devices  140 us (41%)
  waiting for transfers between devices  118 us (35%)
  matrix products  24.7 us (7%)
  local copies, waits for them, and re-layouts  22.1 us (6%)
  between operations  15.9 us (5%)
  other arithmetic  14.6 us (4%)
    ppermute x34, starting transfers between devices, halving_sum(): got = lax.ppermute(send, axis, perm)  62.2 us
    ppermute x34, starting transfers between devices, halving_sum(): got = lax.ppermute(x, axis, perm)  62.2 us
    ppermute x34, waiting for transfers between devices, halving_sum(): got = lax.ppermute(send, axis, perm)  43.8 us
    ppermute x34, waiting for transfers between devices, halving_sum(): got = lax.ppermute(x, axis, perm)  34.7 us
    all_gather x1, waiting for transfers between devices, on_device(): gathered = lax.all_gather(summaries, 'landmark', axis=1, tiled=True)  26.9 us
    ppermute x11, starting transfers between devices, butterfly_sum(): x = x + lax.ppermute(x, axis, perm)  15.1 us
    ppermute x11, waiting for transfers between devices, butterfly_sum(): x = x + lax.ppermute(x, axis, perm)  11.6 us
    dot_general x1, matrix products, raw_block(): jnp.dot(summary_rows, anchors.T, preferred_element_type=jnp.float32)  9.71 us
  transfers between devices with their start and end apart: 80, of which 57 were waited for; matrix products, arithmetic and copies ran while one was open for 12% of the time, Pallas kernels for 0%

profile of v1, /device:TPU:0, one launch (start us, length us, event | category | flops | bytes accessed | tf_op | source)
XLA Modules:
  0.0 334.5 jit_solution(3198858154823495972)
XLA Ops:
  8.6 6.1 %gather_fusion.1 = s32[1024]{0:T(1024)S(1)} fusion(s32[2048]{0:T(1024)S(1)} %copy-done, s32[1024]{0:T(1024)S(1)} %fusion.17), kind=kCustom, calls=%fused_computation.1 | custom fusion | bytes 12288 | tf_op jit(solution)/shard_map/jit(_take)/gather | solution.py:139
  14.8 7.7 %gather_fusion = bf16[1024,1024]{1,0:T(8,128)(2,1)S(1)} fusion(bf16[2048,1024]{1,0:T(8,128)(2,1)} %param.9, s32[1024]{0:T(1024)S(1)} %fusion.17), kind=kCustom, calls=%fused_computation | custom fusion | bytes 4198400 | tf_op jit(solution)/shard_map/jit(_take)/gather | solution.py:138
  22.8 26.9 %all-gather.2.cloned.1.call-done = bf16[2048,1024]{0,1:T(8,128)(2,1)} async-done(((bf16[2048,64]{0,1:T(8,128)(2,1)}), bf16[2048,1024]{0,1:T(8,128)(2,1)}) %all-gather.2.cloned.1.call-update) | async-done | bytes 4194320 | tf_op jit(solution)/shard_map/all_gather | solution.py:136
  49.7 9.7 %fusion = (f32[1024]{0:T(1024)S(1)}, f32[1024,2048]{1,0:T(8,128)}) fusion(f32[1024]{0:T(1024)S(1)} %broadcast_divide_fusion.1, f32[2048]{0:T(1024)S(1)} %broadcast_divide_fusion, bf16[2048,1024]{0,1:T(8,128)(2,1)} %all-gather.2.cloned.1.call-done, bf16[1024,1024]{1,0:T(8,128)(2,1)S(1)} %gather_fusion, pred[1024]{0:T(1024)(128)(4,1)S(1)} %get-tuple-element.59), kind=kOutput, calls=%fused_computation.4 | convolution fusion | flops 4302306304 | bytes 14697472 | tf_op jit(solution)/shard_map/dot_general | solution.py:23
  60.7 2.3 collective-permute-done
  63.0 2.5 collective-permute-start.1
  65.5 2.6 collective-permute-done.1
  68.1 2.9 collective-permute-start.2
  71.0 2.3 collective-permute-done.2
  73.2 4.4 %subtract_convert_fusion = bf16[1024,2048]{1,0:T(8,128)(2,1)S(1)} fusion(f32[1024,2048]{1,0:T(8,128)} %get-tuple-element.101, f32[1024]{0:T(1024)S(1)} %add_multiply_fusion, f32[1024]{0:T(1024)S(1)} %broadcast_divide_fusion.1, f32[2048]{0:T(1024)S(1)} %broadcast_divide_fusion), kind=kLoop, calls=%fused_computation.2 | loop fusion | flops 8388608 | bytes 12599296 | tf_op jit(solution)/shard_map/convert.48
  82.4 4.4 %collective-permute-done.3 = f32[512,128]{1,0:T(8,128)S(1)} collective-permute-done((f32[512,128]{1,0:T(8,128)S(1)}, f32[512,128]{1,0:T(8,128)S(1)}, u32[]{:S(2)}, u32[]{:S(2)}) %collective-permute-start.3) | collective-permute-done | bytes 262176 | tf_op jit(solution)/shard_map/ppermute | solution.py:76
  86.9 2.6 collective-permute-start.4
  89.7 2.6 collective-permute-start.39
  93.5 2.9 collective-permute-start.5
  96.5 2.9 collective-permute-start.40
  99.4 2.9 collective-permute-start.6
  102.3 2.9 collective-permute-start.41
  105.3 2.9 collective-permute-start.7
  108.3 3.4 %collective-permute-start.42 = (f32[256,128]{1,0:T(8,128)S(1)}, f32[256,128]{1,0:T(8,128)S(1)}, u32[]{:S(2)}, u32[]{:S(2)}) collective-permute-start(f32[256,128]{1,0:T(8,128)S(1)} %constant_dynamic-update-slice_fusion.38), channel_id=1, source_target_pairs={{0,16},{16,0},{32,48},{48,32},{64,80},{80,64},{96,112},{112,96},{1... | collective-permute-start | bytes 393224 | tf_op jit(solution)/shard_map/ppermute | solution.py:85
  114.9 2.1 collective-permute-start.43
  121.6 3.5 %fusion.10 = f32[2048,128]{1,0:T(8,128)S(1)} fusion(bf16[1024,2048]{1,0:T(8,128)(2,1)} %copy-done.2, f32[1024,128]{1,0:T(8,128)S(1)} %constant_dynamic-update-slice_fusion.34), kind=kOutput, calls=%fused_computation.48 | convolution fusion | flops 537133056 | bytes 5767168 | tf_op jit(solution)/shard_map/dot_general | solution.py:104
  128.6 1.8 collective-permute-start.10
  130.9 4.2 %collective-permute-done.10 = bf16[518,128]{1,0:T(8,128)(2,1)S(1)} collective-permute-done((bf16[518,128]{1,0:T(8,128)(2,1)S(1)}, bf16[518,128]{1,0:T(8,128)(2,1)S(1)}, u32[]{:S(2)}, u32[]{:S(2)}) %collective-permute-start.10) | collective-permute-done | bytes 132640 | tf_op jit(solution)/shard_map/ppermute | solution.py:76
  139.6 2.1 collective-permute-start.12
  142.4 1.9 collective-permute-start.47
  145.5 2.1 collective-permute-start.13
  148.1 1.9 collective-permute-start.48
  155.3 1.8 collective-permute-start.15
  157.8 1.9 collective-permute-start.50
  160.5 2.4 collective-permute-done.50
  164.9 1.9 collective-permute-start.17
  168.8 5.5 %collective-permute-done.17 = f32[513,128]{1,0:T(8,128)S(1)} collective-permute-done((f32[513,128]{1,0:T(8,128)S(1)}, f32[513,128]{1,0:T(8,128)S(1)}, u32[]{:S(2)}, u32[]{:S(2)}) %collective-permute-start.17) | collective-permute-done | bytes 262688 | tf_op jit(solution)/shard_map/ppermute | solution.py:76
  174.4 12.0 %collective-permute-start.18 = (f32[257,128]{1,0:T(8,128)S(1)}, f32[257,128]{1,0:T(8,128)S(1)}, u32[]{:S(2)}, u32[]{:S(2)}) collective-permute-start(f32[257,128]{1,0:T(8,128)S(1)} %pad_maximum_fusion.6), channel_id=1, source_target_pairs={{0,16},{16,0},{32,48},{48,32},{64,80},{80,64},{96,112},{112,96},{1... | collective-permute-start | bytes 394760 | tf_op jit(solution)/shard_map/ppermute | solution.py:76
  186.9 3.1 collective-permute-done.18
  190.1 3.5 %collective-permute-start.19 = (f32[129,128]{1,0:T(8,128)S(1)}, f32[129,128]{1,0:T(8,128)S(1)}, u32[]{:S(2)}, u32[]{:S(2)}) collective-permute-start(f32[129,128]{1,0:T(8,128)S(1)} %pad_maximum_fusion.14), channel_id=1, source_target_pairs={{0,64},{16,80},{32,96},{48,112},{64,0},{80,16},{96,32},{112,48},{1... | collective-permute-start | bytes 198152 | tf_op jit(solution)/shard_map/ppermute | solution.py:76
  193.7 2.4 collective-permute-start.54
  196.4 3.7 %collective-permute-start.20 = (f32[128,128]{1,0:T(8,128)S(1)}, f32[128,128]{1,0:T(8,128)S(1)}, u32[]{:S(2)}, u32[]{:S(2)}) collective-permute-start(f32[128,128]{1,0:T(8,128)S(1)} %get-tuple-element.21), channel_id=1, source_target_pairs={{0,64},{16,80},{32,96},{48,112},{64,0},{80,16},{96,32},{112,48},{1... | collective-permute-start | bytes 196616 | tf_op jit(solution)/shard_map/ppermute | solution.py:85
  202.4 3.5 %collective-permute-start.21 = (f32[256,128]{1,0:T(8,128)S(1)}, f32[256,128]{1,0:T(8,128)S(1)}, u32[]{:S(2)}, u32[]{:S(2)}) collective-permute-start(f32[256,128]{1,0:T(8,128)S(1)} %constant_dynamic-update-slice_fusion.52), channel_id=1, source_target_pairs={{0,16},{16,0},{32,48},{48,32},{64,80},{80,64},{96,112},{112,96},{1... | collective-permute-start | bytes 393224 | tf_op jit(solution)/shard_map/ppermute | solution.py:85
  206.1 3.4 %collective-permute-start.56 = (f32[256,128]{1,0:T(8,128)S(1)}, f32[256,128]{1,0:T(8,128)S(1)}, u32[]{:S(2)}, u32[]{:S(2)}) collective-permute-start(f32[256,128]{1,0:T(8,128)S(1)} %constant_dynamic-update-slice_fusion.24), channel_id=1, source_target_pairs={{0,16},{16,0},{32,48},{48,32},{64,80},{80,64},{96,112},{112,96},{1... | collective-permute-start | bytes 393224 | tf_op jit(solution)/shard_map/ppermute | solution.py:85
  209.5 1.9 collective-permute-start.22
  214.1 2.9 collective-permute-done.22
  217.3 2.5 collective-permute-done.57
  220.1 1.9 collective-permute-start.24
  227.3 1.9 collective-permute-start.26
  243.5 4.2 %collective-permute-done.28 = bf16[515,128]{1,0:T(8,128)(2,1)S(1)} collective-permute-done((bf16[515,128]{1,0:T(8,128)(2,1)S(1)}, bf16[515,128]{1,0:T(8,128)(2,1)S(1)}, u32[]{:S(2)}, u32[]{:S(2)}) %collective-permute-start.28) | collective-permute-done | bytes 131872 | tf_op jit(solution)/shard_map/ppermute | solution.py:76
  250.6 1.9 collective-permute-done.29
  254.6 1.9 collective-permute-start.65
  258.2 2.0 collective-permute-start.31
  260.3 1.9 collective-permute-start.66
  273.4 2.0 collective-permute-done.68
  281.3 5.5 %collective-permute-done.35 = f32[513,128]{1,0:T(8,128)S(1)} collective-permute-done((f32[513,128]{1,0:T(8,128)S(1)}, f32[513,128]{1,0:T(8,128)S(1)}, u32[]{:S(2)}, u32[]{:S(2)}) %collective-permute-start.35) | collective-permute-done | bytes 262688 | tf_op jit(solution)/shard_map/ppermute | solution.py:76
  286.9 2.4 collective-permute-start.36
  289.2 2.8 collective-permute-done.70
  292.1 2.4 collective-permute-start.71
  294.5 2.4 collective-permute-start.37
  297.0 1.8 collective-permute-done.71
  298.9 2.1 collective-permute-start.72
  301.0 1.9 collective-permute-start.73
  302.9 2.2 collective-permute-done.72
  307.1 3.1 collective-permute-start.74
  311.0 2.7 collective-permute-start.77
  315.5 2.1 collective-permute-done.77
  318.8 4.0 %collective-permute-done.75 = f32[512,128]{1,0:T(8,128)S(1)} collective-permute-done((f32[512,128]{1,0:T(8,128)S(1)}, f32[512,128]{1,0:T(8,128)S(1)}, u32[]{:S(2)}, u32[]{:S(2)}) %collective-permute-start.75) | collective-permute-done | bytes 262176 | tf_op jit(solution)/shard_map/ppermute | solution.py:85
  323.1 2.5 collective-permute-done.78
  (407 shorter events, 96.2 us)
Async XLA Ops:
  7.2 42.5 %all-gather.2.cloned.1.call-start = ((), (), s32[]{:S(2)}) async-start(), calls=%async_computation | async-start | bytes 4456448 | tf_op jit(solution)/shard_map/all_gather | solution.py:136
  63.0 5.1 %collective-permute-start.1 = (f32[1024]{0:T(1024)S(1)}, f32[1024]{0:T(1024)S(1)}, u32[]{:S(2)}, u32[]{:S(2)}) collective-permute-start(f32[1024]{0:T(1024)S(1)} %add.823), channel_id=1, source_target_pairs={{0,16},{16,0},{32,48},{48,32},{64,80},{80,64},{96,112},{112,96},{1... | collective-permute-start | bytes 12296 | tf_op jit(solution)/shard_map/ppermute | solution.py:37
  68.1 5.1 %collective-permute-start.2 = (f32[1024]{0:T(1024)S(1)}, f32[1024]{0:T(1024)S(1)}, u32[]{:S(2)}, u32[]{:S(2)}) collective-permute-start(f32[1024]{0:T(1024)S(1)} %add.824), channel_id=1, source_target_pairs={{0,64},{16,80},{32,96},{48,112},{64,0},{80,16},{96,32},{112,48},{1... | collective-permute-start | bytes 12296 | tf_op jit(solution)/shard_map/ppermute | solution.py:37
  78.9 7.9 %collective-permute-start.3 = (f32[512,128]{1,0:T(8,128)S(1)}, f32[512,128]{1,0:T(8,128)S(1)}, u32[]{:S(2)}, u32[]{:S(2)}) collective-permute-start(f32[512,128]{1,0:T(8,128)S(1)} %constant_dynamic-slice_fusion.17), channel_id=1, source_target_pairs={{0,32},{16,48},{32,0},{48,16},{64,96},{80,112},{96,64},{112,80},{1... | collective-permute-start | bytes 786440 | tf_op jit(solution)/shard_map/ppermute | solution.py:76
  81.7 8.0 %collective-permute-start.38 = (f32[512,128]{1,0:T(8,128)S(1)}, f32[512,128]{1,0:T(8,128)S(1)}, u32[]{:S(2)}, u32[]{:S(2)}) collective-permute-start(f32[512,128]{1,0:T(8,128)S(1)} %constant_dynamic-slice_fusion.8), channel_id=1, source_target_pairs={{0,32},{16,48},{32,0},{48,16},{64,96},{80,112},{96,64},{112,80},{1... | collective-permute-start | bytes 786440 | tf_op jit(solution)/shard_map/ppermute | solution.py:76
  86.9 6.6 %collective-permute-start.4 = (f32[256,128]{1,0:T(8,128)S(1)}, f32[256,128]{1,0:T(8,128)S(1)}, u32[]{:S(2)}, u32[]{:S(2)}) collective-permute-start(f32[256,128]{1,0:T(8,128)S(1)} %constant_dynamic-slice_fusion.16), channel_id=1, source_target_pairs={{0,16},{16,0},{32,48},{48,32},{64,80},{80,64},{96,112},{112,96},{1... | collective-permute-start | bytes 393224 | tf_op jit(solution)/shard_map/ppermute | solution.py:76
  89.7 6.7 %collective-permute-start.39 = (f32[256,128]{1,0:T(8,128)S(1)}, f32[256,128]{1,0:T(8,128)S(1)}, u32[]{:S(2)}, u32[]{:S(2)}) collective-permute-start(f32[256,128]{1,0:T(8,128)S(1)} %constant_dynamic-slice_fusion.7), channel_id=1, source_target_pairs={{0,16},{16,0},{32,48},{48,32},{64,80},{80,64},{96,112},{112,96},{1... | collective-permute-start | bytes 393224 | tf_op jit(solution)/shard_map/ppermute | solution.py:76
  93.5 5.9 %collective-permute-start.5 = (f32[128,128]{1,0:T(8,128)S(1)}, f32[128,128]{1,0:T(8,128)S(1)}, u32[]{:S(2)}, u32[]{:S(2)}) collective-permute-start(f32[128,128]{1,0:T(8,128)S(1)} %constant_dynamic-slice_fusion.15), channel_id=1, source_target_pairs={{0,64},{16,80},{32,96},{48,112},{64,0},{80,16},{96,32},{112,48},{1... | collective-permute-start | bytes 196616 | tf_op jit(solution)/shard_map/ppermute | solution.py:76
  96.5 5.8 %collective-permute-start.40 = (f32[128,128]{1,0:T(8,128)S(1)}, f32[128,128]{1,0:T(8,128)S(1)}, u32[]{:S(2)}, u32[]{:S(2)}) collective-permute-start(f32[128,128]{1,0:T(8,128)S(1)} %constant_dynamic-slice_fusion.6), channel_id=1, source_target_pairs={{0,64},{16,80},{32,96},{48,112},{64,0},{80,16},{96,32},{112,48},{1... | collective-permute-start | bytes 196616 | tf_op jit(solution)/shard_map/ppermute | solution.py:76
  99.4 5.8 %collective-permute-start.6 = (f32[128,128]{1,0:T(8,128)S(1)}, f32[128,128]{1,0:T(8,128)S(1)}, u32[]{:S(2)}, u32[]{:S(2)}) collective-permute-start(f32[128,128]{1,0:T(8,128)S(1)} %get-tuple-element.31), channel_id=1, source_target_pairs={{0,64},{16,80},{32,96},{48,112},{64,0},{80,16},{96,32},{112,48},{1... | collective-permute-start | bytes 196616 | tf_op jit(solution)/shard_map/ppermute | solution.py:85
  102.3 6.0 %collective-permute-start.41 = (f32[128,128]{1,0:T(8,128)S(1)}, f32[128,128]{1,0:T(8,128)S(1)}, u32[]{:S(2)}, u32[]{:S(2)}) collective-permute-start(f32[128,128]{1,0:T(8,128)S(1)} %get-tuple-element.57), channel_id=1, source_target_pairs={{0,64},{16,80},{32,96},{48,112},{64,0},{80,16},{96,32},{112,48},{1... | collective-permute-start | bytes 196616 | tf_op jit(solution)/shard_map/ppermute | solution.py:85
  105.3 6.6 %collective-permute-start.7 = (f32[256,128]{1,0:T(8,128)S(1)}, f32[256,128]{1,0:T(8,128)S(1)}, u32[]{:S(2)}, u32[]{:S(2)}) collective-permute-start(f32[256,128]{1,0:T(8,128)S(1)} %constant_dynamic-update-slice_fusion.66), channel_id=1, source_target_pairs={{0,16},{16,0},{32,48},{48,32},{64,80},{80,64},{96,112},{112,96},{1... | collective-permute-start | bytes 393224 | tf_op jit(solution)/shard_map/ppermute | solution.py:85
  108.3 6.6 %collective-permute-start.42 = (f32[256,128]{1,0:T(8,128)S(1)}, f32[256,128]{1,0:T(8,128)S(1)}, u32[]{:S(2)}, u32[]{:S(2)}) collective-permute-start(f32[256,128]{1,0:T(8,128)S(1)} %constant_dynamic-update-slice_fusion.38), channel_id=1, source_target_pairs={{0,16},{16,0},{32,48},{48,32},{64,80},{80,64},{96,112},{112,96},{1... | collective-permute-start | bytes 393224 | tf_op jit(solution)/shard_map/ppermute | solution.py:85
  111.8 6.5 %collective-permute-start.8 = (f32[512,128]{1,0:T(8,128)S(1)}, f32[512,128]{1,0:T(8,128)S(1)}, u32[]{:S(2)}, u32[]{:S(2)}) collective-permute-start(f32[512,128]{1,0:T(8,128)S(1)} %constant_dynamic-update-slice_fusion.64), channel_id=1, source_target_pairs={{0,32},{16,48},{32,0},{48,16},{64,96},{80,112},{96,64},{112,80},{1... | collective-permute-start | bytes 786440 | tf_op jit(solution)/shard_map/ppermute | solution.py:85
  114.9 6.7 %collective-permute-start.43 = (f32[512,128]{1,0:T(8,128)S(1)}, f32[512,128]{1,0:T(8,128)S(1)}, u32[]{:S(2)}, u32[]{:S(2)}) collective-permute-start(f32[512,128]{1,0:T(8,128)S(1)} %constant_dynamic-update-slice_fusion.36), channel_id=1, source_target_pairs={{0,32},{16,48},{32,0},{48,16},{64,96},{80,112},{96,64},{112,80},{1... | collective-permute-start | bytes 786440 | tf_op jit(solution)/shard_map/ppermute | solution.py:85
  121.2 5.6 %collective-permute-start.9 = (bf16[1030,128]{1,0:T(8,128)(2,1)}, bf16[1030,128]{1,0:T(8,128)(2,1)}, u32[]{:S(2)}, u32[]{:S(2)}) collective-permute-start(bf16[1030,128]{1,0:T(8,128)(2,1)} %concatenate.145), channel_id=1, source_target_pairs={{0,1},{1,0},{2,3},{3,2},{4,5},{5,4},{6,7},{7,6},{8,9},{9,8},{10,11... | collective-permute-start | bytes 791048 | tf_op jit(solution)/shard_map/ppermute | solution.py:76
  128.6 6.5 %collective-permute-start.10 = (bf16[518,128]{1,0:T(8,128)(2,1)S(1)}, bf16[518,128]{1,0:T(8,128)(2,1)S(1)}, u32[]{:S(2)}, u32[]{:S(2)}) collective-permute-start(bf16[518,128]{1,0:T(8,128)(2,1)S(1)} %pad_maximum_fusion.10), channel_id=1, source_target_pairs={{0,2},{1,3},{2,0},{3,1},{4,6},{5,7},{6,4},{7,5},{8,10},{9,11},{10,... | collective-permute-start | bytes 397832 | tf_op jit(solution)/shard_map/ppermute | solution.py:76
  130.5 6.9 %collective-permute-start.45 = (bf16[518,128]{1,0:T(8,128)(2,1)S(1)}, bf16[518,128]{1,0:T(8,128)(2,1)S(1)}, u32[]{:S(2)}, u32[]{:S(2)}) collective-permute-start(bf16[518,128]{1,0:T(8,128)(2,1)S(1)} %pad_maximum_fusion.12), channel_id=1, source_target_pairs={{0,2},{1,3},{2,0},{3,1},{4,6},{5,7},{6,4},{7,5},{8,10},{9,11},{10,... | collective-permute-start | bytes 397832 | tf_op jit(solution)/shard_map/ppermute | solution.py:76
  135.2 4.4 %collective-permute-start.11 = (bf16[262,128]{1,0:T(8,128)(2,1)S(1)}, bf16[262,128]{1,0:T(8,128)(2,1)S(1)}, u32[]{:S(2)}, u32[]{:S(2)}) collective-permute-start(bf16[262,128]{1,0:T(8,128)(2,1)S(1)} %pad_maximum_fusion.18), channel_id=1, source_target_pairs={{0,4},{1,5},{2,6},{3,7},{4,0},{5,1},{6,2},{7,3},{8,12},{9,13},{10,... | collective-permute-start | bytes 201224 | tf_op jit(solution)/shard_map/ppermute | solution.py:76
  137.6 4.7 %collective-permute-start.46 = (bf16[262,128]{1,0:T(8,128)(2,1)S(1)}, bf16[262,128]{1,0:T(8,128)(2,1)S(1)}, u32[]{:S(2)}, u32[]{:S(2)}) collective-permute-start(bf16[262,128]{1,0:T(8,128)(2,1)S(1)} %pad_maximum_fusion.20), channel_id=1, source_target_pairs={{0,4},{1,5},{2,6},{3,7},{4,0},{5,1},{6,2},{7,3},{8,12},{9,13},{10,... | collective-permute-start | bytes 201224 | tf_op jit(solution)/shard_map/ppermute | solution.py:76
  139.6 5.8 %collective-permute-start.12 = (bf16[134,128]{1,0:T(8,128)(2,1)S(1)}, bf16[134,128]{1,0:T(8,128)(2,1)S(1)}, u32[]{:S(2)}, u32[]{:S(2)}) collective-permute-start(bf16[134,128]{1,0:T(8,128)(2,1)S(1)} %pad_maximum_fusion.22), channel_id=1, source_target_pairs={{0,8},{1,9},{2,10},{3,11},{4,12},{5,13},{6,14},{7,15},{8,0},{9,1},... | collective-permute-start | bytes 102920 | tf_op jit(solution)/shard_map/ppermute | solution.py:76
  142.4 5.6 %collective-permute-start.47 = (bf16[134,128]{1,0:T(8,128)(2,1)S(1)}, bf16[134,128]{1,0:T(8,128)(2,1)S(1)}, u32[]{:S(2)}, u32[]{:S(2)}) collective-permute-start(bf16[134,128]{1,0:T(8,128)(2,1)S(1)} %pad_maximum_fusion.24), channel_id=1, source_target_pairs={{0,8},{1,9},{2,10},{3,11},{4,12},{5,13},{6,14},{7,15},{8,0},{9,1},... | collective-permute-start | bytes 102920 | tf_op jit(solution)/shard_map/ppermute | solution.py:76
  145.5 5.5 %collective-permute-start.13 = (bf16[128,128]{1,0:T(8,128)(2,1)S(1)}, bf16[128,128]{1,0:T(8,128)(2,1)S(1)}, u32[]{:S(2)}, u32[]{:S(2)}) collective-permute-start(bf16[128,128]{1,0:T(8,128)(2,1)S(1)} %get-tuple-element.23), channel_id=1, source_target_pairs={{0,8},{1,9},{2,10},{3,11},{4,12},{5,13},{6,14},{7,15},{8,0},{9,1},... | collective-permute-start | bytes 98312 | tf_op jit(solution)/shard_map/ppermute | solution.py:85
  148.1 5.5 %collective-permute-start.48 = (bf16[128,128]{1,0:T(8,128)(2,1)S(1)}, bf16[128,128]{1,0:T(8,128)(2,1)S(1)}, u32[]{:S(2)}, u32[]{:S(2)}) collective-permute-start(bf16[128,128]{1,0:T(8,128)(2,1)S(1)} %get-tuple-element.49), channel_id=1, source_target_pairs={{0,8},{1,9},{2,10},{3,11},{4,12},{5,13},{6,14},{7,15},{8,0},{9,1},... | collective-permute-start | bytes 98312 | tf_op jit(solution)/shard_map/ppermute | solution.py:85
  153.6 4.3 %collective-permute-start.49 = (bf16[256,128]{1,0:T(8,128)(2,1)S(1)}, bf16[256,128]{1,0:T(8,128)(2,1)S(1)}, u32[]{:S(2)}, u32[]{:S(2)}) collective-permute-start(bf16[256,128]{1,0:T(8,128)(2,1)S(1)} %constant_dynamic-update-slice_fusion.32), channel_id=1, source_target_pairs={{0,4},{1,5},{2,6},{3,7},{4,0},{5,1},{6,2},{7,3},{8,12},{9,13},{10,... | collective-permute-start | bytes 196616 | tf_op jit(solution)/shard_map/ppermute | solution.py:85
  155.3 5.0 %collective-permute-start.15 = (bf16[512,128]{1,0:T(8,128)(2,1)S(1)}, bf16[512,128]{1,0:T(8,128)(2,1)S(1)}, u32[]{:S(2)}, u32[]{:S(2)}) collective-permute-start(bf16[512,128]{1,0:T(8,128)(2,1)S(1)} %constant_dynamic-update-slice_fusion.58), channel_id=1, source_target_pairs={{0,2},{1,3},{2,0},{3,1},{4,6},{5,7},{6,4},{7,5},{8,10},{9,11},{10,... | collective-permute-start | bytes 393224 | tf_op jit(solution)/shard_map/ppermute | solution.py:85
  157.8 5.0 %collective-permute-start.50 = (bf16[512,128]{1,0:T(8,128)(2,1)S(1)}, bf16[512,128]{1,0:T(8,128)(2,1)S(1)}, u32[]{:S(2)}, u32[]{:S(2)}) collective-permute-start(bf16[512,128]{1,0:T(8,128)(2,1)S(1)} %constant_dynamic-update-slice_fusion.30), channel_id=1, source_target_pairs={{0,2},{1,3},{2,0},{3,1},{4,6},{5,7},{6,4},{7,5},{8,10},{9,11},{10,... | collective-permute-start | bytes 393224 | tf_op jit(solution)/shard_map/ppermute | solution.py:85
  164.9 9.3 %collective-permute-start.17 = (f32[513,128]{1,0:T(8,128)S(1)}, f32[513,128]{1,0:T(8,128)S(1)}, u32[]{:S(2)}, u32[]{:S(2)}) collective-permute-start(f32[513,128]{1,0:T(8,128)S(1)} %pad_maximum_fusion.2), channel_id=1, source_target_pairs={{0,32},{16,48},{32,0},{48,16},{64,96},{80,112},{96,64},{112,80},{1... | collective-permute-start | bytes 787976 | tf_op jit(solution)/shard_map/ppermute | solution.py:76
  168.4 17.9 %collective-permute-start.52 = (f32[513,128]{1,0:T(8,128)S(1)}, f32[513,128]{1,0:T(8,128)S(1)}, u32[]{:S(2)}, u32[]{:S(2)}) collective-permute-start(f32[513,128]{1,0:T(8,128)S(1)} %pad_maximum_fusion.4), channel_id=1, source_target_pairs={{0,32},{16,48},{32,0},{48,16},{64,96},{80,112},{96,64},{112,80},{1... | collective-permute-start | bytes 787976 | tf_op jit(solution)/shard_map/ppermute | solution.py:76
  174.4 15.7 %collective-permute-start.18 = (f32[257,128]{1,0:T(8,128)S(1)}, f32[257,128]{1,0:T(8,128)S(1)}, u32[]{:S(2)}, u32[]{:S(2)}) collective-permute-start(f32[257,128]{1,0:T(8,128)S(1)} %pad_maximum_fusion.6), channel_id=1, source_target_pairs={{0,16},{16,0},{32,48},{48,32},{64,80},{80,64},{96,112},{112,96},{1... | collective-permute-start | bytes 394760 | tf_op jit(solution)/shard_map/ppermute | solution.py:76
  186.4 7.2 %collective-permute-start.53 = (f32[257,128]{1,0:T(8,128)S(1)}, f32[257,128]{1,0:T(8,128)S(1)}, u32[]{:S(2)}, u32[]{:S(2)}) collective-permute-start(f32[257,128]{1,0:T(8,128)S(1)} %pad_maximum_fusion.8), channel_id=1, source_target_pairs={{0,16},{16,0},{32,48},{48,32},{64,80},{80,64},{96,112},{112,96},{1... | collective-permute-start | bytes 394760 | tf_op jit(solution)/shard_map/ppermute | solution.py:76
  190.1 6.2 %collective-permute-start.19 = (f32[129,128]{1,0:T(8,128)S(1)}, f32[129,128]{1,0:T(8,128)S(1)}, u32[]{:S(2)}, u32[]{:S(2)}) collective-permute-start(f32[129,128]{1,0:T(8,128)S(1)} %pad_maximum_fusion.14), channel_id=1, source_target_pairs={{0,64},{16,80},{32,96},{48,112},{64,0},{80,16},{96,32},{112,48},{1... | collective-permute-start | bytes 198152 | tf_op jit(solution)/shard_map/ppermute | solution.py:76
  193.7 6.5 %collective-permute-start.54 = (f32[129,128]{1,0:T(8,128)S(1)}, f32[129,128]{1,0:T(8,128)S(1)}, u32[]{:S(2)}, u32[]{:S(2)}) collective-permute-start(f32[129,128]{1,0:T(8,128)S(1)} %pad_maximum_fusion.16), channel_id=1, source_target_pairs={{0,64},{16,80},{32,96},{48,112},{64,0},{80,16},{96,32},{112,48},{1... | collective-permute-start | bytes 198152 | tf_op jit(solution)/shard_map/ppermute | solution.py:76
  196.4 6.0 %collective-permute-start.20 = (f32[128,128]{1,0:T(8,128)S(1)}, f32[128,128]{1,0:T(8,128)S(1)}, u32[]{:S(2)}, u32[]{:S(2)}) collective-permute-start(f32[128,128]{1,0:T(8,128)S(1)} %get-tuple-element.21), channel_id=1, source_target_pairs={{0,64},{16,80},{32,96},{48,112},{64,0},{80,16},{96,32},{112,48},{1... | collective-permute-start | bytes 196616 | tf_op jit(solution)/shard_map/ppermute | solution.py:85
  200.2 5.8 %collective-permute-start.55 = (f32[128,128]{1,0:T(8,128)S(1)}, f32[128,128]{1,0:T(8,128)S(1)}, u32[]{:S(2)}, u32[]{:S(2)}) collective-permute-start(f32[128,128]{1,0:T(8,128)S(1)} %get-tuple-element.47), channel_id=1, source_target_pairs={{0,64},{16,80},{32,96},{48,112},{64,0},{80,16},{96,32},{112,48},{1... | collective-permute-start | bytes 196616 | tf_op jit(solution)/shard_map/ppermute | solution.py:85
  202.4 7.1 %collective-permute-start.21 = (f32[256,128]{1,0:T(8,128)S(1)}, f32[256,128]{1,0:T(8,128)S(1)}, u32[]{:S(2)}, u32[]{:S(2)}) collective-permute-start(f32[256,128]{1,0:T(8,128)S(1)} %constant_dynamic-update-slice_fusion.52), channel_id=1, source_target_pairs={{0,16},{16,0},{32,48},{48,32},{64,80},{80,64},{96,112},{112,96},{1... | collective-permute-start | bytes 393224 | tf_op jit(solution)/shard_map/ppermute | solution.py:85
  206.1 6.6 %collective-permute-start.56 = (f32[256,128]{1,0:T(8,128)S(1)}, f32[256,128]{1,0:T(8,128)S(1)}, u32[]{:S(2)}, u32[]{:S(2)}) collective-permute-start(f32[256,128]{1,0:T(8,128)S(1)} %constant_dynamic-update-slice_fusion.24), channel_id=1, source_target_pairs={{0,16},{16,0},{32,48},{48,32},{64,80},{80,64},{96,112},{112,96},{1... | collective-permute-start | bytes 393224 | tf_op jit(solution)/shard_map/ppermute | solution.py:85
  209.5 7.5 %collective-permute-start.22 = (f32[512,128]{1,0:T(8,128)S(1)}, f32[512,128]{1,0:T(8,128)S(1)}, u32[]{:S(2)}, u32[]{:S(2)}) collective-permute-start(f32[512,128]{1,0:T(8,128)S(1)} %constant_dynamic-update-slice_fusion.50), channel_id=1, source_target_pairs={{0,32},{16,48},{32,0},{48,16},{64,96},{80,112},{96,64},{112,80},{1... | collective-permute-start | bytes 786440 | tf_op jit(solution)/shard_map/ppermute | solution.py:85
  212.7 7.2 %collective-permute-start.57 = (f32[512,128]{1,0:T(8,128)S(1)}, f32[512,128]{1,0:T(8,128)S(1)}, u32[]{:S(2)}, u32[]{:S(2)}) collective-permute-start(f32[512,128]{1,0:T(8,128)S(1)} %constant_dynamic-update-slice_fusion.22), channel_id=1, source_target_pairs={{0,32},{16,48},{32,0},{48,16},{64,96},{80,112},{96,64},{112,80},{1... | collective-permute-start | bytes 786440 | tf_op jit(solution)/shard_map/ppermute | solution.py:85
  227.3 5.1 %collective-permute-start.26 = (f32[128]{0:T(128)S(1)}, f32[128]{0:T(128)S(1)}, u32[]{:S(2)}, u32[]{:S(2)}) collective-permute-start(f32[128]{0:T(128)S(1)} %add.885), channel_id=1, source_target_pairs={{0,8},{1,9},{2,10},{3,11},{4,12},{5,13},{6,14},{7,15},{8,0},{9,1},... | collective-permute-start | bytes 1544 | tf_op jit(solution)/shard_map/ppermute | solution.py:37
  229.3 5.1 %collective-permute-start.61 = (f32[128]{0:T(128)S(1)}, f32[128]{0:T(128)S(1)}, u32[]{:S(2)}, u32[]{:S(2)}) collective-permute-start(f32[128]{0:T(128)S(1)} %add.954), channel_id=1, source_target_pairs={{0,8},{1,9},{2,10},{3,11},{4,12},{5,13},{6,14},{7,15},{8,0},{9,1},... | collective-permute-start | bytes 1544 | tf_op jit(solution)/shard_map/ppermute | solution.py:37
  241.1 6.5 %collective-permute-start.28 = (bf16[515,128]{1,0:T(8,128)(2,1)S(1)}, bf16[515,128]{1,0:T(8,128)(2,1)S(1)}, u32[]{:S(2)}, u32[]{:S(2)}) collective-permute-start(bf16[515,128]{1,0:T(8,128)(2,1)S(1)} %pad_maximum_fusion.11), channel_id=1, source_target_pairs={{0,2},{1,3},{2,0},{3,1},{4,6},{5,7},{6,4},{7,5},{8,10},{9,11},{10,... | collective-permute-start | bytes 395528 | tf_op jit(solution)/shard_map/ppermute | solution.py:76
  243.1 6.6 %collective-permute-start.63 = (bf16[515,128]{1,0:T(8,128)(2,1)S(1)}, bf16[515,128]{1,0:T(8,128)(2,1)S(1)}, u32[]{:S(2)}, u32[]{:S(2)}) collective-permute-start(bf16[515,128]{1,0:T(8,128)(2,1)S(1)} %pad_maximum_fusion.13), channel_id=1, source_target_pairs={{0,2},{1,3},{2,0},{3,1},{4,6},{5,7},{6,4},{7,5},{8,10},{9,11},{10,... | collective-permute-start | bytes 395528 | tf_op jit(solution)/shard_map/ppermute | solution.py:76
  247.7 4.8 %collective-permute-start.29 = (bf16[259,128]{1,0:T(8,128)(2,1)S(1)}, bf16[259,128]{1,0:T(8,128)(2,1)S(1)}, u32[]{:S(2)}, u32[]{:S(2)}) collective-permute-start(bf16[259,128]{1,0:T(8,128)(2,1)S(1)} %pad_maximum_fusion.19), channel_id=1, source_target_pairs={{0,4},{1,5},{2,6},{3,7},{4,0},{5,1},{6,2},{7,3},{8,12},{9,13},{10,... | collective-permute-start | bytes 198920 | tf_op jit(solution)/shard_map/ppermute | solution.py:76
  249.7 4.7 %collective-permute-start.64 = (bf16[259,128]{1,0:T(8,128)(2,1)S(1)}, bf16[259,128]{1,0:T(8,128)(2,1)S(1)}, u32[]{:S(2)}, u32[]{:S(2)}) collective-permute-start(bf16[259,128]{1,0:T(8,128)(2,1)S(1)} %pad_maximum_fusion.21), channel_id=1, source_target_pairs={{0,4},{1,5},{2,6},{3,7},{4,0},{5,1},{6,2},{7,3},{8,12},{9,13},{10,... | collective-permute-start | bytes 198920 | tf_op jit(solution)/shard_map/ppermute | solution.py:76
  252.7 5.5 %collective-permute-start.30 = (bf16[131,128]{1,0:T(8,128)(2,1)S(1)}, bf16[131,128]{1,0:T(8,128)(2,1)S(1)}, u32[]{:S(2)}, u32[]{:S(2)}) collective-permute-start(bf16[131,128]{1,0:T(8,128)(2,1)S(1)} %pad_maximum_fusion.23), channel_id=1, source_target_pairs={{0,8},{1,9},{2,10},{3,11},{4,12},{5,13},{6,14},{7,15},{8,0},{9,1},... | collective-permute-start | bytes 100616 | tf_op jit(solution)/shard_map/ppermute | solution.py:76
  254.6 5.7 %collective-permute-start.65 = (bf16[131,128]{1,0:T(8,128)(2,1)S(1)}, bf16[131,128]{1,0:T(8,128)(2,1)S(1)}, u32[]{:S(2)}, u32[]{:S(2)}) collective-permute-start(bf16[131,128]{1,0:T(8,128)(2,1)S(1)} %pad_maximum_fusion.25), channel_id=1, source_target_pairs={{0,8},{1,9},{2,10},{3,11},{4,12},{5,13},{6,14},{7,15},{8,0},{9,1},... | collective-permute-start | bytes 100616 | tf_op jit(solution)/shard_map/ppermute | solution.py:76
  258.2 5.7 %collective-permute-start.31 = (bf16[128,128]{1,0:T(8,128)(2,1)S(1)}, bf16[128,128]{1,0:T(8,128)(2,1)S(1)}, u32[]{:S(2)}, u32[]{:S(2)}) collective-permute-start(bf16[128,128]{1,0:T(8,128)(2,1)S(1)} %get-tuple-element.9), channel_id=1, source_target_pairs={{0,8},{1,9},{2,10},{3,11},{4,12},{5,13},{6,14},{7,15},{8,0},{9,1},... | collective-permute-start | bytes 98312 | tf_op jit(solution)/shard_map/ppermute | solution.py:85
  260.3 5.8 %collective-permute-start.66 = (bf16[128,128]{1,0:T(8,128)(2,1)S(1)}, bf16[128,128]{1,0:T(8,128)(2,1)S(1)}, u32[]{:S(2)}, u32[]{:S(2)}) collective-permute-start(bf16[128,128]{1,0:T(8,128)(2,1)S(1)} %get-tuple-element.35), channel_id=1, source_target_pairs={{0,8},{1,9},{2,10},{3,11},{4,12},{5,13},{6,14},{7,15},{8,0},{9,1},... | collective-permute-start | bytes 98312 | tf_op jit(solution)/shard_map/ppermute | solution.py:85
  264.0 4.3 %collective-permute-start.32 = (bf16[256,128]{1,0:T(8,128)(2,1)S(1)}, bf16[256,128]{1,0:T(8,128)(2,1)S(1)}, u32[]{:S(2)}, u32[]{:S(2)}) collective-permute-start(bf16[256,128]{1,0:T(8,128)(2,1)S(1)} %constant_dynamic-update-slice_fusion.46), channel_id=1, source_target_pairs={{0,4},{1,5},{2,6},{3,7},{4,0},{5,1},{6,2},{7,3},{8,12},{9,13},{10,... | collective-permute-start | bytes 196616 | tf_op jit(solution)/shard_map/ppermute | solution.py:85
  268.2 5.0 %collective-permute-start.33 = (bf16[512,128]{1,0:T(8,128)(2,1)S(1)}, bf16[512,128]{1,0:T(8,128)(2,1)S(1)}, u32[]{:S(2)}, u32[]{:S(2)}) collective-permute-start(bf16[512,128]{1,0:T(8,128)(2,1)S(1)} %constant_dynamic-update-slice_fusion.44), channel_id=1, source_target_pairs={{0,2},{1,3},{2,0},{3,1},{4,6},{5,7},{6,4},{7,5},{8,10},{9,11},{10,... | collective-permute-start | bytes 393224 | tf_op jit(solution)/shard_map/ppermute | solution.py:85
  270.3 5.0 %collective-permute-start.68 = (bf16[512,128]{1,0:T(8,128)(2,1)S(1)}, bf16[512,128]{1,0:T(8,128)(2,1)S(1)}, u32[]{:S(2)}, u32[]{:S(2)}) collective-permute-start(bf16[512,128]{1,0:T(8,128)(2,1)S(1)} %constant_dynamic-update-slice_fusion.16), channel_id=1, source_target_pairs={{0,2},{1,3},{2,0},{3,1},{4,6},{5,7},{6,4},{7,5},{8,10},{9,11},{10,... | collective-permute-start | bytes 393224 | tf_op jit(solution)/shard_map/ppermute | solution.py:85
  277.4 9.3 %collective-permute-start.35 = (f32[513,128]{1,0:T(8,128)S(1)}, f32[513,128]{1,0:T(8,128)S(1)}, u32[]{:S(2)}, u32[]{:S(2)}) collective-permute-start(f32[513,128]{1,0:T(8,128)S(1)} %pad_maximum_fusion.3), channel_id=1, source_target_pairs={{0,32},{16,48},{32,0},{48,16},{64,96},{80,112},{96,64},{112,80},{1... | collective-permute-start | bytes 787976 | tf_op jit(solution)/shard_map/ppermute | solution.py:76
  280.1 11.9 %collective-permute-start.70 = (f32[513,128]{1,0:T(8,128)S(1)}, f32[513,128]{1,0:T(8,128)S(1)}, u32[]{:S(2)}, u32[]{:S(2)}) collective-permute-start(f32[513,128]{1,0:T(8,128)S(1)} %pad_maximum_fusion.5), channel_id=1, source_target_pairs={{0,32},{16,48},{32,0},{48,16},{64,96},{80,112},{96,64},{112,80},{1... | collective-permute-start | bytes 787976 | tf_op jit(solution)/shard_map/ppermute | solution.py:76
  286.9 7.6 %collective-permute-start.36 = (f32[257,128]{1,0:T(8,128)S(1)}, f32[257,128]{1,0:T(8,128)S(1)}, u32[]{:S(2)}, u32[]{:S(2)}) collective-permute-start(f32[257,128]{1,0:T(8,128)S(1)} %pad_maximum_fusion.7), channel_id=1, source_target_pairs={{0,16},{16,0},{32,48},{48,32},{64,80},{80,64},{96,112},{112,96},{1... | collective-permute-start | bytes 394760 | tf_op jit(solution)/shard_map/ppermute | solution.py:76
  292.1 6.7 %collective-permute-start.71 = (f32[257,128]{1,0:T(8,128)S(1)}, f32[257,128]{1,0:T(8,128)S(1)}, u32[]{:S(2)}, u32[]{:S(2)}) collective-permute-start(f32[257,128]{1,0:T(8,128)S(1)} %pad_maximum_fusion.9), channel_id=1, source_target_pairs={{0,16},{16,0},{32,48},{48,32},{64,80},{80,64},{96,112},{112,96},{1... | collective-permute-start | bytes 394760 | tf_op jit(solution)/shard_map/ppermute | solution.py:76
  294.5 6.4 %collective-permute-start.37 = (f32[129,128]{1,0:T(8,128)S(1)}, f32[129,128]{1,0:T(8,128)S(1)}, u32[]{:S(2)}, u32[]{:S(2)}) collective-permute-start(f32[129,128]{1,0:T(8,128)S(1)} %pad_maximum_fusion.15), channel_id=1, source_target_pairs={{0,64},{16,80},{32,96},{48,112},{64,0},{80,16},{96,32},{112,48},{1... | collective-permute-start | bytes 198152 | tf_op jit(solution)/shard_map/ppermute | solution.py:76
  298.9 6.2 %collective-permute-start.72 = (f32[129,128]{1,0:T(8,128)S(1)}, f32[129,128]{1,0:T(8,128)S(1)}, u32[]{:S(2)}, u32[]{:S(2)}) collective-permute-start(f32[129,128]{1,0:T(8,128)S(1)} %pad_maximum_fusion.17), channel_id=1, source_target_pairs={{0,64},{16,80},{32,96},{48,112},{64,0},{80,16},{96,32},{112,48},{1... | collective-permute-start | bytes 198152 | tf_op jit(solution)/shard_map/ppermute | solution.py:76
  301.0 6.1 %collective-permute-start.73 = (f32[128,128]{1,0:T(8,128)S(1)}, f32[128,128]{1,0:T(8,128)S(1)}, u32[]{:S(2)}, u32[]{:S(2)}) collective-permute-start(f32[128,128]{1,0:T(8,128)S(1)} %get-tuple-element.3), channel_id=1, source_target_pairs={{0,64},{16,80},{32,96},{48,112},{64,0},{80,16},{96,32},{112,48},{1... | collective-permute-start | bytes 196616 | tf_op jit(solution)/shard_map/ppermute | solution.py:85
  305.1 5.8 %collective-permute-start.76 = (f32[128,128]{1,0:T(8,128)S(1)}, f32[128,128]{1,0:T(8,128)S(1)}, u32[]{:S(2)}, u32[]{:S(2)}) collective-permute-start(f32[128,128]{1,0:T(8,128)S(1)} %get-tuple-element.5), channel_id=1, source_target_pairs={{0,64},{16,80},{32,96},{48,112},{64,0},{80,16},{96,32},{112,48},{1... | collective-permute-start | bytes 196616 | tf_op jit(solution)/shard_map/ppermute | solution.py:85
  307.1 7.6 %collective-permute-start.74 = (f32[256,128]{1,0:T(8,128)S(1)}, f32[256,128]{1,0:T(8,128)S(1)}, u32[]{:S(2)}, u32[]{:S(2)}) collective-permute-start(f32[256,128]{1,0:T(8,128)S(1)} %constant_dynamic-update-slice_fusion.10), channel_id=1, source_target_pairs={{0,16},{16,0},{32,48},{48,32},{64,80},{80,64},{96,112},{112,96},{1... | collective-permute-start | bytes 393224 | tf_op jit(solution)/shard_map/ppermute | solution.py:85
  311.0 6.6 %collective-permute-start.77 = (f32[256,128]{1,0:T(8,128)S(1)}, f32[256,128]{1,0:T(8,128)S(1)}, u32[]{:S(2)}, u32[]{:S(2)}) collective-permute-start(f32[256,128]{1,0:T(8,128)S(1)} %constant_dynamic-update-slice_fusion.4), channel_id=1, source_target_pairs={{0,16},{16,0},{32,48},{48,32},{64,80},{80,64},{96,112},{112,96},{1... | collective-permute-start | bytes 393224 | tf_op jit(solution)/shard_map/ppermute | solution.py:85
  314.7 8.1 %collective-permute-start.75 = (f32[512,128]{1,0:T(8,128)S(1)}, f32[512,128]{1,0:T(8,128)S(1)}, u32[]{:S(2)}, u32[]{:S(2)}) collective-permute-start(f32[512,128]{1,0:T(8,128)S(1)} %constant_dynamic-update-slice_fusion.8), channel_id=1, source_target_pairs={{0,32},{16,48},{32,0},{48,16},{64,96},{80,112},{96,64},{112,80},{1... | collective-permute-start | bytes 786440 | tf_op jit(solution)/shard_map/ppermute | solution.py:85
  317.6 8.0 %collective-permute-start.78 = (f32[512,128]{1,0:T(8,128)S(1)}, f32[512,128]{1,0:T(8,128)S(1)}, u32[]{:S(2)}, u32[]{:S(2)}) collective-permute-start(f32[512,128]{1,0:T(8,128)S(1)} %constant_dynamic-update-slice_fusion.2), channel_id=1, source_target_pairs={{0,32},{16,48},{32,0},{48,16},{64,96},{80,112},{96,64},{112,80},{1... | collective-permute-start | bytes 786440 | tf_op jit(solution)/shard_map/ppermute | solution.py:85
  (26 other events, 186.7 us)
Sparse Core Ops, SparseCore 0:
  9.7 39.9 all-gather.1

commit v2 on v1

--- a/solution.py
+++ b/solution.py
@@ -6,7 +6,11 @@
 from jax.sharding import PartitionSpec as P
 
 ITERS = 2
-GROUPS = 2
+GROUPS = 1
+
+
+def REDUCE(x, extra, axis, bits, gather_dtype, wire_dtype=jnp.bfloat16):
+    return exchange_sum(x, extra, axis, gather_dtype, wire_dtype)
 
 
 ridge = 0.5
@@ -89,11 +93,29 @@
     return x, extra
 
 
+def exchange_sum(x, extra, axis, gather_dtype, wire_dtype=jnp.bfloat16):
+    size = lax.axis_size(axis)
+    rows, columns = x.shape
+    chunks = x.reshape(size, rows // size, columns).astype(wire_dtype)
+    if extra is not None:
+        packed = pack_rows(extra, columns, wire_dtype)
+        chunks = jnp.concatenate(
+            [chunks, jnp.broadcast_to(packed[None], (size,) + packed.shape)], axis=1
+        )
+    got = lax.all_to_all(chunks, axis, 0, 0, tiled=False)
+    total = jnp.sum(got.astype(jnp.float32), axis=0)
+    part = total[: rows // size].astype(gather_dtype)
+    if extra is not None:
+        extra = unpack_rows(total[rows // size:], extra.shape[0] // columns, wire_dtype)
+    whole = lax.all_to_all(
+        jnp.broadcast_to(part[None], (size,) + part.shape), axis, 0, 0, tiled=False
+    )
+    return whole.reshape(rows, columns), extra
+
+
 def conjugate_gradients(kernel, targets, n_rows, sample_bits, landmark_bits):
     rhs_part = jnp.dot(kernel.T, targets, preferred_element_type=jnp.float32)
-    rhs_total, _ = halving_sum(
-        rhs_part, None, "sample", sample_bits, jnp.float32, jnp.float32
-    )
+    rhs_total, _ = REDUCE(rhs_part, None, "sample", sample_bits, jnp.float32, jnp.float32)
     rhs = rhs_total / math.sqrt(n_rows)
     weights = jnp.zeros_like(rhs)
     residual = rhs
@@ -105,7 +127,7 @@
         sums = [jnp.sum(direction * direction, axis=0)]
         if norm_now is None:
             sums.append(jnp.sum(residual * residual, axis=0))
-        row_half, landmark_sums = halving_sum(
+        row_half, landmark_sums = REDUCE(
             row_part, jnp.concatenate(sums), "landmark", landmark_bits, jnp.bfloat16
         )
         column_count = direction.shape[1]
@@ -114,7 +136,7 @@
             norm_now = landmark_sums[column_count:]
         row_square = jnp.sum(jnp.square(row_half.astype(jnp.float32)), axis=0)
         column_part = jnp.dot(kernel.T, row_half, preferred_element_type=jnp.float32)
-        column_total, row_square_total = halving_sum(
+        column_total, row_square_total = REDUCE(
             column_part, row_square, "sample", sample_bits, jnp.float32, jnp.float32
         )
         image = column_total / n_rows + ridge * direction

time: 340 us -> 311 us (0.915); the launches traced: 335 us -> 311 us
  blocking collectives: 0 us -> 147 us
  starting transfers between devices: 140 us -> 23.1 us
  waiting for transfers between devices: 118 us -> 71.5 us
  matrix products: 24.7 us -> 15.7 us
    all_to_all x0 -> x7, blocking collectives: none -> 147 us  [the longest x5 109 us: exchange_sum(): got = lax.all_to_all(chunks, axis, 0, 0, tiled=False)]
    ppermute x68 -> x0, starting transfers between devices: 124 us -> none  [the longest x34 62.2 us: halving_sum(): got = lax.ppermute(send, axis, perm)]
    ppermute x68 -> x0, waiting for transfers between devices: 78.5 us -> none  [the longest x34 43.8 us: halving_sum(): got = lax.ppermute(send, axis, perm)]
    all_to_all x0 -> x3, waiting for transfers between devices: none -> 28.6 us  [exchange_sum(): lax.all_to_all(jnp.broadcast_to(part[None], (size,) + part.shape), axis,...]
    all_to_all x0 -> x3, starting transfers between devices: none -> 10.7 us  [exchange_sum(): lax.all_to_all(jnp.broadcast_to(part[None], (size,) + part.shape), axis,...]
    dot_general x0 -> x1, local copies, waits for them, and re-layouts: none -> 6.4 us  [conjugate_gradients(): jnp.dot(kernel, direction_half, preferred_element_type=jnp.float32)]
    sub x0 -> x1, other arithmetic: none -> 5.64 us  [on_device(): kernel = (raw - column_mean[None, :]).astype(jnp.bfloat16)]
    concatenate x4 -> x0, local copies, waits for them, and re-layouts: 5.4 us -> none  [halving_sum(): jnp.concatenate([send, pack_rows(extra, columns, wire_dtype)], axis=0)]
  transfers between devices with their start and end apart: 80 -> 11, of which waited for: 57 -> 11; matrix products, arithmetic and copies ran while one was open for 12% -> 9% of each run, Pallas kernels for 0% -> 0%
where the time goes in v2:
time: 311 us
  blocking collectives  147 us (47%)
  waiting for transfers between devices  71.5 us (23%)
  local copies, waits for them, and re-layouts  24.1 us (8%)
  starting transfers between devices  23.1 us (7%)
  matrix products  15.7 us (5%)
  other arithmetic  15.1 us (5%)
  between operations  14.4 us (5%)
    all_to_all x5, blocking collectives, exchange_sum(): got = lax.all_to_all(chunks, axis, 0, 0, tiled=False)  109 us
    all_to_all x2, blocking collectives, exchange_sum(): lax.all_to_all(jnp.broadcast_to(part[None], (size,) + part.shape), axis,...  38.1 us
    all_to_all x3, waiting for transfers between devices, exchange_sum(): lax.all_to_all(jnp.broadcast_to(part[None], (size,) + part.shape), axis,...  28.6 us
    all_gather x1, waiting for transfers between devices, on_device(): gathered = lax.all_gather(summaries, 'landmark', axis=1, tiled=True)  27.2 us
    ppermute x7, waiting for transfers between devices, butterfly_sum(): x = x + lax.ppermute(x, axis, perm)  15 us
    ppermute x7, starting transfers between devices, butterfly_sum(): x = x + lax.ppermute(x, axis, perm)  12.4 us
    all_to_all x3, starting transfers between devices, exchange_sum(): lax.all_to_all(jnp.broadcast_to(part[None], (size,) + part.shape), axis,...  10.7 us
    gather x1, local copies, waits for them, and re-layouts, on_device(): anchors = jnp.take(pool, landmark_index, axis=0)  7.72 us
  transfers between devices with their start and end apart: 11, of which 11 were waited for; matrix products, arithmetic and copies ran while one was open for 9% of the time, Pallas kernels for 0%

profile of v2, /device:TPU:0, one launch (start us, length us, event | category | flops | bytes accessed | tf_op | source)
XLA Modules:
  0.0 310.6 jit_solution(12658293716645689984)
XLA Ops:
  7.2 0.7 all-gather.2.cloned.1.call-update
  7.9 0.7 fusion.12
  8.6 5.7 %gather_fusion.1 = s32[1024]{0:T(1024)S(1)} fusion(s32[2048]{0:T(1024)} %param.10, s32[1024]{0:T(1024)S(1)} %fusion.12), kind=kCustom, calls=%fused_computation.1 | custom fusion | bytes 12288 | tf_op jit(solution)/shard_map/jit(_take)/gather | solution.py:161
  14.4 7.7 %gather_fusion = bf16[1024,1024]{1,0:T(8,128)(2,1)S(1)} fusion(bf16[2048,1024]{1,0:T(8,128)(2,1)} %param.9, s32[1024]{0:T(1024)S(1)} %fusion.12), kind=kCustom, calls=%fused_computation | custom fusion | bytes 4198400 | tf_op jit(solution)/shard_map/jit(_take)/gather | solution.py:160
  22.1 0.1 select_reduce_fusion.1
  22.2 0.1 select_reduce_fusion
  22.4 27.2 %all-gather.2.cloned.1.call-done = bf16[2048,1024]{0,1:T(8,128)(2,1)} async-done(((bf16[2048,64]{0,1:T(8,128)(2,1)}), bf16[2048,1024]{0,1:T(8,128)(2,1)}) %all-gather.2.cloned.1.call-update) | async-done | bytes 4194320 | tf_op jit(solution)/shard_map/all_gather | solution.py:158
  49.6 7.3 %fusion = (f32[1024]{0:T(1024)S(1)}, f32[1024,2048]{1,0:T(8,128)S(1)}) fusion(f32[1024]{0:T(1024)S(1)} %broadcast_divide_fusion.1, f32[2048]{0:T(1024)S(1)} %broadcast_divide_fusion, bf16[2048,1024]{0,1:T(8,128)(2,1)} %all-gather.2.cloned.1.call-done, bf16[1024,1024]{1,0:T(8,128)(2,1)S(1)} %gather_fusion, pred[1024]{0:T(1024)(128)(4,1)S(1)} %get-tuple-element.5), kind=kOutput, calls=%fused_computation.4 | convolution fusion | flops 4302306304 | bytes 14697472 | tf_op jit(solution)/shard_map/dot_general | solution.py:27
  56.8 1.5 collective-permute-start
  58.4 2.1 collective-permute-done
  60.5 2.8 collective-permute-start.1
  63.3 2.3 collective-permute-done.1
  65.6 3.0 collective-permute-start.2
  68.6 2.1 collective-permute-done.2
  70.8 1.8 subtract_convert_fusion
  72.6 1.3 fusion.22
  73.9 0.7 copy-done.2
  74.6 20.1 %all_to_all.50 = f32[8,128,256]{2,1,0:T(8,128)S(1)} all-to-all(f32[8,128,256]{2,1,0:T(8,128)S(1)} %bitcast.75), channel_id=1, replica_groups=mesh['sample'=8,'landmark'=16] {'sample'}, dimensions={0} | all-to-all | bytes 2097152 | tf_op jit(solution)/shard_map/all_to_all | solution.py:105
  94.8 1.1 broadcast_in_dim.76
  95.8 3.6 %all-to-all-start.1 = ((f32[8,128,256]{2,1,0:T(8,128)}), f32[8,128,256]{2,1,0:T(8,128)S(1)}, u32[]{:S(2)}, u32[]{:S(2)}) async-start(f32[8,128,256]{2,1,0:T(8,128)} %broadcast_in_dim.76), calls=%async_computation.1 | async-start | bytes 2097152 | tf_op jit(solution)/shard_map/all_to_all | solution.py:110
  99.4 5.6 %fusion.36 = bf16[2048,1024]{0,1:T(8,128)(2,1)} fusion(f32[1024]{0:T(1024)S(1)} %add_multiply_fusion, f32[1024]{0:T(1024)S(1)} %broadcast_divide_fusion.1, f32[1024,2048]{1,0:T(8,128)} %copy-done.1, f32[2048]{0:T(1024)S(1)} %broadcast_divide_fusion), kind=kLoop, calls=%fused_computation.85 | loop fusion | flops 8388608 | bytes 12599296 | tf_op jit(solution)/shard_map/sub | solution.py:166
  105.0 6.4 %copy.15 = bf16[2048,1024]{1,0:T(8,128)(2,1)} copy(bf16[2048,1024]{0,1:T(8,128)(2,1)} %fusion.36) | data formatting | bytes 8388608 | tf_op jit(solution)/shard_map/dot_general | solution.py:126
  111.4 0.2 all-to-all-done.1
  111.6 0.2 multiply_convert_fusion
  111.9 3.4 %convolution_convert_fusion.1 = bf16[16,128,256]{2,1,0:T(8,128)(2,1)S(1)} fusion(bf16[16,128,1024]{2,1,0:T(8,128)(2,1)} %bitcast.71, bf16[1024,256,1]{1,0,2:T(8,128)(2,1)S(1)} %bitcast.76), kind=kOutput, calls=%fused_computation.13 | convolution fusion | flops 1074266112 | bytes 5767168 | tf_op jit(solution)/shard_map/dot_general | solution.py:126
  115.4 0.1 pad_maximum_fusion
  115.5 20.8 %all_to_all.51 = bf16[16,134,256]{2,1,0:T(8,128)(2,1)S(1)} all-to-all(bf16[16,134,256]{2,1,0:T(8,128)(2,1)S(1)} %pad_maximum_fusion), channel_id=1, replica_groups=mesh['sample'=8,'landmark'=16] {'landmark'}, dimensions={0} | all-to-all | bytes 2195456 | tf_op jit(solution)/shard_map/all_to_all | solution.py:105
  136.3 0.2 convert_reduce_fusion.1
  136.5 0.1 broadcast_in_dim.78
  136.6 19.1 %all_to_all.52 = bf16[16,128,256]{2,1,0:T(8,128)(2,1)S(1)} all-to-all(bf16[16,128,256]{2,1,0:T(8,128)(2,1)S(1)} %broadcast_in_dim.78), channel_id=1, replica_groups=mesh['sample'=8,'landmark'=16] {'landmark'}, dimensions={0} | all-to-all | bytes 2097152 | tf_op jit(solution)/shard_map/all_to_all | solution.py:110
  155.7 1.2 fusion.23
  156.9 0.3 multiply_reduce_fusion.1
  157.2 0.1 pad_maximum_fusion.1
  157.3 24.7 %all_to_all.53 = f32[8,129,256]{2,1,0:T(8,128)S(1)} all-to-all(f32[8,129,256]{2,1,0:T(8,128)S(1)} %pad_maximum_fusion.1), channel_id=1, replica_groups=mesh['sample'=8,'landmark'=16] {'sample'}, dimensions={0} | all-to-all | bytes 2113536 | tf_op jit(solution)/shard_map/all_to_all | solution.py:105
  182.0 0.1 reduce_sum.130
  182.1 1.1 broadcast_in_dim.80
  183.2 3.6 %all-to-all-start.5 = ((f32[8,128,256]{2,1,0:T(8,128)}), f32[8,128,256]{2,1,0:T(8,128)S(1)}, u32[]{:S(2)}, u32[]{:S(2)}) async-start(f32[8,128,256]{2,1,0:T(8,128)} %broadcast_in_dim.80), calls=%async_computation.5 | async-start | bytes 2097152 | tf_op jit(solution)/shard_map/all_to_all | solution.py:110
  186.7 14.2 %all-to-all-done.5 = f32[8,128,256]{2,1,0:T(8,128)S(1)} async-done(((f32[8,128,256]{2,1,0:T(8,128)}), f32[8,128,256]{2,1,0:T(8,128)S(1)}, u32[]{:S(2)}, u32[]{:S(2)}) %all-to-all-start.5) | async-done | bytes 1048608 | tf_op jit(solution)/shard_map/all_to_all | solution.py:110
  201.0 0.3 multiply_reduce_fusion.3
  201.3 0.1 collective-permute-start.3
  201.3 1.1 collective-permute-done.3
  202.5 1.8 collective-permute-start.4
  204.3 1.8 collective-permute-done.4
  206.1 0.9 collective-permute-start.5
  207.0 2.7 collective-permute-done.5
  209.7 2.3 collective-permute-start.6
  212.0 2.7 collective-permute-done.6
  214.7 1.3 fusion.11
  216.1 1.3 convolution_convert_fusion
  217.4 0.1 pad_maximum_fusion.2
  217.5 21.0 %all_to_all.54 = bf16[16,131,256]{2,1,0:T(8,128)(2,1)S(1)} all-to-all(bf16[16,131,256]{2,1,0:T(8,128)(2,1)S(1)} %pad_maximum_fusion.2), channel_id=1, replica_groups=mesh['sample'=8,'landmark'=16] {'landmark'}, dimensions={0} | all-to-all | bytes 2146304 | tf_op jit(solution)/shard_map/all_to_all | solution.py:105
  238.5 0.2 convert_reduce_fusion
  238.7 0.1 broadcast_in_dim.130
  238.8 19.1 %all_to_all.55 = bf16[16,128,256]{2,1,0:T(8,128)(2,1)S(1)} all-to-all(bf16[16,128,256]{2,1,0:T(8,128)(2,1)S(1)} %broadcast_in_dim.130), channel_id=1, replica_groups=mesh['sample'=8,'landmark'=16] {'landmark'}, dimensions={0} | all-to-all | bytes 2097152 | tf_op jit(solution)/shard_map/all_to_all | solution.py:110
  257.8 1.3 fusion.24
  259.1 0.3 multiply_reduce_fusion
  259.4 0.1 pad_maximum_fusion.3
  259.5 21.9 %all_to_all.56 = f32[8,129,256]{2,1,0:T(8,128)S(1)} all-to-all(f32[8,129,256]{2,1,0:T(8,128)S(1)} %pad_maximum_fusion.3), channel_id=1, replica_groups=mesh['sample'=8,'landmark'=16] {'sample'}, dimensions={0} | all-to-all | bytes 2113536 | tf_op jit(solution)/shard_map/all_to_all | solution.py:105
  281.4 0.1 reduce_sum.136
  281.5 1.1 broadcast_in_dim.132
  282.6 3.6 %all-to-all-start.9 = ((f32[8,128,256]{2,1,0:T(8,128)}), f32[8,128,256]{2,1,0:T(8,128)S(1)}, u32[]{:S(2)}, u32[]{:S(2)}) async-start(f32[8,128,256]{2,1,0:T(8,128)} %broadcast_in_dim.132), calls=%async_computation.9 | async-start | bytes 2097152 | tf_op jit(solution)/shard_map/all_to_all | solution.py:110
  286.2 14.2 %all-to-all-done.9 = f32[8,128,256]{2,1,0:T(8,128)S(1)} async-done(((f32[8,128,256]{2,1,0:T(8,128)}), f32[8,128,256]{2,1,0:T(8,128)S(1)}, u32[]{:S(2)}, u32[]{:S(2)}) %all-to-all-start.9) | async-done | bytes 1048608 | tf_op jit(solution)/shard_map/all_to_all | solution.py:110
  300.4 0.1 broadcast_multiply_fusion
  300.5 3.2 %fusion.5 = (f32[1024,256]{1,0:T(8,128)}, f32[1024,256]{1,0:T(8,128)}) fusion(f32[8,128,256]{2,1,0:T(8,128)S(1)} %broadcast_multiply_fusion, f32[256]{0:T(256)S(1)} %get-tuple-element.2, f32[8,128,256]{2,1,0:T(8,128)S(1)} %all-to-all-done.1, f32[8,128,256]{2,1,0:T(8,128)} %get-tuple-element.10, f32[256]{0:T(256)S(1)} %bitcast.81, f32[256]{0:T(256)S(1)} %div.75, ...), kind=kLoop, calls=%fused_computation.20 | loop fusion | flops 3670016 | bytes 5246976 | tf_op jit(solution)/shard_map/sub | solution.py:146
  (48 shorter events, 0.4 us)
Async XLA Ops:
  7.2 65.4 %copy-start = (bf16[2048,256]{1,0:T(8,128)(2,1)S(1)}, bf16[2048,256]{1,0:T(8,128)(2,1)}, u32[]{:S(2)}) copy-start(bf16[2048,256]{1,0:T(8,128)(2,1)} %param.13) | copy-start | bytes 3145732
  7.2 42.4 %all-gather.2.cloned.1.call-start = ((), (), s32[]{:S(2)}) async-start(), calls=%async_computation.10 | async-start | bytes 4456448 | tf_op jit(solution)/shard_map/all_gather | solution.py:158
  14.3 7.8 %copy-start.6 = (s32[1024]{0:T(1024)S(1)}, s32[1024]{0:T(1024)}, u32[]{:S(2)}) copy-start(s32[1024]{0:T(1024)} %param.11) | copy-start | bytes 12292
  14.4 7.8 %copy-start.8 = (f32[4]{0:T(128)S(1)}, f32[4]{0:T(128)}, u32[]{:S(2)}) copy-start(f32[4]{0:T(128)} %param.12) | copy-start | bytes 52
  14.4 7.9 %copy-start.7 = (s32[2048]{0:T(1024)S(1)}, s32[2048]{0:T(1024)}, u32[]{:S(2)}) copy-start(s32[2048]{0:T(1024)} %param.8) | copy-start | bytes 24580
  56.8 15.8 %copy-start.1 = (f32[1024,2048]{1,0:T(8,128)}, f32[1024,2048]{1,0:T(8,128)S(1)}, u32[]{:S(2)}) copy-start(f32[1024,2048]{1,0:T(8,128)S(1)} %get-tuple-element.22) | copy-start | bytes 25165828
  56.8 3.7 %collective-permute-start = (f32[1024]{0:T(1024)S(1)}, f32[1024]{0:T(1024)S(1)}, u32[]{:S(2)}, u32[]{:S(2)}) collective-permute-start(f32[1024]{0:T(1024)S(1)} %get-tuple-element.21), channel_id=1, source_target_pairs={{0,32},{16,48},{32,0},{48,16},{64,96},{80,112},{96,64},{112,80},{1... | collective-permute-start | bytes 12296 | tf_op jit(solution)/shard_map/ppermute | solution.py:41
  60.5 5.1 %collective-permute-start.1 = (f32[1024]{0:T(1024)S(1)}, f32[1024]{0:T(1024)S(1)}, u32[]{:S(2)}, u32[]{:S(2)}) collective-permute-start(f32[1024]{0:T(1024)S(1)} %add.82), channel_id=1, source_target_pairs={{0,16},{16,0},{32,48},{48,32},{64,80},{80,64},{96,112},{112,96},{1... | collective-permute-start | bytes 12296 | tf_op jit(solution)/shard_map/ppermute | solution.py:41
  65.6 5.1 %collective-permute-start.2 = (f32[1024]{0:T(1024)S(1)}, f32[1024]{0:T(1024)S(1)}, u32[]{:S(2)}, u32[]{:S(2)}) collective-permute-start(f32[1024]{0:T(1024)S(1)} %add.83), channel_id=1, source_target_pairs={{0,64},{16,80},{32,96},{48,112},{64,0},{80,16},{96,32},{112,48},{1... | collective-permute-start | bytes 12296 | tf_op jit(solution)/shard_map/ppermute | solution.py:41
  72.6 2.0 copy-start.2
  95.8 15.8 %all-to-all-start.1 = ((f32[8,128,256]{2,1,0:T(8,128)}), f32[8,128,256]{2,1,0:T(8,128)S(1)}, u32[]{:S(2)}, u32[]{:S(2)}) async-start(f32[8,128,256]{2,1,0:T(8,128)} %broadcast_in_dim.76), calls=%async_computation.1 | async-start | bytes 2097152 | tf_op jit(solution)/shard_map/all_to_all | solution.py:110
  115.4 40.3 %copy-start.3 = (bf16[1024,2048]{1,0:T(8,128)(2,1)S(1)}, bf16[1024,2048]{1,0:T(8,128)(2,1)}, u32[]{:S(2)}) copy-start(bf16[1024,2048]{1,0:T(8,128)(2,1)} %copy-done.2) | copy-start | bytes 12582916
  183.2 17.8 %all-to-all-start.5 = ((f32[8,128,256]{2,1,0:T(8,128)}), f32[8,128,256]{2,1,0:T(8,128)S(1)}, u32[]{:S(2)}, u32[]{:S(2)}) async-start(f32[8,128,256]{2,1,0:T(8,128)} %broadcast_in_dim.80), calls=%async_computation.5 | async-start | bytes 2097152 | tf_op jit(solution)/shard_map/all_to_all | solution.py:110
  201.0 15.1 %copy-start.5 = (bf16[2048,1024]{1,0:T(8,128)(2,1)S(1)}, bf16[2048,1024]{1,0:T(8,128)(2,1)}, u32[]{:S(2)}) copy-start(bf16[2048,1024]{1,0:T(8,128)(2,1)} %copy.15) | copy-start | bytes 12582916
  201.3 1.2 collective-permute-start.3
  202.5 3.6 %collective-permute-start.4 = (f32[256]{0:T(256)S(1)}, f32[256]{0:T(256)S(1)}, u32[]{:S(2)}, u32[]{:S(2)}) collective-permute-start(f32[256]{0:T(256)S(1)} %add.89), channel_id=1, source_target_pairs={{0,2},{1,3},{2,0},{3,1},{4,6},{5,7},{6,4},{7,5},{8,10},{9,11},{10,... | collective-permute-start | bytes 3080 | tf_op jit(solution)/shard_map/ppermute | solution.py:41
  206.1 3.6 %collective-permute-start.5 = (f32[256]{0:T(256)S(1)}, f32[256]{0:T(256)S(1)}, u32[]{:S(2)}, u32[]{:S(2)}) collective-permute-start(f32[256]{0:T(256)S(1)} %add.90), channel_id=1, source_target_pairs={{0,4},{1,5},{2,6},{3,7},{4,0},{5,1},{6,2},{7,3},{8,12},{9,13},{10,... | collective-permute-start | bytes 3080 | tf_op jit(solution)/shard_map/ppermute | solution.py:41
  209.7 5.1 %collective-permute-start.6 = (f32[256]{0:T(256)S(1)}, f32[256]{0:T(256)S(1)}, u32[]{:S(2)}, u32[]{:S(2)}) collective-permute-start(f32[256]{0:T(256)S(1)} %add.91), channel_id=1, source_target_pairs={{0,8},{1,9},{2,10},{3,11},{4,12},{5,13},{6,14},{7,15},{8,0},{9,1},... | collective-permute-start | bytes 3080 | tf_op jit(solution)/shard_map/ppermute | solution.py:41
  217.4 40.4 %copy-start.4 = (bf16[1024,2048]{1,0:T(8,128)(2,1)S(1)}, bf16[1024,2048]{1,0:T(8,128)(2,1)}, u32[]{:S(2)}) copy-start(bf16[1024,2048]{1,0:T(8,128)(2,1)} %copy-done.2) | copy-start | bytes 12582916
  282.6 17.8 %all-to-all-start.9 = ((f32[8,128,256]{2,1,0:T(8,128)}), f32[8,128,256]{2,1,0:T(8,128)S(1)}, u32[]{:S(2)}, u32[]{:S(2)}) async-start(f32[8,128,256]{2,1,0:T(8,128)} %broadcast_in_dim.132), calls=%async_computation.9 | async-start | bytes 2097152 | tf_op jit(solution)/shard_map/all_to_all | solution.py:110
Sparse Core Ops, SparseCore 0:
  9.7 39.8 all-gather.1

commit v3 on v2

--- a/solution.py
+++ b/solution.py
@@ -6,7 +6,7 @@
 from jax.sharding import PartitionSpec as P
 
 ITERS = 2
-GROUPS = 1
+GROUPS = 2
 
 
 def REDUCE(x, extra, axis, bits, gather_dtype, wire_dtype=jnp.bfloat16):

time: 311 us -> 406 us (1.31)
  blocking collectives: 147 us -> 0 us
  waiting for transfers between devices: 71.5 us -> 202 us
  starting transfers between devices: 23.1 us -> 92.7 us
  matrix products: 15.7 us -> 41.1 us
  other arithmetic: 15.1 us -> 21.9 us
  local copies, waits for them, and re-layouts: 24.1 us -> 30.9 us
    all_to_all x7 -> x0, blocking collectives: 147 us -> none  [the longest x5 109 us: exchange_sum(): got = lax.all_to_all(chunks, axis, 0, 0, tiled=False)]
    all_to_all x0 -> x10, waiting for transfers between devices: none -> 82.8 us  [exchange_sum(): got = lax.all_to_all(chunks, axis, 0, 0, tiled=False)]
    all_to_all x3 -> x10, waiting for transfers between devices: 28.6 us -> 80.2 us  [exchange_sum(): lax.all_to_all(jnp.broadcast_to(part[None], (size,) + part.shape), axis,...]
    all_to_all x0 -> x10, starting transfers between devices: none -> 39.3 us  [exchange_sum(): got = lax.all_to_all(chunks, axis, 0, 0, tiled=False)]
    all_to_all x3 -> x10, starting transfers between devices: 10.7 us -> 38.9 us  [exchange_sum(): lax.all_to_all(jnp.broadcast_to(part[None], (size,) + part.shape), axis,...]
    dot_general x2 -> x4, matrix products: 2.5 us -> 13.7 us  [conjugate_gradients(): jnp.dot(kernel.T, row_half, preferred_element_type=jnp.float32)]
    dot_general x2 -> x4, matrix products: 4.72 us -> 13.8 us  [conjugate_gradients(): jnp.dot(kernel, direction_half, preferred_element_type=jnp.float32)]
    concatenate x4 -> x8, other arithmetic: 0.31 us -> 6.77 us  [exchange_sum(): jnp.concatenate([chunks, jnp.broadcast_to(packed[None], (size,) + packed....]
  transfers between devices with their start and end apart: 11 -> 32, of which waited for: 11 -> 27; matrix products, arithmetic and copies ran while one was open for 9% -> 17% of each run, Pallas kernels for 0% -> 0%
where the time goes in v3:
time: 406 us; the launch traced here: 404 us
  waiting for transfers between devices  202 us (50%)
  starting transfers between devices  92.7 us (23%)
  matrix products  41.1 us (10%)
  local copies, waits for them, and re-layouts  30.9 us (8%)
  other arithmetic  21.9 us (5%)
  between operations  14.7 us (4%)
    all_to_all x10, waiting for transfers between devices, exchange_sum(): got = lax.all_to_all(chunks, axis, 0, 0, tiled=False)  82.8 us
    all_to_all x10, waiting for transfers between devices, exchange_sum(): lax.all_to_all(jnp.broadcast_to(part[None], (size,) + part.shape), axis,...  80.2 us
    all_to_all x10, starting transfers between devices, exchange_sum(): got = lax.all_to_all(chunks, axis, 0, 0, tiled=False)  39.3 us
    all_to_all x10, starting transfers between devices, exchange_sum(): lax.all_to_all(jnp.broadcast_to(part[None], (size,) + part.shape), axis,...  38.9 us
    all_gather x1, waiting for transfers between devices, on_device(): gathered = lax.all_gather(summaries, 'landmark', axis=1, tiled=True)  26.9 us
    ppermute x11, starting transfers between devices, butterfly_sum(): x = x + lax.ppermute(x, axis, perm)  14.5 us
    dot_general x4, matrix products, conjugate_gradients(): jnp.dot(kernel, direction_half, preferred_element_type=jnp.float32)  13.8 us
    dot_general x4, matrix products, conjugate_gradients(): jnp.dot(kernel.T, row_half, preferred_element_type=jnp.float32)  13.7 us
  transfers between devices with their start and end apart: 32, of which 27 were waited for; matrix products, arithmetic and copies ran while one was open for 17% of the time, Pallas kernels for 0%

profile of v3, /device:TPU:0, one launch (start us, length us, event | category | flops | bytes accessed | tf_op | source)
XLA Modules:
  0.0 403.7 jit_solution(3475542436662570057)
XLA Ops:
  8.6 6.1 %gather_fusion.1 = s32[1024]{0:T(1024)S(1)} fusion(s32[2048]{0:T(1024)S(1)} %copy-done, s32[1024]{0:T(1024)S(1)} %fusion.23), kind=kCustom, calls=%fused_computation.1 | custom fusion | bytes 12288 | tf_op jit(solution)/shard_map/jit(_take)/gather | solution.py:161
  14.8 7.7 %gather_fusion = bf16[1024,1024]{1,0:T(8,128)(2,1)S(1)} fusion(bf16[2048,1024]{1,0:T(8,128)(2,1)} %param.9, s32[1024]{0:T(1024)S(1)} %fusion.23), kind=kCustom, calls=%fused_computation | custom fusion | bytes 4198400 | tf_op jit(solution)/shard_map/jit(_take)/gather | solution.py:160
  22.8 26.9 %all-gather.2.cloned.1.call-done = bf16[2048,1024]{0,1:T(8,128)(2,1)} async-done(((bf16[2048,64]{0,1:T(8,128)(2,1)}), bf16[2048,1024]{0,1:T(8,128)(2,1)}) %all-gather.2.cloned.1.call-update) | async-done | bytes 4194320 | tf_op jit(solution)/shard_map/all_gather | solution.py:158
  49.7 7.3 %fusion = (f32[1024]{0:T(1024)S(1)}, f32[1024,2048]{1,0:T(8,128)S(1)}) fusion(f32[1024]{0:T(1024)S(1)} %broadcast_divide_fusion.1, f32[2048]{0:T(1024)S(1)} %broadcast_divide_fusion, bf16[2048,1024]{0,1:T(8,128)(2,1)} %all-gather.2.cloned.1.call-done, bf16[1024,1024]{1,0:T(8,128)(2,1)S(1)} %gather_fusion, pred[1024]{0:T(1024)(128)(4,1)S(1)} %get-tuple-element.11), kind=kOutput, calls=%fused_computation.4 | convolution fusion | flops 4302306304 | bytes 14697472 | tf_op jit(solution)/shard_map/dot_general | solution.py:27
  58.4 2.2 collective-permute-done
  60.7 2.5 collective-permute-start.1
  63.2 2.6 collective-permute-done.1
  65.8 2.8 collective-permute-start.2
  68.6 2.3 collective-permute-done.2
  70.9 1.8 subtract_convert_fusion
  72.7 2.0 copy-done.2
  74.7 2.0 fusion.19
  76.7 6.4 %all-to-all-start = ((f32[8,128,128]{2,1,0:T(8,128)}), f32[8,128,128]{2,1,0:T(8,128)S(1)}, u32[]{:S(2)}, u32[]{:S(2)}) async-start(f32[8,128,128]{2,1,0:T(8,128)} %bitcast), calls=%async_computation | async-start | bytes 1048576 | tf_op jit(solution)/shard_map/all_to_all | solution.py:105
  83.1 4.2 %fusion.17 = f32[1024,128]{1,0:T(8,128)} fusion(bf16[1024,2048]{1,0:T(8,128)(2,1)} %copy-done.2, bf16[2048,256]{1,0:T(8,128)(2,1)S(1)} %copy-done.7), kind=kOutput, calls=%fused_computation.60 | convolution fusion | flops 536870912 | bytes 5242880 | tf_op jit(solution)/shard_map/dot_general | solution.py:117
  87.4 5.5 %all-to-all-done = f32[8,128,128]{2,1,0:T(8,128)S(1)} async-done(((f32[8,128,128]{2,1,0:T(8,128)}), f32[8,128,128]{2,1,0:T(8,128)S(1)}, u32[]{:S(2)}, u32[]{:S(2)}) %all-to-all-start) | async-done | bytes 524320 | tf_op jit(solution)/shard_map/all_to_all | solution.py:105
  92.8 3.5 all-to-all-start.9
  96.3 9.6 %all-to-all-done.9 = f32[8,128,128]{2,1,0:T(8,128)S(1)} async-done(((f32[8,128,128]{2,1,0:T(8,128)}), f32[8,128,128]{2,1,0:T(8,128)S(1)}, u32[]{:S(2)}, u32[]{:S(2)}) %all-to-all-start.9) | async-done | bytes 524320 | tf_op jit(solution)/shard_map/all_to_all | solution.py:105
  106.7 3.5 all-to-all-start.1
  110.2 5.6 %fusion.70 = bf16[2048,1024]{0,1:T(8,128)(2,1)} fusion(f32[1024]{0:T(1024)S(1)} %add_multiply_fusion, f32[1024]{0:T(1024)S(1)} %broadcast_divide_fusion.1, f32[1024,2048]{1,0:T(8,128)} %copy-done.3, f32[2048]{0:T(1024)S(1)} %broadcast_divide_fusion), kind=kLoop, calls=%fused_computation.157 | loop fusion | flops 8388608 | bytes 12599296 | tf_op jit(solution)/shard_map/sub | solution.py:166
  115.8 6.4 %copy.21 = bf16[2048,1024]{1,0:T(8,128)(2,1)} copy(bf16[2048,1024]{0,1:T(8,128)(2,1)} %fusion.70) | data formatting | bytes 8388608 | tf_op jit(solution)/shard_map/dot_general | solution.py:126
  123.1 7.1 %all-to-all-start.10 = ((f32[8,128,128]{2,1,0:T(8,128)}), f32[8,128,128]{2,1,0:T(8,128)S(1)}, u32[]{:S(2)}, u32[]{:S(2)}) async-start(f32[8,128,128]{2,1,0:T(8,128)} %broadcast_in_dim.102), calls=%async_computation.10 | async-start | bytes 1048576 | tf_op jit(solution)/shard_map/all_to_all | solution.py:110
  130.4 3.4 convolution_convert_fusion.3
  134.7 5.2 %all-to-all-done.10 = f32[8,128,128]{2,1,0:T(8,128)S(1)} async-done(((f32[8,128,128]{2,1,0:T(8,128)}), f32[8,128,128]{2,1,0:T(8,128)S(1)}, u32[]{:S(2)}, u32[]{:S(2)}) %all-to-all-start.10) | async-done | bytes 524320 | tf_op jit(solution)/shard_map/all_to_all | solution.py:110
  139.9 3.6 all-to-all-start.2
  143.7 3.4 convolution_convert_fusion.1
  148.0 6.7 %all-to-all-done.2 = bf16[16,134,128]{2,1,0:T(8,128)(2,1)S(1)} async-done(((bf16[16,134,128]{2,1,0:T(8,128)(2,1)}), bf16[16,134,128]{2,1,0:T(8,128)(2,1)S(1)}, u32[]{:S(2)}, u32[]{:S(2)}) %all-to-all-start.2) | async-done | bytes 548896 | tf_op jit(solution)/shard_map/all_to_all | solution.py:105
  154.7 3.6 all-to-all-start.11
  158.3 11.0 %all-to-all-done.11 = bf16[16,134,128]{2,1,0:T(8,128)(2,1)S(1)} async-done(((bf16[16,134,128]{2,1,0:T(8,128)(2,1)}), bf16[16,134,128]{2,1,0:T(8,128)(2,1)S(1)}, u32[]{:S(2)}, u32[]{:S(2)}) %all-to-all-start.11) | async-done | bytes 548896 | tf_op jit(solution)/shard_map/all_to_all | solution.py:105
  170.3 3.6 all-to-all-start.3
  174.0 10.7 %all-to-all-done.3 = bf16[16,128,128]{2,1,0:T(8,128)(2,1)S(1)} async-done(((bf16[16,128,128]{2,1,0:T(8,128)(2,1)}), bf16[16,128,128]{2,1,0:T(8,128)(2,1)S(1)}, u32[]{:S(2)}, u32[]{:S(2)}) %all-to-all-start.3) | async-done | bytes 524320 | tf_op jit(solution)/shard_map/all_to_all | solution.py:110
  185.6 3.6 all-to-all-start.12
  189.4 3.4 fusion.47
  193.7 6.2 %all-to-all-done.12 = bf16[16,128,128]{2,1,0:T(8,128)(2,1)S(1)} async-done(((bf16[16,128,128]{2,1,0:T(8,128)(2,1)}), bf16[16,128,128]{2,1,0:T(8,128)(2,1)S(1)}, u32[]{:S(2)}, u32[]{:S(2)}) %all-to-all-start.12) | async-done | bytes 524320 | tf_op jit(solution)/shard_map/all_to_all | solution.py:110
  199.9 3.7 all-to-all-start.4
  204.0 3.4 fusion.49
  208.3 6.0 %all-to-all-done.4 = f32[8,129,128]{2,1,0:T(8,128)S(1)} async-done(((f32[8,129,128]{2,1,0:T(8,128)}), f32[8,129,128]{2,1,0:T(8,128)S(1)}, u32[]{:S(2)}, u32[]{:S(2)}) %all-to-all-start.4) | async-done | bytes 528416 | tf_op jit(solution)/shard_map/all_to_all | solution.py:105
  214.3 3.5 all-to-all-start.13
  217.9 10.6 %all-to-all-done.13 = f32[8,129,128]{2,1,0:T(8,128)S(1)} async-done(((f32[8,129,128]{2,1,0:T(8,128)}), f32[8,129,128]{2,1,0:T(8,128)S(1)}, u32[]{:S(2)}, u32[]{:S(2)}) %all-to-all-start.13) | async-done | bytes 528416 | tf_op jit(solution)/shard_map/all_to_all | solution.py:105
  229.4 3.5 all-to-all-start.5
  232.9 10.4 %all-to-all-done.5 = f32[8,128,128]{2,1,0:T(8,128)S(1)} async-done(((f32[8,128,128]{2,1,0:T(8,128)}), f32[8,128,128]{2,1,0:T(8,128)S(1)}, u32[]{:S(2)}, u32[]{:S(2)}) %all-to-all-start.5) | async-done | bytes 524320 | tf_op jit(solution)/shard_map/all_to_all | solution.py:110
  244.1 3.5 all-to-all-start.14
  247.9 10.1 %all-to-all-done.14 = f32[8,128,128]{2,1,0:T(8,128)S(1)} async-done(((f32[8,128,128]{2,1,0:T(8,128)}), f32[8,128,128]{2,1,0:T(8,128)S(1)}, u32[]{:S(2)}, u32[]{:S(2)}) %all-to-all-start.14) | async-done | bytes 524320 | tf_op jit(solution)/shard_map/all_to_all | solution.py:110
  258.3 1.7 collective-permute-start.4
  267.2 1.9 collective-permute-start.10
  270.8 3.4 convolution_convert_fusion.2
  275.2 3.8 all-to-all-start.6
  280.0 3.4 convolution_convert_fusion
  284.4 5.6 %all-to-all-done.6 = bf16[16,131,128]{2,1,0:T(8,128)(2,1)S(1)} async-done(((bf16[16,131,128]{2,1,0:T(8,128)(2,1)}), bf16[16,131,128]{2,1,0:T(8,128)(2,1)S(1)}, u32[]{:S(2)}, u32[]{:S(2)}) %all-to-all-start.6) | async-done | bytes 536608 | tf_op jit(solution)/shard_map/all_to_all | solution.py:105
  290.0 3.6 all-to-all-start.15
  293.7 11.0 %all-to-all-done.15 = bf16[16,131,128]{2,1,0:T(8,128)(2,1)S(1)} async-done(((bf16[16,131,128]{2,1,0:T(8,128)(2,1)}), bf16[16,131,128]{2,1,0:T(8,128)(2,1)S(1)}, u32[]{:S(2)}, u32[]{:S(2)}) %all-to-all-start.15) | async-done | bytes 536608 | tf_op jit(solution)/shard_map/all_to_all | solution.py:105
  305.6 3.6 all-to-all-start.7
  309.3 10.7 %all-to-all-done.7 = bf16[16,128,128]{2,1,0:T(8,128)(2,1)S(1)} async-done(((bf16[16,128,128]{2,1,0:T(8,128)(2,1)}), bf16[16,128,128]{2,1,0:T(8,128)(2,1)S(1)}, u32[]{:S(2)}, u32[]{:S(2)}) %all-to-all-start.7) | async-done | bytes 524320 | tf_op jit(solution)/shard_map/all_to_all | solution.py:110
  320.9 3.6 all-to-all-start.16
  324.8 3.4 fusion.48
  329.1 6.2 %all-to-all-done.16 = bf16[16,128,128]{2,1,0:T(8,128)(2,1)S(1)} async-done(((bf16[16,128,128]{2,1,0:T(8,128)(2,1)}), bf16[16,128,128]{2,1,0:T(8,128)(2,1)S(1)}, u32[]{:S(2)}, u32[]{:S(2)}) %all-to-all-start.16) | async-done | bytes 524320 | tf_op jit(solution)/shard_map/all_to_all | solution.py:110
  335.3 4.0 %all-to-all-start.8 = ((f32[8,129,128]{2,1,0:T(8,128)}), f32[8,129,128]{2,1,0:T(8,128)S(1)}, u32[]{:S(2)}, u32[]{:S(2)}) async-start(f32[8,129,128]{2,1,0:T(8,128)} %pad_maximum_fusion.5), calls=%async_computation.8 | async-start | bytes 1114112 | tf_op jit(solution)/shard_map/all_to_all | solution.py:105
  339.6 3.4 fusion.50
  343.9 6.0 %all-to-all-done.8 = f32[8,129,128]{2,1,0:T(8,128)S(1)} async-done(((f32[8,129,128]{2,1,0:T(8,128)}), f32[8,129,128]{2,1,0:T(8,128)S(1)}, u32[]{:S(2)}, u32[]{:S(2)}) %all-to-all-start.8) | async-done | bytes 528416 | tf_op jit(solution)/shard_map/all_to_all | solution.py:105
  349.9 3.5 all-to-all-start.17
  353.5 10.6 %all-to-all-done.17 = f32[8,129,128]{2,1,0:T(8,128)S(1)} async-done(((f32[8,129,128]{2,1,0:T(8,128)}), f32[8,129,128]{2,1,0:T(8,128)S(1)}, u32[]{:S(2)}, u32[]{:S(2)}) %all-to-all-start.17) | async-done | bytes 528416 | tf_op jit(solution)/shard_map/all_to_all | solution.py:105
  365.0 3.5 all-to-all-start.18
  368.6 10.4 %all-to-all-done.18 = f32[8,128,128]{2,1,0:T(8,128)S(1)} async-done(((f32[8,128,128]{2,1,0:T(8,128)}), f32[8,128,128]{2,1,0:T(8,128)S(1)}, u32[]{:S(2)}, u32[]{:S(2)}) %all-to-all-start.18) | async-done | bytes 524320 | tf_op jit(solution)/shard_map/all_to_all | solution.py:110
  379.8 3.5 all-to-all-start.19
  383.3 10.3 %all-to-all-done.19 = f32[8,128,128]{2,1,0:T(8,128)S(1)} async-done(((f32[8,128,128]{2,1,0:T(8,128)}), f32[8,128,128]{2,1,0:T(8,128)S(1)}, u32[]{:S(2)}, u32[]{:S(2)}) %all-to-all-start.19) | async-done | bytes 524320 | tf_op jit(solution)/shard_map/all_to_all | solution.py:110
  (123 shorter events, 34.2 us)
Async XLA Ops:
  7.2 1.4 copy-start
  7.2 42.5 %all-gather.2.cloned.1.call-start = ((), (), s32[]{:S(2)}) async-start(), calls=%async_computation.20 | async-start | bytes 4456448 | tf_op jit(solution)/shard_map/all_gather | solution.py:158
  14.8 7.8 %copy-start.4 = (s32[1024]{0:T(1024)S(1)}, s32[1024]{0:T(1024)}, u32[]{:S(2)}) copy-start(s32[1024]{0:T(1024)} %param.11) | copy-start | bytes 12292
  14.8 7.8 %copy-start.6 = (f32[4]{0:T(128)S(1)}, f32[4]{0:T(128)}, u32[]{:S(2)}) copy-start(f32[4]{0:T(128)} %param.12) | copy-start | bytes 52
  14.8 7.9 %copy-start.5 = (s32[2048]{0:T(1024)S(1)}, s32[2048]{0:T(1024)}, u32[]{:S(2)}) copy-start(s32[2048]{0:T(1024)} %param.8) | copy-start | bytes 24580
  57.0 15.7 %copy-start.3 = (f32[1024,2048]{1,0:T(8,128)}, f32[1024,2048]{1,0:T(8,128)S(1)}, u32[]{:S(2)}) copy-start(f32[1024,2048]{1,0:T(8,128)S(1)} %get-tuple-element.39) | copy-start | bytes 25165828
  57.0 3.7 collective-permute-start
  60.7 5.1 %collective-permute-start.1 = (f32[1024]{0:T(1024)S(1)}, f32[1024]{0:T(1024)S(1)}, u32[]{:S(2)}, u32[]{:S(2)}) collective-permute-start(f32[1024]{0:T(1024)S(1)} %add.141), channel_id=1, source_target_pairs={{0,16},{16,0},{32,48},{48,32},{64,80},{80,64},{96,112},{112,96},{1... | collective-permute-start | bytes 12296 | tf_op jit(solution)/shard_map/ppermute | solution.py:41
  65.8 5.1 %collective-permute-start.2 = (f32[1024]{0:T(1024)S(1)}, f32[1024]{0:T(1024)S(1)}, u32[]{:S(2)}, u32[]{:S(2)}) collective-permute-start(f32[1024]{0:T(1024)S(1)} %add.142), channel_id=1, source_target_pairs={{0,64},{16,80},{32,96},{48,112},{64,0},{80,16},{96,32},{112,48},{1... | collective-permute-start | bytes 12296 | tf_op jit(solution)/shard_map/ppermute | solution.py:41
  70.9 3.8 copy-start.7
  72.7 2.0 copy-start.2
  76.7 16.1 %all-to-all-start = ((f32[8,128,128]{2,1,0:T(8,128)}), f32[8,128,128]{2,1,0:T(8,128)S(1)}, u32[]{:S(2)}, u32[]{:S(2)}) async-start(f32[8,128,128]{2,1,0:T(8,128)} %bitcast), calls=%async_computation | async-start | bytes 1048576 | tf_op jit(solution)/shard_map/all_to_all | solution.py:105
  92.8 13.1 %all-to-all-start.9 = ((f32[8,128,128]{2,1,0:T(8,128)}), f32[8,128,128]{2,1,0:T(8,128)S(1)}, u32[]{:S(2)}, u32[]{:S(2)}) async-start(f32[8,128,128]{2,1,0:T(8,128)} %bitcast.18), calls=%async_computation.9 | async-start | bytes 1048576 | tf_op jit(solution)/shard_map/all_to_all | solution.py:105
  106.7 15.5 %all-to-all-start.1 = ((f32[8,128,128]{2,1,0:T(8,128)}), f32[8,128,128]{2,1,0:T(8,128)S(1)}, u32[]{:S(2)}, u32[]{:S(2)}) async-start(f32[8,128,128]{2,1,0:T(8,128)} %broadcast_in_dim.94), calls=%async_computation.1 | async-start | bytes 1048576 | tf_op jit(solution)/shard_map/all_to_all | solution.py:110
  123.1 16.8 %all-to-all-start.10 = ((f32[8,128,128]{2,1,0:T(8,128)}), f32[8,128,128]{2,1,0:T(8,128)S(1)}, u32[]{:S(2)}, u32[]{:S(2)}) async-start(f32[8,128,128]{2,1,0:T(8,128)} %broadcast_in_dim.102), calls=%async_computation.10 | async-start | bytes 1048576 | tf_op jit(solution)/shard_map/all_to_all | solution.py:110
  139.9 14.7 %all-to-all-start.2 = ((bf16[16,134,128]{2,1,0:T(8,128)(2,1)}), bf16[16,134,128]{2,1,0:T(8,128)(2,1)S(1)}, u32[]{:S(2)}, u32[]{:S(2)}) async-start(bf16[16,134,128]{2,1,0:T(8,128)(2,1)} %pad_maximum_fusion.2), calls=%async_computation.2 | async-start | bytes 1114112 | tf_op jit(solution)/shard_map/all_to_all | solution.py:105
  154.7 14.7 %all-to-all-start.11 = ((bf16[16,134,128]{2,1,0:T(8,128)(2,1)}), bf16[16,134,128]{2,1,0:T(8,128)(2,1)S(1)}, u32[]{:S(2)}, u32[]{:S(2)}) async-start(bf16[16,134,128]{2,1,0:T(8,128)(2,1)} %pad_maximum_fusion.6), calls=%async_computation.11 | async-start | bytes 1114112 | tf_op jit(solution)/shard_map/all_to_all | solution.py:105
  170.3 14.4 %all-to-all-start.3 = ((bf16[16,128,128]{2,1,0:T(8,128)(2,1)}), bf16[16,128,128]{2,1,0:T(8,128)(2,1)S(1)}, u32[]{:S(2)}, u32[]{:S(2)}) async-start(bf16[16,128,128]{2,1,0:T(8,128)(2,1)} %broadcast_in_dim.96), calls=%async_computation.3 | async-start | bytes 1048576 | tf_op jit(solution)/shard_map/all_to_all | solution.py:110
  185.6 14.4 %all-to-all-start.12 = ((bf16[16,128,128]{2,1,0:T(8,128)(2,1)}), bf16[16,128,128]{2,1,0:T(8,128)(2,1)S(1)}, u32[]{:S(2)}, u32[]{:S(2)}) async-start(bf16[16,128,128]{2,1,0:T(8,128)(2,1)} %broadcast_in_dim.104), calls=%async_computation.12 | async-start | bytes 1048576 | tf_op jit(solution)/shard_map/all_to_all | solution.py:110
  199.9 14.4 %all-to-all-start.4 = ((f32[8,129,128]{2,1,0:T(8,128)}), f32[8,129,128]{2,1,0:T(8,128)S(1)}, u32[]{:S(2)}, u32[]{:S(2)}) async-start(f32[8,129,128]{2,1,0:T(8,128)} %pad_maximum_fusion.3), calls=%async_computation.4 | async-start | bytes 1114112 | tf_op jit(solution)/shard_map/all_to_all | solution.py:105
  214.3 14.2 %all-to-all-start.13 = ((f32[8,129,128]{2,1,0:T(8,128)}), f32[8,129,128]{2,1,0:T(8,128)S(1)}, u32[]{:S(2)}, u32[]{:S(2)}) async-start(f32[8,129,128]{2,1,0:T(8,128)} %pad_maximum_fusion.7), calls=%async_computation.13 | async-start | bytes 1114112 | tf_op jit(solution)/shard_map/all_to_all | solution.py:105
  229.4 13.9 %all-to-all-start.5 = ((f32[8,128,128]{2,1,0:T(8,128)}), f32[8,128,128]{2,1,0:T(8,128)S(1)}, u32[]{:S(2)}, u32[]{:S(2)}) async-start(f32[8,128,128]{2,1,0:T(8,128)} %broadcast_in_dim.98), calls=%async_computation.5 | async-start | bytes 1048576 | tf_op jit(solution)/shard_map/all_to_all | solution.py:110
  244.1 13.9 %all-to-all-start.14 = ((f32[8,128,128]{2,1,0:T(8,128)}), f32[8,128,128]{2,1,0:T(8,128)S(1)}, u32[]{:S(2)}, u32[]{:S(2)}) async-start(f32[8,128,128]{2,1,0:T(8,128)} %broadcast_in_dim.106), calls=%async_computation.14 | async-start | bytes 1048576 | tf_op jit(solution)/shard_map/all_to_all | solution.py:110
  247.8 10.5 %collective-permute-start.3 = (f32[128]{0:T(128)S(1)}, f32[128]{0:T(128)S(1)}, u32[]{:S(2)}, u32[]{:S(2)}) collective-permute-start(f32[128]{0:T(128)S(1)} %multiply_reduce_fusion.8), channel_id=1, source_target_pairs={{0,1},{1,0},{2,3},{3,2},{4,5},{5,4},{6,7},{7,6},{8,9},{9,8},{10,11... | collective-permute-start | bytes 1544 | tf_op jit(solution)/shard_map/ppermute | solution.py:41
  258.2 1.9 collective-permute-start.7
  258.3 3.6 collective-permute-start.4
  260.1 3.6 collective-permute-start.8
  262.0 3.6 collective-permute-start.5
  263.6 3.6 collective-permute-start.9
  265.5 5.1 %collective-permute-start.6 = (f32[128]{0:T(128)S(1)}, f32[128]{0:T(128)S(1)}, u32[]{:S(2)}, u32[]{:S(2)}) collective-permute-start(f32[128]{0:T(128)S(1)} %add.150), channel_id=1, source_target_pairs={{0,8},{1,9},{2,10},{3,11},{4,12},{5,13},{6,14},{7,15},{8,0},{9,1},... | collective-permute-start | bytes 1544 | tf_op jit(solution)/shard_map/ppermute | solution.py:41
  267.2 11.8 %collective-permute-start.10 = (f32[128]{0:T(128)S(1)}, f32[128]{0:T(128)S(1)}, u32[]{:S(2)}, u32[]{:S(2)}) collective-permute-start(f32[128]{0:T(128)S(1)} %add.166), channel_id=1, source_target_pairs={{0,8},{1,9},{2,10},{3,11},{4,12},{5,13},{6,14},{7,15},{8,0},{9,1},... | collective-permute-start | bytes 1544 | tf_op jit(solution)/shard_map/ppermute | solution.py:41
  275.2 14.8 %all-to-all-start.6 = ((bf16[16,131,128]{2,1,0:T(8,128)(2,1)}), bf16[16,131,128]{2,1,0:T(8,128)(2,1)S(1)}, u32[]{:S(2)}, u32[]{:S(2)}) async-start(bf16[16,131,128]{2,1,0:T(8,128)(2,1)} %pad_maximum_fusion.4), calls=%async_computation.6 | async-start | bytes 1114112 | tf_op jit(solution)/shard_map/all_to_all | solution.py:105
  290.0 14.7 %all-to-all-start.15 = ((bf16[16,131,128]{2,1,0:T(8,128)(2,1)}), bf16[16,131,128]{2,1,0:T(8,128)(2,1)S(1)}, u32[]{:S(2)}, u32[]{:S(2)}) async-start(bf16[16,131,128]{2,1,0:T(8,128)(2,1)} %pad_maximum_fusion.8), calls=%async_computation.15 | async-start | bytes 1114112 | tf_op jit(solution)/shard_map/all_to_all | solution.py:105
  305.6 14.4 %all-to-all-start.7 = ((bf16[16,128,128]{2,1,0:T(8,128)(2,1)}), bf16[16,128,128]{2,1,0:T(8,128)(2,1)S(1)}, u32[]{:S(2)}, u32[]{:S(2)}) async-start(bf16[16,128,128]{2,1,0:T(8,128)(2,1)} %broadcast_in_dim.100), calls=%async_computation.7 | async-start | bytes 1048576 | tf_op jit(solution)/shard_map/all_to_all | solution.py:110
  320.9 14.4 %all-to-all-start.16 = ((bf16[16,128,128]{2,1,0:T(8,128)(2,1)}), bf16[16,128,128]{2,1,0:T(8,128)(2,1)S(1)}, u32[]{:S(2)}, u32[]{:S(2)}) async-start(bf16[16,128,128]{2,1,0:T(8,128)(2,1)} %broadcast_in_dim.108), calls=%async_computation.16 | async-start | bytes 1048576 | tf_op jit(solution)/shard_map/all_to_all | solution.py:110
  335.3 14.7 %all-to-all-start.8 = ((f32[8,129,128]{2,1,0:T(8,128)}), f32[8,129,128]{2,1,0:T(8,128)S(1)}, u32[]{:S(2)}, u32[]{:S(2)}) async-start(f32[8,129,128]{2,1,0:T(8,128)} %pad_maximum_fusion.5), calls=%async_computation.8 | async-start | bytes 1114112 | tf_op jit(solution)/shard_map/all_to_all | solution.py:105
  349.9 14.2 %all-to-all-start.17 = ((f32[8,129,128]{2,1,0:T(8,128)}), f32[8,129,128]{2,1,0:T(8,128)S(1)}, u32[]{:S(2)}, u32[]{:S(2)}) async-start(f32[8,129,128]{2,1,0:T(8,128)} %pad_maximum_fusion.9), calls=%async_computation.17 | async-start | bytes 1114112 | tf_op jit(solution)/shard_map/all_to_all | solution.py:105
  365.0 13.9 %all-to-all-start.18 = ((f32[8,128,128]{2,1,0:T(8,128)}), f32[8,128,128]{2,1,0:T(8,128)S(1)}, u32[]{:S(2)}, u32[]{:S(2)}) async-start(f32[8,128,128]{2,1,0:T(8,128)} %broadcast_in_dim.110), calls=%async_computation.18 | async-start | bytes 1048576 | tf_op jit(solution)/shard_map/all_to_all | solution.py:110
  379.8 13.9 %all-to-all-start.19 = ((f32[8,128,128]{2,1,0:T(8,128)}), f32[8,128,128]{2,1,0:T(8,128)S(1)}, u32[]{:S(2)}, u32[]{:S(2)}) async-start(f32[8,128,128]{2,1,0:T(8,128)} %broadcast_in_dim.111), calls=%async_computation.19 | async-start | bytes 1048576 | tf_op jit(solution)/shard_map/all_to_all | solution.py:110
  393.7 3.1 copy-start.1
Sparse Core Ops, SparseCore 0:
  9.7 39.9 all-gather.1

commit v4 on v2

--- a/solution.py
+++ b/solution.py
@@ -93,7 +93,7 @@
     return x, extra
 
 
-def exchange_sum(x, extra, axis, gather_dtype, wire_dtype=jnp.bfloat16):
+def exchange_scatter(x, extra, axis, wire_dtype):
     size = lax.axis_size(axis)
     rows, columns = x.shape
     chunks = x.reshape(size, rows // size, columns).astype(wire_dtype)
@@ -104,49 +104,66 @@
         )
     got = lax.all_to_all(chunks, axis, 0, 0, tiled=False)
     total = jnp.sum(got.astype(jnp.float32), axis=0)
-    part = total[: rows // size].astype(gather_dtype)
+    part = total[: rows // size]
     if extra is not None:
         extra = unpack_rows(total[rows // size:], extra.shape[0] // columns, wire_dtype)
+    return part, extra
+
+
+def exchange_gather(part, axis):
+    size = lax.axis_size(axis)
     whole = lax.all_to_all(
         jnp.broadcast_to(part[None], (size,) + part.shape), axis, 0, 0, tiled=False
     )
-    return whole.reshape(rows, columns), extra
+    return whole.reshape((size * part.shape[0],) + part.shape[1:])
+
+
+def exchange_sum(x, extra, axis, gather_dtype, wire_dtype=jnp.bfloat16):
+    part, extra = exchange_scatter(x, extra, axis, wire_dtype)
+    return exchange_gather(part.astype(gather_dtype), axis), extra
 
 
 def conjugate_gradients(kernel, targets, n_rows, sample_bits, landmark_bits):
     rhs_part = jnp.dot(kernel.T, targets, preferred_element_type=jnp.float32)
-    rhs_total, _ = REDUCE(rhs_part, None, "sample", sample_bits, jnp.float32, jnp.float32)
+    rhs_total, _ = exchange_sum(rhs_part, None, "sample", jnp.float32, jnp.float32)
     rhs = rhs_total / math.sqrt(n_rows)
+    column_count = rhs.shape[1]
     weights = jnp.zeros_like(rhs)
     residual = rhs
     direction = rhs
-    norm_now = None
     for iteration in range(ITERS):
-        direction_half = direction.astype(jnp.bfloat16)
-        row_part = jnp.dot(kernel, direction_half, preferred_element_type=jnp.float32)
-        sums = [jnp.sum(direction * direction, axis=0)]
-        if norm_now is None:
-            sums.append(jnp.sum(residual * residual, axis=0))
-        row_half, landmark_sums = REDUCE(
-            row_part, jnp.concatenate(sums), "landmark", landmark_bits, jnp.bfloat16
-        )
-        column_count = direction.shape[1]
-        direction_square = landmark_sums[:column_count]
-        if norm_now is None:
+        if iteration == 0:
+            row_part = jnp.dot(kernel, direction.astype(jnp.bfloat16), preferred_element_type=jnp.float32)
+            sums = jnp.concatenate(
+                [jnp.sum(direction * direction, axis=0), jnp.sum(residual * residual, axis=0)]
+            )
+            row_chunk, landmark_sums = exchange_scatter(row_part, sums, "landmark", jnp.bfloat16)
+            direction_square = landmark_sums[:column_count]
             norm_now = landmark_sums[column_count:]
+        else:
+            row_part = jnp.dot(kernel, residual.astype(jnp.bfloat16), preferred_element_type=jnp.float32)
+            sums = jnp.concatenate(
+                [jnp.sum(residual * residual, axis=0), jnp.sum(residual * direction, axis=0)]
+            )
+            residual_chunk, landmark_sums = exchange_scatter(row_part, sums, "landmark", jnp.bfloat16)
+            norm_next = landmark_sums[:column_count]
+            cross = landmark_sums[column_count:]
+            beta = norm_next / norm_now
+            row_chunk = residual_chunk + beta * row_chunk
+            direction = residual + beta * direction
+            direction_square = norm_next + 2.0 * beta * cross + beta * beta * direction_square
+            norm_now = norm_next
+        row_half = exchange_gather(row_chunk.astype(jnp.bfloat16), "landmark")
         row_square = jnp.sum(jnp.square(row_half.astype(jnp.float32)), axis=0)
         column_part = jnp.dot(kernel.T, row_half, preferred_element_type=jnp.float32)
-        column_total, row_square_total = REDUCE(
-            column_part, row_square, "sample", sample_bits, jnp.float32, jnp.float32
+        column_total, row_square_total = exchange_sum(
+            column_part, row_square, "sample", jnp.float32, jnp.float32
         )
         image = column_total / n_rows + ridge * direction
         curvature = row_square_total / n_rows + ridge * direction_square
         step_size = norm_now / curvature
         weights = weights + step_size * direction
         residual = residual - step_size * image
-        norm_next = butterfly_sum(jnp.sum(residual * residual, axis=0), "landmark", landmark_bits)
-        direction = residual + norm_next / norm_now * direction
-        norm_now = norm_next
     return weights, residual
 
 

time: 311 us -> 300 us (0.965)
  waiting for transfers between devices: 71.5 us -> 62 us
  starting transfers between devices: 23.1 us -> 18.1 us
    ppermute x7 -> x3, waiting for transfers between devices: 15 us -> 6.55 us  [butterfly_sum(): x = x + lax.ppermute(x, axis, perm)]
    ppermute x7 -> x3, starting transfers between devices: 12.4 us -> 7.36 us  [butterfly_sum(): x = x + lax.ppermute(x, axis, perm)]
  transfers between devices with their start and end apart: 11 -> 7, of which waited for: 11 -> 7; matrix products, arithmetic and copies ran while one was open for 9% -> 9% of each run, Pallas kernels for 0% -> 0%
where the time goes in v4:
time: 300 us; the launch traced here: 299 us
  blocking collectives  146 us (49%)
  waiting for transfers between devices  62 us (21%)
  local copies, waits for them, and re-layouts  25.1 us (8%)
  matrix products  18.5 us (6%)
  starting transfers between devices  18.1 us (6%)
  other arithmetic  14.8 us (5%)
  between operations  14.4 us (5%)
    all_to_all x5, blocking collectives, exchange_scatter(): got = lax.all_to_all(chunks, axis, 0, 0, tiled=False)  108 us
    all_to_all x2, blocking collectives, exchange_gather(): lax.all_to_all(jnp.broadcast_to(part[None], (size,) + part.shape), axis,...  38.1 us
    all_to_all x3, waiting for transfers between devices, exchange_gather(): lax.all_to_all(jnp.broadcast_to(part[None], (size,) + part.shape), axis,...  28.6 us
    all_gather x1, waiting for transfers between devices, on_device(): gathered = lax.all_gather(summaries, 'landmark', axis=1, tiled=True)  26.2 us
    all_to_all x3, starting transfers between devices, exchange_gather(): lax.all_to_all(jnp.broadcast_to(part[None], (size,) + part.shape), axis,...  10.7 us
    gather x1, local copies, waits for them, and re-layouts, on_device(): anchors = jnp.take(pool, landmark_index, axis=0)  8.79 us
    dot_general x1, matrix products, raw_block(): jnp.dot(summary_rows, anchors.T, preferred_element_type=jnp.float32)  7.88 us
    ppermute x3, starting transfers between devices, butterfly_sum(): x = x + lax.ppermute(x, axis, perm)  7.36 us
  transfers between devices with their start and end apart: 7, of which 7 were waited for; matrix products, arithmetic and copies ran while one was open for 9% of the time, Pallas kernels for 0%

profile of v4, /device:TPU:0, one launch (start us, length us, event | category | flops | bytes accessed | tf_op | source)
XLA Modules:
  0.0 299.4 jit_solution(426647577573389490)
XLA Ops:
  7.2 0.0 copy-start
  7.2 0.0 all-gather.2.cloned.1.call-start
  7.2 0.7 all-gather.2.cloned.1.call-update
  7.9 0.7 fusion.12
  8.6 5.7 %gather_fusion.1 = s32[1024]{0:T(1024)S(1)} fusion(s32[2048]{0:T(1024)} %param.10, s32[1024]{0:T(1024)S(1)} %fusion.12), kind=kCustom, calls=%fused_computation.1 | custom fusion | bytes 12288 | tf_op jit(solution)/shard_map/jit(_take)/gather | solution.py:178
  14.3 0.0 copy-start.5
  14.4 0.0 copy-start.7
  14.4 0.0 copy-start.6
  14.4 8.8 %gather_fusion = bf16[1024,1024]{1,0:T(8,128)(2,1)} fusion(bf16[2048,1024]{1,0:T(8,128)(2,1)} %param.9, s32[1024]{0:T(1024)S(1)} %fusion.12), kind=kCustom, calls=%fused_computation | custom fusion | bytes 4198400 | tf_op jit(solution)/shard_map/jit(_take)/gather | solution.py:177
  23.2 0.0 copy-done.5
  23.2 0.0 copy-done.7
  23.2 0.1 select_reduce_fusion.1
  23.3 0.1 select_reduce_fusion
  23.4 26.2 %all-gather.2.cloned.1.call-done = bf16[2048,1024]{0,1:T(8,128)(2,1)} async-done(((bf16[2048,64]{0,1:T(8,128)(2,1)}), bf16[2048,1024]{0,1:T(8,128)(2,1)}) %all-gather.2.cloned.1.call-update) | async-done | bytes 4194320 | tf_op jit(solution)/shard_map/all_gather | solution.py:175
  49.6 7.9 %fusion = (f32[1024]{0:T(1024)S(1)}, f32[1024,2048]{1,0:T(8,128)S(1)}) fusion(f32[1024]{0:T(1024)S(1)} %broadcast_divide_fusion.1, f32[2048]{0:T(1024)S(1)} %broadcast_divide_fusion, bf16[2048,1024]{0,1:T(8,128)(2,1)} %all-gather.2.cloned.1.call-done, bf16[1024,1024]{1,0:T(8,128)(2,1)} %gather_fusion, pred[1024]{0:T(1024)(128)(4,1)S(1)} %get-tuple-element.5), kind=kOutput, calls=%fused_computation.4 | convolution fusion | flops 4302306304 | bytes 14697472 | tf_op jit(solution)/shard_map/dot_general | solution.py:27
  57.5 0.0 copy-start.1
  57.5 1.6 collective-permute-start
  59.1 2.1 collective-permute-done
  61.2 2.8 collective-permute-start.1
  64.0 2.3 collective-permute-done.1
  66.3 3.0 collective-permute-start.2
  69.3 2.1 collective-permute-done.2
  71.4 1.8 subtract_convert_fusion
  73.3 1.3 fusion.25
  74.5 0.7 copy-done.2
  75.2 20.1 %all_to_all.50 = f32[8,128,256]{2,1,0:T(8,128)S(1)} all-to-all(f32[8,128,256]{2,1,0:T(8,128)S(1)} %bitcast.74), channel_id=1, replica_groups=mesh['sample'=8,'landmark'=16] {'sample'}, dimensions={0} | all-to-all | bytes 2097152 | tf_op jit(solution)/shard_map/all_to_all | solution.py:105
  95.3 0.1 reduce_sum.124
  95.4 1.1 broadcast_in_dim.76
  96.4 3.6 %all-to-all-start.1 = ((f32[8,128,256]{2,1,0:T(8,128)}), f32[8,128,256]{2,1,0:T(8,128)S(1)}, u32[]{:S(2)}, u32[]{:S(2)}) async-start(f32[8,128,256]{2,1,0:T(8,128)} %broadcast_in_dim.76), calls=%async_computation.1 | async-start | bytes 2097152 | tf_op jit(solution)/shard_map/all_to_all | solution.py:115
  100.0 5.6 %fusion.39 = bf16[2048,1024]{0,1:T(8,128)(2,1)} fusion(f32[1024]{0:T(1024)S(1)} %add_multiply_fusion, f32[1024]{0:T(1024)S(1)} %broadcast_divide_fusion.1, f32[1024,2048]{1,0:T(8,128)} %copy-done.1, f32[2048]{0:T(1024)S(1)} %broadcast_divide_fusion), kind=kLoop, calls=%fused_computation.89 | loop fusion | flops 8388608 | bytes 12599296 | tf_op jit(solution)/shard_map/sub | solution.py:183
  105.6 6.4 %copy.15 = bf16[2048,1024]{1,0:T(8,128)(2,1)} copy(bf16[2048,1024]{0,1:T(8,128)(2,1)} %fusion.39) | data formatting | bytes 8388608 | tf_op jit(solution)/shard_map/dot_general | solution.py:136
  112.0 0.2 all-to-all-done.1
  112.2 0.2 multiply_convert_fusion
  112.5 3.4 %convolution_convert_fusion.1 = bf16[16,128,256]{2,1,0:T(8,128)(2,1)S(1)} fusion(bf16[16,128,1024]{2,1,0:T(8,128)(2,1)} %bitcast.70, bf16[1024,256,1]{1,0,2:T(8,128)(2,1)S(1)} %bitcast.75), kind=kOutput, calls=%fused_computation.13 | convolution fusion | flops 1074266112 | bytes 5767168 | tf_op jit(solution)/shard_map/dot_general | solution.py:136
  116.0 0.1 pad_maximum_fusion
  116.1 20.7 %all_to_all.51 = bf16[16,134,256]{2,1,0:T(8,128)(2,1)S(1)} all-to-all(bf16[16,134,256]{2,1,0:T(8,128)(2,1)S(1)} %pad_maximum_fusion), channel_id=1, replica_groups=mesh['sample'=8,'landmark'=16] {'landmark'}, dimensions={0} | all-to-all | bytes 2195456 | tf_op jit(solution)/shard_map/all_to_all | solution.py:105
  136.8 0.2 convert_reduce_fusion.1
  136.9 0.1 broadcast_in_dim.78
  137.0 19.1 %all_to_all.52 = bf16[16,128,256]{2,1,0:T(8,128)(2,1)S(1)} all-to-all(bf16[16,128,256]{2,1,0:T(8,128)(2,1)S(1)} %broadcast_in_dim.78), channel_id=1, replica_groups=mesh['sample'=8,'landmark'=16] {'landmark'}, dimensions={0} | all-to-all | bytes 2097152 | tf_op jit(solution)/shard_map/all_to_all | solution.py:115
  156.1 1.2 fusion.26
  157.4 0.3 multiply_reduce_fusion.1
  157.7 0.1 pad_maximum_fusion.1
  157.8 24.7 %all_to_all.53 = f32[8,129,256]{2,1,0:T(8,128)S(1)} all-to-all(f32[8,129,256]{2,1,0:T(8,128)S(1)} %pad_maximum_fusion.1), channel_id=1, replica_groups=mesh['sample'=8,'landmark'=16] {'sample'}, dimensions={0} | all-to-all | bytes 2113536 | tf_op jit(solution)/shard_map/all_to_all | solution.py:105
  182.4 0.1 reduce_sum.128
  182.5 1.1 broadcast_in_dim.80
  183.6 3.6 %all-to-all-start.5 = ((f32[8,128,256]{2,1,0:T(8,128)}), f32[8,128,256]{2,1,0:T(8,128)S(1)}, u32[]{:S(2)}, u32[]{:S(2)}) async-start(f32[8,128,256]{2,1,0:T(8,128)} %broadcast_in_dim.80), calls=%async_computation.5 | async-start | bytes 2097152 | tf_op jit(solution)/shard_map/all_to_all | solution.py:115
  187.2 14.2 %all-to-all-done.5 = f32[8,128,256]{2,1,0:T(8,128)S(1)} async-done(((f32[8,128,256]{2,1,0:T(8,128)}), f32[8,128,256]{2,1,0:T(8,128)S(1)}, u32[]{:S(2)}, u32[]{:S(2)}) %all-to-all-start.5) | async-done | bytes 1048608 | tf_op jit(solution)/shard_map/all_to_all | solution.py:115
  201.4 1.3 multiply_reduce_fusion.3
  202.7 3.4 %convolution_convert_fusion = bf16[16,128,256]{2,1,0:T(8,128)(2,1)S(1)} fusion(bf16[16,128,1024]{2,1,0:T(8,128)(2,1)} %bitcast.71, bf16[1024,256,1]{1,0,2:T(8,128)(2,1)S(1)} %bitcast.76), kind=kOutput, calls=%fused_computation.12 | convolution fusion | flops 1074266112 | bytes 5767168 | tf_op jit(solution)/shard_map/dot_general | solution.py:144
  206.3 0.1 pad_maximum_fusion.2
  206.3 21.0 %all_to_all.54 = bf16[16,134,256]{2,1,0:T(8,128)(2,1)S(1)} all-to-all(bf16[16,134,256]{2,1,0:T(8,128)(2,1)S(1)} %pad_maximum_fusion.2), channel_id=1, replica_groups=mesh['sample'=8,'landmark'=16] {'landmark'}, dimensions={0} | all-to-all | bytes 2195456 | tf_op jit(solution)/shard_map/all_to_all | solution.py:105
  227.3 0.2 convert_reduce_fusion
  227.5 0.1 broadcast_in_dim.82
  227.6 19.1 %all_to_all.55 = bf16[16,128,256]{2,1,0:T(8,128)(2,1)S(1)} all-to-all(bf16[16,128,256]{2,1,0:T(8,128)(2,1)S(1)} %broadcast_in_dim.82), channel_id=1, replica_groups=mesh['sample'=8,'landmark'=16] {'landmark'}, dimensions={0} | all-to-all | bytes 2097152 | tf_op jit(solution)/shard_map/all_to_all | solution.py:115
  246.7 1.3 fusion.27
  248.0 0.3 multiply_reduce_fusion
  248.3 0.1 pad_maximum_fusion.3
  248.4 21.9 %all_to_all.56 = f32[8,129,256]{2,1,0:T(8,128)S(1)} all-to-all(f32[8,129,256]{2,1,0:T(8,128)S(1)} %pad_maximum_fusion.3), channel_id=1, replica_groups=mesh['sample'=8,'landmark'=16] {'sample'}, dimensions={0} | all-to-all | bytes 2113536 | tf_op jit(solution)/shard_map/all_to_all | solution.py:105
  270.3 0.1 reduce_sum.133
  270.4 1.1 broadcast_in_dim.133
  271.4 3.6 %all-to-all-start.9 = ((f32[8,128,256]{2,1,0:T(8,128)}), f32[8,128,256]{2,1,0:T(8,128)S(1)}, u32[]{:S(2)}, u32[]{:S(2)}) async-start(f32[8,128,256]{2,1,0:T(8,128)} %broadcast_in_dim.133), calls=%async_computation.9 | async-start | bytes 2097152 | tf_op jit(solution)/shard_map/all_to_all | solution.py:115
  275.1 14.2 %all-to-all-done.9 = f32[8,128,256]{2,1,0:T(8,128)S(1)} async-done(((f32[8,128,256]{2,1,0:T(8,128)}), f32[8,128,256]{2,1,0:T(8,128)S(1)}, u32[]{:S(2)}, u32[]{:S(2)}) %all-to-all-start.9) | async-done | bytes 1048608 | tf_op jit(solution)/shard_map/all_to_all | solution.py:115
  289.3 0.1 broadcast_multiply_fusion
  289.3 3.2 %fusion.5 = (f32[1024,256]{1,0:T(8,128)}, f32[1024,256]{1,0:T(8,128)}) fusion(f32[8,128,256]{2,1,0:T(8,128)S(1)} %broadcast_multiply_fusion, f32[256]{0:T(256)S(1)} %broadcast_multiply_fusion.2, f32[8,128,256]{2,1,0:T(8,128)S(1)} %all-to-all-done.1, f32[8,128,256]{2,1,0:T(8,128)} %get-tuple-element.9, f32[256]{0:T(256)S(1)} %bitcast.81, f32[256]{0:T(256)S(1)} %bitcast.82, ...), kind=kLoop, calls=%fused_computation.20 | loop fusion | flops 3670016 | bytes 5246976 | tf_op jit(solution)/shard_map/sub | solution.py:166
  (37 shorter events, 0.3 us)
Async XLA Ops:
  7.2 66.1 %copy-start = (bf16[2048,256]{1,0:T(8,128)(2,1)S(1)}, bf16[2048,256]{1,0:T(8,128)(2,1)}, u32[]{:S(2)}) copy-start(bf16[2048,256]{1,0:T(8,128)(2,1)} %param.13) | copy-start | bytes 3145732
  7.2 42.4 %all-gather.2.cloned.1.call-start = ((), (), s32[]{:S(2)}) async-start(), calls=%async_computation.10 | async-start | bytes 4456448 | tf_op jit(solution)/shard_map/all_gather | solution.py:175
  14.3 8.8 %copy-start.5 = (s32[1024]{0:T(1024)S(1)}, s32[1024]{0:T(1024)}, u32[]{:S(2)}) copy-start(s32[1024]{0:T(1024)} %param.11) | copy-start | bytes 12292
  14.4 8.8 %copy-start.7 = (f32[4]{0:T(128)S(1)}, f32[4]{0:T(128)}, u32[]{:S(2)}) copy-start(f32[4]{0:T(128)} %param.12) | copy-start | bytes 52
  14.4 8.9 %copy-start.6 = (s32[2048]{0:T(1024)S(1)}, s32[2048]{0:T(1024)}, u32[]{:S(2)}) copy-start(s32[2048]{0:T(1024)} %param.8) | copy-start | bytes 24580
  57.5 15.8 %copy-start.1 = (f32[1024,2048]{1,0:T(8,128)}, f32[1024,2048]{1,0:T(8,128)S(1)}, u32[]{:S(2)}) copy-start(f32[1024,2048]{1,0:T(8,128)S(1)} %get-tuple-element.19) | copy-start | bytes 25165828
  57.5 3.7 %collective-permute-start = (f32[1024]{0:T(1024)S(1)}, f32[1024]{0:T(1024)S(1)}, u32[]{:S(2)}, u32[]{:S(2)}) collective-permute-start(f32[1024]{0:T(1024)S(1)} %get-tuple-element.18), channel_id=1, source_target_pairs={{0,32},{16,48},{32,0},{48,16},{64,96},{80,112},{96,64},{112,80},{1... | collective-permute-start | bytes 12296 | tf_op jit(solution)/shard_map/ppermute | solution.py:41
  61.2 5.1 %collective-permute-start.1 = (f32[1024]{0:T(1024)S(1)}, f32[1024]{0:T(1024)S(1)}, u32[]{:S(2)}, u32[]{:S(2)}) collective-permute-start(f32[1024]{0:T(1024)S(1)} %add.71), channel_id=1, source_target_pairs={{0,16},{16,0},{32,48},{48,32},{64,80},{80,64},{96,112},{112,96},{1... | collective-permute-start | bytes 12296 | tf_op jit(solution)/shard_map/ppermute | solution.py:41
  66.3 5.1 %collective-permute-start.2 = (f32[1024]{0:T(1024)S(1)}, f32[1024]{0:T(1024)S(1)}, u32[]{:S(2)}, u32[]{:S(2)}) collective-permute-start(f32[1024]{0:T(1024)S(1)} %add.72), channel_id=1, source_target_pairs={{0,64},{16,80},{32,96},{48,112},{64,0},{80,16},{96,32},{112,48},{1... | collective-permute-start | bytes 12296 | tf_op jit(solution)/shard_map/ppermute | solution.py:41
  73.2 2.0 copy-start.2
  96.4 15.8 %all-to-all-start.1 = ((f32[8,128,256]{2,1,0:T(8,128)}), f32[8,128,256]{2,1,0:T(8,128)S(1)}, u32[]{:S(2)}, u32[]{:S(2)}) async-start(f32[8,128,256]{2,1,0:T(8,128)} %broadcast_in_dim.76), calls=%async_computation.1 | async-start | bytes 2097152 | tf_op jit(solution)/shard_map/all_to_all | solution.py:115
  116.0 40.1 %copy-start.3 = (bf16[1024,2048]{1,0:T(8,128)(2,1)S(1)}, bf16[1024,2048]{1,0:T(8,128)(2,1)}, u32[]{:S(2)}) copy-start(bf16[1024,2048]{1,0:T(8,128)(2,1)} %copy-done.2) | copy-start | bytes 12582916
  183.6 17.8 %all-to-all-start.5 = ((f32[8,128,256]{2,1,0:T(8,128)}), f32[8,128,256]{2,1,0:T(8,128)S(1)}, u32[]{:S(2)}, u32[]{:S(2)}) async-start(f32[8,128,256]{2,1,0:T(8,128)} %broadcast_in_dim.80), calls=%async_computation.5 | async-start | bytes 2097152 | tf_op jit(solution)/shard_map/all_to_all | solution.py:115
  206.2 40.5 %copy-start.4 = (bf16[1024,2048]{1,0:T(8,128)(2,1)S(1)}, bf16[1024,2048]{1,0:T(8,128)(2,1)}, u32[]{:S(2)}) copy-start(bf16[1024,2048]{1,0:T(8,128)(2,1)} %copy-done.2) | copy-start | bytes 12582916
  271.4 17.8 %all-to-all-start.9 = ((f32[8,128,256]{2,1,0:T(8,128)}), f32[8,128,256]{2,1,0:T(8,128)S(1)}, u32[]{:S(2)}, u32[]{:S(2)}) async-start(f32[8,128,256]{2,1,0:T(8,128)} %broadcast_in_dim.133), calls=%async_computation.9 | async-start | bytes 2097152 | tf_op jit(solution)/shard_map/all_to_all | solution.py:115
Sparse Core Ops, SparseCore 0:
  9.7 39.8 all-gather.1

commit v5 on v4

--- a/solution.py
+++ b/solution.py
@@ -123,10 +123,7 @@
     return exchange_gather(part.astype(gather_dtype), axis), extra
 
 
-def conjugate_gradients(kernel, targets, n_rows, sample_bits, landmark_bits):
-    rhs_part = jnp.dot(kernel.T, targets, preferred_element_type=jnp.float32)
-    rhs_total, _ = exchange_sum(rhs_part, None, "sample", jnp.float32, jnp.float32)
-    rhs = rhs_total / math.sqrt(n_rows)
+def conjugate_gradients(kernel, rhs, n_rows, sample_bits, landmark_bits):
     column_count = rhs.shape[1]
     weights = jnp.zeros_like(rhs)
     residual = rhs
@@ -167,6 +164,40 @@
     return weights, residual
 
 
+def centred_rhs(raw, targets, n_rows):
+    size = lax.axis_size("sample")
+    row_count, landmark_count = raw.shape
+    column_count = targets.shape[1]
+    chunk = landmark_count // size
+    column_sum = jnp.sum(raw, axis=0)
+    local_mean = column_sum / row_count
+    centred = (raw - local_mean[None, :]).astype(jnp.bfloat16)
+    product = jnp.dot(centred.T, targets, preferred_element_type=jnp.float32)
+    target_sum = jnp.sum(targets.astype(jnp.float32), axis=0)
+    payload = jnp.concatenate(
+        [
+            product.reshape(size, chunk, column_count),
+            jnp.broadcast_to(target_sum[None, None, :], (size, 1, column_count)),
+            jnp.pad(column_sum.reshape(size, 1, chunk), ((0, 0), (0, 0), (0, column_count - chunk))),
+        ],
+        axis=1,
+    )
+    got = lax.all_to_all(payload, "sample", 0, 0, tiled=False)
+    target_sums = got[:, chunk, :]
+    column_sums = got[:, chunk + 1, :chunk]
+    mean_chunk = jnp.sum(column_sums, axis=0) / n_rows
+    offsets = column_sums / row_count - mean_chunk[None, :]
+    correction = jnp.sum(offsets[:, :, None] * target_sums[:, None, :], axis=0)
+    rhs_chunk = (jnp.sum(got[:, :chunk, :], axis=0) + correction) / math.sqrt(n_rows)
+    back = jnp.concatenate(
+        [rhs_chunk, jnp.pad(mean_chunk[None, :], ((0, 0), (0, column_count - chunk)))], axis=0
+    )
+    whole = lax.all_to_all(jnp.broadcast_to(back[None], (size,) + back.shape), "sample", 0, 0, tiled=False)
+    rhs = whole[:, :chunk, :].reshape(landmark_count, column_count)
+    column_mean = whole[:, chunk, :chunk].reshape(landmark_count)
+    return rhs, column_mean
+
+
 def on_device(summaries, row_level, pool, pool_level, landmark_index, level_scale, targets):
     sample_bits = partner_bits(lax.axis_size("sample"), (2, 1, 4, 8, 16, 32, 64))
     landmark_bits = partner_bits(lax.axis_size("landmark"), (1, 2, 4, 8, 16, 32, 64))
@@ -179,13 +210,13 @@
     row_factor = 1.0 / math.sqrt(feature_count) / level_values(row_level, level_scale)
     anchor_factor = 1.0 / level_values(anchor_level, level_scale)
     raw = raw_block(gathered, row_factor, anchors, anchor_factor)
-    column_mean = butterfly_sum(jnp.sum(raw, axis=0), "sample", sample_bits) / n_rows
+    rhs, column_mean = centred_rhs(raw, targets, n_rows)
     kernel = (raw - column_mean[None, :]).astype(jnp.bfloat16)
     column_count = targets.shape[1]
     group_width = column_count // GROUPS
     results = [
         conjugate_gradients(
-            kernel, targets[:, g * group_width:(g + 1) * group_width], n_rows, sample_bits, landmark_bits
+            kernel, rhs[:, g * group_width:(g + 1) * group_width], n_rows, sample_bits, landmark_bits
         )
         for g in range(GROUPS)
     ]

time: 300 us -> 299 us (level)
  starting transfers between devices: 18.1 us -> 11.1 us
  waiting for transfers between devices: 62 us -> 66.8 us
    all_to_all x0 -> x2, blocking collectives: none -> 44.3 us  [the longest x1 24.5 us: centred_rhs(): got = lax.all_to_all(payload, 'sample', 0, 0, tiled=False)]
    all_to_all x5 -> x4, blocking collectives: 108 us -> 83.4 us  [exchange_scatter(): got = lax.all_to_all(chunks, axis, 0, 0, tiled=False)]
    all_to_all x2 -> x1, blocking collectives: 38.1 us -> 19.3 us  [exchange_gather(): lax.all_to_all(jnp.broadcast_to(part[None], (size,) + part.shape), axis,...]
    all_to_all x3, waiting for transfers between devices: 28.6 us -> 39.6 us  [exchange_gather(): lax.all_to_all(jnp.broadcast_to(part[None], (size,) + part.shape), axis,...]
    ppermute x3 -> x0, starting transfers between devices: 7.36 us -> none  [butterfly_sum(): x = x + lax.ppermute(x, axis, perm)]
    ppermute x3 -> x0, waiting for transfers between devices: 6.55 us -> none  [butterfly_sum(): x = x + lax.ppermute(x, axis, perm)]
    another operation x3, other arithmetic: 1.83 us -> 5.67 us
  transfers between devices with their start and end apart: 7 -> 4, of which waited for: 7 -> 4; matrix products, arithmetic and copies ran while one was open for 9% -> 7% of each run, Pallas kernels for 0% -> 0%
where the time goes in v5:
time: 299 us; the launch traced here: 298 us
  blocking collectives  147 us (49%)
  waiting for transfers between devices  66.8 us (22%)
  local copies, waits for them, and re-layouts  25.1 us (8%)
  matrix products  18.5 us (6%)
  other arithmetic  15.2 us (5%)
  between operations  14.5 us (5%)
  starting transfers between devices  11.1 us (4%)
    all_to_all x4, blocking collectives, exchange_scatter(): got = lax.all_to_all(chunks, axis, 0, 0, tiled=False)  83.4 us
    all_to_all x3, waiting for transfers between devices, exchange_gather(): lax.all_to_all(jnp.broadcast_to(part[None], (size,) + part.shape), axis,...  39.6 us
    all_gather x1, waiting for transfers between devices, on_device(): gathered = lax.all_gather(summaries, 'landmark', axis=1, tiled=True)  26.5 us
    all_to_all x1, blocking collectives, centred_rhs(): got = lax.all_to_all(payload, 'sample', 0, 0, tiled=False)  24.5 us
    all_to_all x1, blocking collectives, centred_rhs(): lax.all_to_all(jnp.broadcast_to(back[None], (size,) + back.shape), 'sampl...  19.8 us
    all_to_all x1, blocking collectives, exchange_gather(): lax.all_to_all(jnp.broadcast_to(part[None], (size,) + part.shape), axis,...  19.3 us
    all_to_all x3, starting transfers between devices, exchange_gather(): lax.all_to_all(jnp.broadcast_to(part[None], (size,) + part.shape), axis,...  11.1 us
    gather x1, local copies, waits for them, and re-layouts, on_device(): anchors = jnp.take(pool, landmark_index, axis=0)  7.79 us
  transfers between devices with their start and end apart: 4, of which 4 were waited for; matrix products, arithmetic and copies ran while one was open for 7% of the time, Pallas kernels for 0%

profile of v5, /device:TPU:0, one launch (start us, length us, event | category | flops | bytes accessed | tf_op | source)
XLA Modules:
  0.0 298.2 jit_solution(1105036814121075629)
XLA Ops:
  7.2 0.0 copy-start
  7.2 0.0 all-gather.2.cloned.1.call-start
  7.2 0.7 all-gather.2.cloned.1.call-update
  7.9 0.7 fusion.14
  8.6 6.1 %gather_fusion.1 = s32[1024]{0:T(1024)S(1)} fusion(s32[2048]{0:T(1024)S(1)} %copy-done, s32[1024]{0:T(1024)S(1)} %fusion.14), kind=kCustom, calls=%fused_computation.1 | custom fusion | bytes 12288 | tf_op jit(solution)/shard_map/jit(_take)/gather | solution.py:209
  14.8 0.0 copy-start.7
  14.8 0.0 copy-start.9
  14.8 0.0 copy-start.8
  14.8 0.0 copy-start.6
  14.8 7.8 %gather_fusion = bf16[1024,1024]{1,0:T(8,128)(2,1)S(1)} fusion(bf16[2048,1024]{1,0:T(8,128)(2,1)} %param.9, s32[1024]{0:T(1024)S(1)} %fusion.14), kind=kCustom, calls=%fused_computation | custom fusion | bytes 4198400 | tf_op jit(solution)/shard_map/jit(_take)/gather | solution.py:208
  22.6 0.0 copy-done.9
  22.7 0.1 select_reduce_fusion.1
  22.7 0.1 select_reduce_fusion
  22.8 0.0 copy-done.6
  22.9 0.3 convert_reduce_fusion.2
  23.2 26.5 %all-gather.2.cloned.1.call-done = bf16[2048,1024]{0,1:T(8,128)(2,1)} async-done(((bf16[2048,64]{0,1:T(8,128)(2,1)}), bf16[2048,1024]{0,1:T(8,128)(2,1)}) %all-gather.2.cloned.1.call-update) | async-done | bytes 4194320 | tf_op jit(solution)/shard_map/all_gather | solution.py:206
  49.7 7.3 %fusion = (f32[1024]{0:T(1024)S(1)}, f32[1024,2048]{1,0:T(8,128)S(1)}) fusion(f32[1024]{0:T(1024)S(1)} %broadcast_divide_fusion.1, f32[2048]{0:T(1024)S(1)} %broadcast_divide_fusion, bf16[2048,1024]{0,1:T(8,128)(2,1)} %all-gather.2.cloned.1.call-done, bf16[1024,1024]{1,0:T(8,128)(2,1)S(1)} %gather_fusion, pred[1024]{0:T(1024)(128)(4,1)S(1)} %get-tuple-element.5), kind=kOutput, calls=%fused_computation.5 | convolution fusion | flops 4302306304 | bytes 14697472 | tf_op jit(solution)/shard_map/dot_general | solution.py:27
  57.0 0.0 copy-start.2
  57.0 1.8 fusion.1
  58.8 0.1 select_maximum_fusion
  58.9 24.5 %all_to_all.50 = f32[8,130,256]{2,1,0:T(8,128)S(1)} all-to-all(f32[8,130,256]{2,1,0:T(8,128)S(1)} %select_maximum_fusion), channel_id=1, replica_groups=mesh['sample'=8,'landmark'=16] {'sample'}, dimensions={0} | all-to-all | bytes 2129920 | tf_op jit(solution)/shard_map/all_to_all | solution.py:185
  83.5 0.2 slice_reduce_fusion
  83.8 0.1 broadcast_in_dim.79
  83.9 19.8 %all_to_all.51 = f32[8,129,256]{2,1,0:T(8,128)S(1)} all-to-all(f32[8,129,256]{2,1,0:T(8,128)S(1)} %broadcast_in_dim.79), channel_id=1, replica_groups=mesh['sample'=8,'landmark'=16] {'sample'}, dimensions={0} | all-to-all | bytes 2113536 | tf_op jit(solution)/shard_map/all_to_all | solution.py:195
  103.6 3.2 %fusion.39 = bf16[2048,1024]{0,1:T(8,128)(2,1)} fusion(f32[1024]{0:T(1024)S(1)} %bitcast.82, f32[1024]{0:T(1024)S(1)} %broadcast_divide_fusion.1, f32[1024,2048]{1,0:T(8,128)S(1)} %get-tuple-element.22, f32[2048]{0:T(1024)S(1)} %broadcast_divide_fusion), kind=kLoop, calls=%fused_computation.101 | loop fusion | flops 8388608 | bytes 12599296 | tf_op jit(solution)/shard_map/sub | solution.py:214
  106.8 6.4 %copy.15 = bf16[2048,1024]{1,0:T(8,128)(2,1)} copy(bf16[2048,1024]{0,1:T(8,128)(2,1)} %fusion.39) | data formatting | bytes 8388608 | tf_op jit(solution)/shard_map/dot_general | solution.py:133
  113.2 0.2 multiply_reduce_fusion.4
  113.4 0.1 slice.174
  113.4 3.4 %convolution_convert_fusion.1 = bf16[16,128,256]{2,1,0:T(8,128)(2,1)S(1)} fusion(bf16[16,128,1024]{2,1,0:T(8,128)(2,1)} %bitcast.73, bf16[1024,256,1]{1,0,2:T(8,128)(2,1)S(1)} %bitcast.81), kind=kOutput, calls=%fused_computation.16 | convolution fusion | flops 1074266112 | bytes 5767168 | tf_op jit(solution)/shard_map/dot_general | solution.py:133
  116.9 0.1 pad_maximum_fusion
  117.0 20.4 %all_to_all.52 = bf16[16,134,256]{2,1,0:T(8,128)(2,1)S(1)} all-to-all(bf16[16,134,256]{2,1,0:T(8,128)(2,1)S(1)} %pad_maximum_fusion), channel_id=1, replica_groups=mesh['sample'=8,'landmark'=16] {'landmark'}, dimensions={0} | all-to-all | bytes 2195456 | tf_op jit(solution)/shard_map/all_to_all | solution.py:105
  137.4 0.2 convert_reduce_fusion.1
  137.6 1.1 broadcast_in_dim.81
  138.7 3.8 %all-to-all-start.3 = ((bf16[16,128,256]{2,1,0:T(8,128)(2,1)}), bf16[16,128,256]{2,1,0:T(8,128)(2,1)S(1)}, u32[]{:S(2)}, u32[]{:S(2)}) async-start(bf16[16,128,256]{2,1,0:T(8,128)(2,1)} %broadcast_in_dim.81), calls=%async_computation.3 | async-start | bytes 2097152 | tf_op jit(solution)/shard_map/all_to_all | solution.py:115
  142.5 5.6 %subtract_convert_fusion = bf16[1024,2048]{1,0:T(8,128)(2,1)} fusion(f32[1024,2048]{1,0:T(8,128)} %copy-done.2, f32[1024]{0:T(1024)S(1)} %bitcast.83, f32[1024]{0:T(1024)S(1)} %broadcast_divide_fusion.1, f32[2048]{0:T(1024)S(1)} %broadcast_divide_fusion), kind=kLoop, calls=%fused_computation.2 | loop fusion | flops 8388608 | bytes 12599296 | tf_op jit(solution)/shard_map/convert.6
  148.2 10.9 %all-to-all-done.3 = bf16[16,128,256]{2,1,0:T(8,128)(2,1)S(1)} async-done(((bf16[16,128,256]{2,1,0:T(8,128)(2,1)}), bf16[16,128,256]{2,1,0:T(8,128)(2,1)S(1)}, u32[]{:S(2)}, u32[]{:S(2)}) %all-to-all-start.3) | async-done | bytes 1048608 | tf_op jit(solution)/shard_map/all_to_all | solution.py:115
  159.0 3.5 %fusion.27 = f32[8,128,256]{2,1,0:T(8,128)S(1)} fusion(bf16[8,128,2048]{2,1,0:T(8,128)(2,1)} %bitcast.75, bf16[2048,256,1]{1,0,2:T(8,128)(2,1)S(1)} %bitcast.77), kind=kOutput, calls=%fused_computation.99 | convolution fusion | flops 1073741824 | bytes 6291456 | tf_op jit(solution)/shard_map/dot_general | solution.py:155
  162.5 0.3 multiply_reduce_fusion.1
  162.8 0.1 pad_maximum_fusion.1
  162.9 20.8 %all_to_all.53 = f32[8,129,256]{2,1,0:T(8,128)S(1)} all-to-all(f32[8,129,256]{2,1,0:T(8,128)S(1)} %pad_maximum_fusion.1), channel_id=1, replica_groups=mesh['sample'=8,'landmark'=16] {'sample'}, dimensions={0} | all-to-all | bytes 2113536 | tf_op jit(solution)/shard_map/all_to_all | solution.py:105
  183.6 0.1 reduce_sum.158
  183.7 1.1 broadcast_in_dim.83
  184.8 3.6 %all-to-all-start.5 = ((f32[8,128,256]{2,1,0:T(8,128)}), f32[8,128,256]{2,1,0:T(8,128)S(1)}, u32[]{:S(2)}, u32[]{:S(2)}) async-start(f32[8,128,256]{2,1,0:T(8,128)} %broadcast_in_dim.83), calls=%async_computation.5 | async-start | bytes 2097152 | tf_op jit(solution)/shard_map/all_to_all | solution.py:115
  188.4 14.5 %all-to-all-done.5 = f32[8,128,256]{2,1,0:T(8,128)S(1)} async-done(((f32[8,128,256]{2,1,0:T(8,128)}), f32[8,128,256]{2,1,0:T(8,128)S(1)}, u32[]{:S(2)}, u32[]{:S(2)}) %all-to-all-start.5) | async-done | bytes 1048608 | tf_op jit(solution)/shard_map/all_to_all | solution.py:115
  202.9 1.3 multiply_reduce_fusion.3
  204.2 1.2 copy-done.3
  205.4 1.3 convolution_convert_fusion
  206.8 0.1 pad_maximum_fusion.2
  206.9 20.3 %all_to_all.54 = bf16[16,134,256]{2,1,0:T(8,128)(2,1)S(1)} all-to-all(bf16[16,134,256]{2,1,0:T(8,128)(2,1)S(1)} %pad_maximum_fusion.2), channel_id=1, replica_groups=mesh['sample'=8,'landmark'=16] {'landmark'}, dimensions={0} | all-to-all | bytes 2195456 | tf_op jit(solution)/shard_map/all_to_all | solution.py:105
  227.1 0.2 convert_reduce_fusion
  227.3 0.1 broadcast_in_dim.85
  227.4 19.3 %all_to_all.55 = bf16[16,128,256]{2,1,0:T(8,128)(2,1)S(1)} all-to-all(bf16[16,128,256]{2,1,0:T(8,128)(2,1)S(1)} %broadcast_in_dim.85), channel_id=1, replica_groups=mesh['sample'=8,'landmark'=16] {'landmark'}, dimensions={0} | all-to-all | bytes 2097152 | tf_op jit(solution)/shard_map/all_to_all | solution.py:115
  246.8 1.3 fusion.28
  248.0 0.3 multiply_reduce_fusion
  248.4 0.1 pad_maximum_fusion.3
  248.4 21.9 %all_to_all.56 = f32[8,129,256]{2,1,0:T(8,128)S(1)} all-to-all(f32[8,129,256]{2,1,0:T(8,128)S(1)} %pad_maximum_fusion.3), channel_id=1, replica_groups=mesh['sample'=8,'landmark'=16] {'sample'}, dimensions={0} | all-to-all | bytes 2113536 | tf_op jit(solution)/shard_map/all_to_all | solution.py:105
  270.4 0.1 reduce_sum.163
  270.4 1.1 broadcast_in_dim.87
  271.5 3.7 %all-to-all-start.9 = ((f32[8,128,256]{2,1,0:T(8,128)}), f32[8,128,256]{2,1,0:T(8,128)S(1)}, u32[]{:S(2)}, u32[]{:S(2)}) async-start(f32[8,128,256]{2,1,0:T(8,128)} %broadcast_in_dim.87), calls=%async_computation.9 | async-start | bytes 2097152 | tf_op jit(solution)/shard_map/all_to_all | solution.py:115
  275.2 14.2 %all-to-all-done.9 = f32[8,128,256]{2,1,0:T(8,128)S(1)} async-done(((f32[8,128,256]{2,1,0:T(8,128)}), f32[8,128,256]{2,1,0:T(8,128)S(1)}, u32[]{:S(2)}, u32[]{:S(2)}) %all-to-all-start.9) | async-done | bytes 1048608 | tf_op jit(solution)/shard_map/all_to_all | solution.py:115
  289.5 0.1 broadcast_multiply_fusion
  289.6 0.0 copy-start.1
  289.6 1.8 fusion.6
  291.4 0.0 copy-done.1
  (43 shorter events, 0.3 us)
Async XLA Ops:
  7.2 1.4 copy-start
  7.2 42.5 %all-gather.2.cloned.1.call-start = ((), (), s32[]{:S(2)}) async-start(), calls=%async_computation.10 | async-start | bytes 4456448 | tf_op jit(solution)/shard_map/all_gather | solution.py:206
  14.8 7.9 %copy-start.7 = (s32[1024]{0:T(1024)S(1)}, s32[1024]{0:T(1024)}, u32[]{:S(2)}) copy-start(s32[1024]{0:T(1024)} %param.11) | copy-start | bytes 12292
  14.8 7.9 %copy-start.9 = (f32[4]{0:T(128)S(1)}, f32[4]{0:T(128)}, u32[]{:S(2)}) copy-start(f32[4]{0:T(128)} %param.12) | copy-start | bytes 52
  14.8 7.9 %copy-start.8 = (s32[2048]{0:T(1024)S(1)}, s32[2048]{0:T(1024)}, u32[]{:S(2)}) copy-start(s32[2048]{0:T(1024)} %param.8) | copy-start | bytes 24580
  14.8 8.0 %copy-start.6 = (bf16[2048,256]{1,0:T(8,128)(2,1)S(1)}, bf16[2048,256]{1,0:T(8,128)(2,1)}, u32[]{:S(2)}) copy-start(bf16[2048,256]{1,0:T(8,128)(2,1)} %param.13) | copy-start | bytes 3145732
  57.0 46.7 %copy-start.2 = (f32[1024,2048]{1,0:T(8,128)}, f32[1024,2048]{1,0:T(8,128)S(1)}, u32[]{:S(2)}) copy-start(f32[1024,2048]{1,0:T(8,128)S(1)} %get-tuple-element.22) | copy-start | bytes 25165828
  138.7 20.3 %all-to-all-start.3 = ((bf16[16,128,256]{2,1,0:T(8,128)(2,1)}), bf16[16,128,256]{2,1,0:T(8,128)(2,1)S(1)}, u32[]{:S(2)}, u32[]{:S(2)}) async-start(bf16[16,128,256]{2,1,0:T(8,128)(2,1)} %broadcast_in_dim.81), calls=%async_computation.3 | async-start | bytes 2097152 | tf_op jit(solution)/shard_map/all_to_all | solution.py:115
  184.8 18.1 %all-to-all-start.5 = ((f32[8,128,256]{2,1,0:T(8,128)}), f32[8,128,256]{2,1,0:T(8,128)S(1)}, u32[]{:S(2)}, u32[]{:S(2)}) async-start(f32[8,128,256]{2,1,0:T(8,128)} %broadcast_in_dim.83), calls=%async_computation.5 | async-start | bytes 2097152 | tf_op jit(solution)/shard_map/all_to_all | solution.py:115
  202.9 2.6 copy-start.3
  227.1 19.7 %copy-start.4 = (bf16[1024,2048]{1,0:T(8,128)(2,1)S(1)}, bf16[1024,2048]{1,0:T(8,128)(2,1)}, u32[]{:S(2)}) copy-start(bf16[1024,2048]{1,0:T(8,128)(2,1)} %subtract_convert_fusion) | copy-start | bytes 12582916
  271.5 18.1 %copy-start.5 = (f32[8,128,256]{2,1,0:T(8,128)S(1)}, f32[8,128,256]{2,1,0:T(8,128)}, u32[]{:S(2)}) copy-start(f32[8,128,256]{2,1,0:T(8,128)} %get-tuple-element.12) | copy-start | bytes 3145732
  271.5 18.0 %all-to-all-start.9 = ((f32[8,128,256]{2,1,0:T(8,128)}), f32[8,128,256]{2,1,0:T(8,128)S(1)}, u32[]{:S(2)}, u32[]{:S(2)}) async-start(f32[8,128,256]{2,1,0:T(8,128)} %broadcast_in_dim.87), calls=%async_computation.9 | async-start | bytes 2097152 | tf_op jit(solution)/shard_map/all_to_all | solution.py:115
  289.6 1.8 copy-start.1
Sparse Core Ops, SparseCore 0:
  9.7 39.9 all-gather.1

commit v6 on v4

--- a/solution.py
+++ b/solution.py
@@ -123,6 +123,22 @@
     return exchange_gather(part.astype(gather_dtype), axis), extra
 
 
+def native_scatter(x, extra, axis):
+    size = lax.axis_size(axis)
+    rows, columns = x.shape
+    chunks = x.reshape(size, rows // size, columns)
+    packed = extra.reshape(-1, columns)
+    chunks = jnp.concatenate(
+        [chunks, jnp.broadcast_to(packed[None], (size,) + packed.shape)], axis=1
+    )
+    total = lax.psum_scatter(chunks, axis, scatter_dimension=0, tiled=False)
+    return total[: rows // size], total[rows // size:].reshape(-1)
+
+
+def native_gather(part, axis):
+    return lax.all_gather(part, axis, axis=0, tiled=True)
+
+
 def conjugate_gradients(kernel, targets, n_rows, sample_bits, landmark_bits):
     rhs_part = jnp.dot(kernel.T, targets, preferred_element_type=jnp.float32)
     rhs_total, _ = exchange_sum(rhs_part, None, "sample", jnp.float32, jnp.float32)
@@ -137,7 +153,7 @@
             sums = jnp.concatenate(
                 [jnp.sum(direction * direction, axis=0), jnp.sum(residual * residual, axis=0)]
             )
-            row_chunk, landmark_sums = exchange_scatter(row_part, sums, "landmark", jnp.bfloat16)
+            row_chunk, landmark_sums = native_scatter(row_part, sums, "landmark")
             direction_square = landmark_sums[:column_count]
             norm_now = landmark_sums[column_count:]
         else:
@@ -145,7 +161,7 @@
             sums = jnp.concatenate(
                 [jnp.sum(residual * residual, axis=0), jnp.sum(residual * direction, axis=0)]
             )
-            residual_chunk, landmark_sums = exchange_scatter(row_part, sums, "landmark", jnp.bfloat16)
+            residual_chunk, landmark_sums = native_scatter(row_part, sums, "landmark")
             norm_next = landmark_sums[:column_count]
             cross = landmark_sums[column_count:]
             beta = norm_next / norm_now
@@ -153,7 +169,7 @@
             direction = residual + beta * direction
             direction_square = norm_next + 2.0 * beta * cross + beta * beta * direction_square
             norm_now = norm_next
-        row_half = exchange_gather(row_chunk.astype(jnp.bfloat16), "landmark")
+        row_half = native_gather(row_chunk.astype(jnp.bfloat16), "landmark")
         row_square = jnp.sum(jnp.square(row_half.astype(jnp.float32)), axis=0)
         column_part = jnp.dot(kernel.T, row_half, preferred_element_type=jnp.float32)
         column_total, row_square_total = exchange_sum(

time: 300 us -> 432 us (1.44)
  waiting for transfers between devices: 62 us -> 255 us
  blocking collectives: 146 us -> 69.1 us
  other arithmetic: 14.8 us -> 23.3 us
  matrix products: 18.5 us -> 24.9 us
    reduce_scatter x0 -> x2, waiting for transfers between devices: none -> 129 us  [native_scatter(): total = lax.psum_scatter(chunks, axis, scatter_dimension=0, tiled=False)]
    all_gather x0 -> x2, waiting for transfers between devices: none -> 62.5 us  [native_gather(): return lax.all_gather(part, axis, axis=0, tiled=True)]
    all_to_all x5 -> x3, blocking collectives: 108 us -> 69.1 us  [exchange_scatter(): got = lax.all_to_all(chunks, axis, 0, 0, tiled=False)]
    all_to_all x2 -> x0, blocking collectives: 38.1 us -> none  [exchange_gather(): lax.all_to_all(jnp.broadcast_to(part[None], (size,) + part.shape), axis,...]
    dot_general x2, matrix products: 2.5 us -> 7.56 us  [conjugate_gradients(): jnp.dot(kernel.T, row_half, preferred_element_type=jnp.float32)]
    concatenate x2, other arithmetic: 0.02 us -> 4.73 us  [native_scatter(): jnp.concatenate([chunks, jnp.broadcast_to(packed[None], (size,) + packed....]
  transfers between devices with their start and end apart: 7 -> 11, of which waited for: 7 -> 10; matrix products, arithmetic and copies ran while one was open for 9% -> 7% of each run, Pallas kernels for 0% -> 0%
where the time goes in v6:
time: 432 us; the launch traced here: 431 us
  waiting for transfers between devices  255 us (59%)
  blocking collectives  69.1 us (16%)
  local copies, waits for them, and re-layouts  26.5 us (6%)
  matrix products  24.9 us (6%)
  other arithmetic  23.3 us (5%)
  starting transfers between devices  18.4 us (4%)
  between operations  14.1 us (3%)
    reduce_scatter x2, waiting for transfers between devices, native_scatter(): total = lax.psum_scatter(chunks, axis, scatter_dimension=0, tiled=False)  129 us
    all_to_all x3, blocking collectives, exchange_scatter(): got = lax.all_to_all(chunks, axis, 0, 0, tiled=False)  69.1 us
    all_gather x2, waiting for transfers between devices, native_gather(): return lax.all_gather(part, axis, axis=0, tiled=True)  62.5 us
    all_to_all x3, waiting for transfers between devices, exchange_gather(): lax.all_to_all(jnp.broadcast_to(part[None], (size,) + part.shape), axis,...  29.1 us
    all_gather x1, waiting for transfers between devices, on_device(): gathered = lax.all_gather(summaries, 'landmark', axis=1, tiled=True)  26.2 us
    all_to_all x3, starting transfers between devices, exchange_gather(): lax.all_to_all(jnp.broadcast_to(part[None], (size,) + part.shape), axis,...  10.7 us
    gather x1, local copies, waits for them, and re-layouts, on_device(): anchors = jnp.take(pool, landmark_index, axis=0)  8.79 us
  transfers between devices with their start and end apart: 11, of which 10 were waited for; matrix products, arithmetic and copies ran while one was open for 7% of the time, Pallas kernels for 0%

profile of v6, /device:TPU:0, one launch (start us, length us, event | category | flops | bytes accessed | tf_op | source)
XLA Modules:
  0.0 430.9 jit_solution(6700054975939726392)
XLA Ops:
  7.2 0.0 all-gather.4.cloned.1.call-start
  7.2 0.7 all-gather.4.cloned.1.call-update
  7.9 0.7 fusion.14
  8.6 5.7 %gather_fusion.1 = s32[1024]{0:T(1024)S(1)} fusion(s32[2048]{0:T(1024)} %param.10, s32[1024]{0:T(1024)S(1)} %fusion.14), kind=kCustom, calls=%fused_computation.1 | custom fusion | bytes 12288 | tf_op jit(solution)/shard_map/jit(_take)/gather | solution.py:194
  14.4 8.8 %gather_fusion = bf16[1024,1024]{1,0:T(8,128)(2,1)} fusion(bf16[2048,1024]{1,0:T(8,128)(2,1)} %param.9, s32[1024]{0:T(1024)S(1)} %fusion.14), kind=kCustom, calls=%fused_computation | custom fusion | bytes 4198400 | tf_op jit(solution)/shard_map/jit(_take)/gather | solution.py:193
  23.2 0.1 select_reduce_fusion.1
  23.3 0.1 select_reduce_fusion
  23.4 26.2 %all-gather.4.cloned.1.call-done = bf16[2048,1024]{0,1:T(8,128)(2,1)} async-done(((bf16[2048,64]{0,1:T(8,128)(2,1)}), bf16[2048,1024]{0,1:T(8,128)(2,1)}) %all-gather.4.cloned.1.call-update) | async-done | bytes 4194320 | tf_op jit(solution)/shard_map/all_gather | solution.py:191
  49.6 7.9 %fusion = (f32[1024]{0:T(1024)S(1)}, f32[1024,2048]{1,0:T(8,128)S(1)}) fusion(f32[1024]{0:T(1024)S(1)} %broadcast_divide_fusion.1, f32[2048]{0:T(1024)S(1)} %broadcast_divide_fusion, bf16[2048,1024]{0,1:T(8,128)(2,1)} %all-gather.4.cloned.1.call-done, bf16[1024,1024]{1,0:T(8,128)(2,1)} %gather_fusion, pred[1024]{0:T(1024)(128)(4,1)S(1)} %get-tuple-element.5), kind=kOutput, calls=%fused_computation.4 | convolution fusion | flops 4302306304 | bytes 14697472 | tf_op jit(solution)/shard_map/dot_general | solution.py:27
  57.5 1.6 collective-permute-start
  59.1 2.1 collective-permute-done
  61.2 2.8 collective-permute-start.1
  64.0 2.3 collective-permute-done.1
  66.3 3.0 collective-permute-start.2
  69.3 2.1 collective-permute-done.2
  71.4 1.8 subtract_convert_fusion
  73.3 1.3 fusion.24
  74.5 0.7 copy-done.2
  75.2 20.1 %all_to_all.30 = f32[8,128,256]{2,1,0:T(8,128)S(1)} all-to-all(f32[8,128,256]{2,1,0:T(8,128)S(1)} %bitcast.108), channel_id=1, replica_groups=mesh['sample'=8,'landmark'=16] {'sample'}, dimensions={0} | all-to-all | bytes 2097152 | tf_op jit(solution)/shard_map/all_to_all | solution.py:105
  95.3 0.1 reduce_sum.106
  95.4 1.1 broadcast_in_dim.115
  96.4 3.6 all-to-all-start.1
  100.0 0.2 reduce-scatter.3.cloned.1.call-start
  100.2 5.6 %fusion.40 = bf16[2048,1024]{0,1:T(8,128)(2,1)} fusion(f32[1024]{0:T(1024)S(1)} %add_multiply_fusion, f32[1024]{0:T(1024)S(1)} %broadcast_divide_fusion.1, f32[1024,2048]{1,0:T(8,128)} %copy-done.1, f32[2048]{0:T(1024)S(1)} %broadcast_divide_fusion), kind=kLoop, calls=%fused_computation.74 | loop fusion | flops 8388608 | bytes 12599296 | tf_op jit(solution)/shard_map/sub | solution.py:199
  105.9 6.4 %copy.15 = bf16[2048,1024]{1,0:T(8,128)(2,1)} copy(bf16[2048,1024]{0,1:T(8,128)(2,1)} %fusion.40) | data formatting | bytes 8388608 | tf_op jit(solution)/shard_map/dot_general | solution.py:152
  112.3 0.2 multiply_convert_fusion
  112.5 3.5 fusion.25
  116.0 1.5 pad_maximum_fusion
  117.5 0.0 reduce-scatter.3.cloned.1.call-update
  117.6 0.0 all-gather.6.cloned.1.call-start
  117.6 66.2 %reduce-scatter.3.cloned.1.call-done = f32[1,130,256]{2,1,0:T(8,128)} async-done(((f32[16,130,256]{2,1,0:T(8,128)}), f32[1,130,256]{2,1,0:T(8,128)}) %reduce-scatter.3.cloned.1.call-update) | async-done | bytes 133136 | tf_op jit(solution)/shard_map/reduce_scatter | solution.py:134
  183.9 1.5 fusion.13
  185.4 0.0 all-gather.6.cloned.1.call-update
  185.4 31.5 %all-gather.6.cloned.1.call-done = bf16[2048,256]{1,0:T(8,128)(2,1)} async-done(((bf16[128,256]{1,0:T(8,128)(2,1)}), bf16[2048,256]{1,0:T(8,128)(2,1)}) %all-gather.6.cloned.1.call-update) | async-done | bytes 1048592 | tf_op jit(solution)/shard_map/all_gather | solution.py:139
  216.9 1.5 multiply_reduce_fusion.1
  218.5 3.7 fusion.26
  222.2 0.1 pad_maximum_fusion.2
  222.3 24.5 %all_to_all.31 = f32[8,129,256]{2,1,0:T(8,128)S(1)} all-to-all(f32[8,129,256]{2,1,0:T(8,128)S(1)} %pad_maximum_fusion.2), channel_id=1, replica_groups=mesh['sample'=8,'landmark'=16] {'sample'}, dimensions={0} | all-to-all | bytes 2113536 | tf_op jit(solution)/shard_map/all_to_all | solution.py:105
  246.9 0.1 reduce_sum.109
  247.0 1.1 broadcast_in_dim.119
  248.0 3.6 all-to-all-start.3
  251.6 0.0 reduce-scatter.5.cloned.1.call-start
  251.7 14.9 %all-to-all-done.3 = f32[8,128,256]{2,1,0:T(8,128)S(1)} async-done(((f32[8,128,256]{2,1,0:T(8,128)}), f32[8,128,256]{2,1,0:T(8,128)S(1)}, u32[]{:S(2)}, u32[]{:S(2)}) %all-to-all-start.3) | async-done | bytes 1048608 | tf_op jit(solution)/shard_map/all_to_all | solution.py:115
  266.6 1.4 multiply_reduce_fusion.3
  267.9 4.8 %fusion.27 = f32[16,128,256]{2,1,0:T(8,128)} fusion(bf16[16,128,1024]{2,1,0:T(8,128)(2,1)} %bitcast.105, bf16[1024,256,1]{1,0,2:T(8,128)(2,1)S(1)} %bitcast.110), kind=kOutput, calls=%fused_computation.72 | convolution fusion | flops 1073741824 | bytes 6815744 | tf_op jit(solution)/shard_map/dot_general | solution.py:160
  272.8 3.2 pad_maximum_fusion.1
  276.0 0.0 reduce-scatter.5.cloned.1.call-update
  276.0 0.0 all-gather.8.cloned.1.call-start
  276.0 63.2 %reduce-scatter.5.cloned.1.call-done = f32[1,130,256]{2,1,0:T(8,128)} async-done(((f32[16,130,256]{2,1,0:T(8,128)}), f32[1,130,256]{2,1,0:T(8,128)}) %reduce-scatter.5.cloned.1.call-update) | async-done | bytes 133136 | tf_op jit(solution)/shard_map/reduce_scatter | solution.py:134
  339.3 0.7 slice_divide_fusion
  340.0 1.6 fusion.12
  341.5 0.0 all-gather.8.cloned.1.call-update
  341.6 31.0 %all-gather.8.cloned.1.call-done = bf16[2048,256]{1,0:T(8,128)(2,1)} async-done(((bf16[128,256]{1,0:T(8,128)(2,1)}), bf16[2048,256]{1,0:T(8,128)(2,1)}) %all-gather.8.cloned.1.call-update) | async-done | bytes 1048592 | tf_op jit(solution)/shard_map/all_gather | solution.py:139
  372.5 3.8 fusion.28
  376.4 0.3 multiply_reduce_fusion
  376.7 0.1 pad_maximum_fusion.3
  376.8 24.5 %all_to_all.32 = f32[8,129,256]{2,1,0:T(8,128)S(1)} all-to-all(f32[8,129,256]{2,1,0:T(8,128)S(1)} %pad_maximum_fusion.3), channel_id=1, replica_groups=mesh['sample'=8,'landmark'=16] {'sample'}, dimensions={0} | all-to-all | bytes 2113536 | tf_op jit(solution)/shard_map/all_to_all | solution.py:105
  401.3 0.1 reduce_sum.113
  401.4 1.1 broadcast_in_dim.123
  402.5 3.6 all-to-all-start.5
  406.1 0.8 fusion.19
  406.9 14.2 %all-to-all-done.5 = f32[8,128,256]{2,1,0:T(8,128)S(1)} async-done(((f32[8,128,256]{2,1,0:T(8,128)}), f32[8,128,256]{2,1,0:T(8,128)S(1)}, u32[]{:S(2)}, u32[]{:S(2)}) %all-to-all-start.5) | async-done | bytes 1048608 | tf_op jit(solution)/shard_map/all_to_all | solution.py:115
  421.0 0.1 broadcast_multiply_fusion
  421.1 3.2 fusion.5
  (35 shorter events, 0.2 us)
Async XLA Ops:
  7.2 66.1 %copy-start = (bf16[2048,256]{1,0:T(8,128)(2,1)S(1)}, bf16[2048,256]{1,0:T(8,128)(2,1)}, u32[]{:S(2)}) copy-start(bf16[2048,256]{1,0:T(8,128)(2,1)} %param.13) | copy-start | bytes 3145732
  7.2 42.4 %all-gather.4.cloned.1.call-start = ((), (), s32[]{:S(2)}) async-start(), calls=%async_computation.8 | async-start | bytes 4456448 | tf_op jit(solution)/shard_map/all_gather | solution.py:191
  14.3 8.8 %copy-start.5 = (s32[1024]{0:T(1024)S(1)}, s32[1024]{0:T(1024)}, u32[]{:S(2)}) copy-start(s32[1024]{0:T(1024)} %param.11) | copy-start | bytes 12292
  14.4 8.8 %copy-start.7 = (f32[4]{0:T(128)S(1)}, f32[4]{0:T(128)}, u32[]{:S(2)}) copy-start(f32[4]{0:T(128)} %param.12) | copy-start | bytes 52
  14.4 8.9 %copy-start.6 = (s32[2048]{0:T(1024)S(1)}, s32[2048]{0:T(1024)}, u32[]{:S(2)}) copy-start(s32[2048]{0:T(1024)} %param.8) | copy-start | bytes 24580
  57.5 15.8 %copy-start.1 = (f32[1024,2048]{1,0:T(8,128)}, f32[1024,2048]{1,0:T(8,128)S(1)}, u32[]{:S(2)}) copy-start(f32[1024,2048]{1,0:T(8,128)S(1)} %get-tuple-element.13) | copy-start | bytes 25165828
  57.5 3.7 collective-permute-start
  61.2 5.1 %collective-permute-start.1 = (f32[1024]{0:T(1024)S(1)}, f32[1024]{0:T(1024)S(1)}, u32[]{:S(2)}, u32[]{:S(2)}) collective-permute-start(f32[1024]{0:T(1024)S(1)} %add.75), channel_id=1, source_target_pairs={{0,16},{16,0},{32,48},{48,32},{64,80},{80,64},{96,112},{112,96},{1... | collective-permute-start | bytes 12296 | tf_op jit(solution)/shard_map/ppermute | solution.py:41
  66.3 5.1 %collective-permute-start.2 = (f32[1024]{0:T(1024)S(1)}, f32[1024]{0:T(1024)S(1)}, u32[]{:S(2)}, u32[]{:S(2)}) collective-permute-start(f32[1024]{0:T(1024)S(1)} %add.76), channel_id=1, source_target_pairs={{0,64},{16,80},{32,96},{48,112},{64,0},{80,16},{96,32},{112,48},{1... | collective-permute-start | bytes 12296 | tf_op jit(solution)/shard_map/ppermute | solution.py:41
  73.2 2.0 copy-start.2
  96.4 15.8 %all-to-all-start.1 = ((f32[8,128,256]{2,1,0:T(8,128)}), f32[8,128,256]{2,1,0:T(8,128)S(1)}, u32[]{:S(2)}, u32[]{:S(2)}) async-start(f32[8,128,256]{2,1,0:T(8,128)} %broadcast_in_dim.115), calls=%async_computation.1 | async-start | bytes 2097152 | tf_op jit(solution)/shard_map/all_to_all | solution.py:115
  100.0 83.9 %reduce-scatter.3.cloned.1.call-start = ((), (), s32[]{:S(2)}) async-start(), calls=%async_computation.9 | async-start | bytes 2367488 | tf_op jit(solution)/shard_map/reduce_scatter | solution.py:134
  117.6 99.4 %all-gather.6.cloned.1.call-start = ((), (), s32[]{:S(2)}) async-start(), calls=%async_computation.10 | async-start | bytes 1114112 | tf_op jit(solution)/shard_map/all_gather | solution.py:139
  222.2 29.4 %copy-start.4 = (f32[1,130,256]{2,1,0:T(8,128)S(1)}, f32[1,130,256]{2,1,0:T(8,128)}, u32[]{:S(2)}) copy-start(f32[1,130,256]{2,1,0:T(8,128)} %reduce-scatter.3.cloned.1.call-done) | copy-start | bytes 399364
  248.0 18.6 %all-to-all-start.3 = ((f32[8,128,256]{2,1,0:T(8,128)}), f32[8,128,256]{2,1,0:T(8,128)S(1)}, u32[]{:S(2)}, u32[]{:S(2)}) async-start(f32[8,128,256]{2,1,0:T(8,128)} %broadcast_in_dim.119), calls=%async_computation.4 | async-start | bytes 2097152 | tf_op jit(solution)/shard_map/all_to_all | solution.py:115
  251.6 87.7 %reduce-scatter.5.cloned.1.call-start = ((), (), s32[]{:S(2)}) async-start(), calls=%async_computation.11 | async-start | bytes 2367488 | tf_op jit(solution)/shard_map/reduce_scatter | solution.py:134
  276.0 96.5 %all-gather.8.cloned.1.call-start = ((), (), s32[]{:S(2)}) async-start(), calls=%async_computation.12 | async-start | bytes 1114112 | tf_op jit(solution)/shard_map/all_gather | solution.py:139
  372.5 3.8 copy-start.3
  402.5 18.6 %all-to-all-start.5 = ((f32[8,128,256]{2,1,0:T(8,128)}), f32[8,128,256]{2,1,0:T(8,128)S(1)}, u32[]{:S(2)}, u32[]{:S(2)}) async-start(f32[8,128,256]{2,1,0:T(8,128)} %broadcast_in_dim.123), calls=%async_computation.7 | async-start | bytes 2097152 | tf_op jit(solution)/shard_map/all_to_all | solution.py:115
Sparse Core Ops, SparseCore 0:
  9.7 39.8 all-gather.3
  117.7 66.1 reduce-scatter.2
  186.1 30.7 all-gather.5
  276.1 63.1 reduce-scatter.4
  341.7 30.8 all-gather.7

commit v7 on v4

--- a/solution.py
+++ b/solution.py
@@ -178,9 +178,13 @@
     anchor_level = jnp.take(pool_level, landmark_index, axis=0)
     row_factor = 1.0 / math.sqrt(feature_count) / level_values(row_level, level_scale)
     anchor_factor = 1.0 / level_values(anchor_level, level_scale)
-    raw = raw_block(gathered, row_factor, anchors, anchor_factor)
-    column_mean = butterfly_sum(jnp.sum(raw, axis=0), "sample", sample_bits) / n_rows
-    kernel = (raw - column_mean[None, :]).astype(jnp.bfloat16)
+    kernel_parts = []
+    half = anchors.shape[0] // 2
+    for h in range(2):
+        raw = raw_block(gathered, row_factor, anchors[h * half:(h + 1) * half], anchor_factor[h * half:(h + 1) * half])
+        column_mean = butterfly_sum(jnp.sum(raw, axis=0), "sample", sample_bits) / n_rows
+        kernel_parts.append((raw - column_mean[None, :]).astype(jnp.bfloat16))
+    kernel = jnp.concatenate(kernel_parts, axis=1)
     column_count = targets.shape[1]
     group_width = column_count // GROUPS
     results = [

time: 300 us -> 301 us (level)
  starting transfers between devices: 18.1 us -> 23 us
    concatenate x0 -> x1, other arithmetic: none -> 4.74 us  [on_device(): kernel = jnp.concatenate(kernel_parts, axis=1)]
    ppermute x3 -> x6, starting transfers between devices: 7.36 us -> 12.1 us  [butterfly_sum(): x = x + lax.ppermute(x, axis, perm)]
    sub x1, other arithmetic: 5.65 us -> 1.75 us  [on_device(): kernel_parts.append((raw - column_mean[None, :]).astype(jnp.bfloat16))]
    ppermute x3 -> x6, waiting for transfers between devices: 6.55 us -> 4.71 us  [butterfly_sum(): x = x + lax.ppermute(x, axis, perm)]
    dot_general x1 -> x2, matrix products: 7.88 us -> 8.26 us  [raw_block(): jnp.dot(summary_rows, anchors.T, preferred_element_type=jnp.float32)]
  transfers between devices with their start and end apart: 7 -> 10, of which waited for: 7 -> 7; matrix products, arithmetic and copies ran while one was open for 9% -> 9% of each run, Pallas kernels for 0% -> 0%
where the time goes in v7:
time: 301 us; the launch traced here: 300 us
  blocking collectives  144 us (48%)
  waiting for transfers between devices  60.3 us (20%)
  local copies, waits for them, and re-layouts  24.1 us (8%)
  starting transfers between devices  23 us (8%)
  matrix products  18.9 us (6%)
  other arithmetic  15.6 us (5%)
  between operations  14.5 us (5%)
    all_to_all x5, blocking collectives, exchange_scatter(): got = lax.all_to_all(chunks, axis, 0, 0, tiled=False)  106 us
    all_to_all x2, blocking collectives, exchange_gather(): lax.all_to_all(jnp.broadcast_to(part[None], (size,) + part.shape), axis,...  38.1 us
    all_to_all x3, waiting for transfers between devices, exchange_gather(): lax.all_to_all(jnp.broadcast_to(part[None], (size,) + part.shape), axis,...  29.3 us
    all_gather x1, waiting for transfers between devices, on_device(): gathered = lax.all_gather(summaries, 'landmark', axis=1, tiled=True)  25.6 us
    ppermute x6, starting transfers between devices, butterfly_sum(): x = x + lax.ppermute(x, axis, perm)  12.1 us
    all_to_all x3, starting transfers between devices, exchange_gather(): lax.all_to_all(jnp.broadcast_to(part[None], (size,) + part.shape), axis,...  10.9 us
    dot_general x2, matrix products, raw_block(): jnp.dot(summary_rows, anchors.T, preferred_element_type=jnp.float32)  8.26 us
    gather x1, local copies, waits for them, and re-layouts, on_device(): anchors = jnp.take(pool, landmark_index, axis=0)  7.72 us
  transfers between devices with their start and end apart: 10, of which 7 were waited for; matrix products, arithmetic and copies ran while one was open for 9% of the time, Pallas kernels for 0%

profile of v7, /device:TPU:0, one launch (start us, length us, event | category | flops | bytes accessed | tf_op | source)
XLA Modules:
  0.0 300.1 jit_solution(14925213668238172983)
XLA Ops:
  7.2 0.0 copy-start
  7.2 0.0 all-gather.2.cloned.1.call-start
  7.2 0.7 all-gather.2.cloned.1.call-update
  7.9 0.7 fusion.15
  8.6 5.7 %gather_fusion.1 = s32[1024]{0:T(1024)S(1)} fusion(s32[2048]{0:T(1024)} %param.10, s32[1024]{0:T(1024)S(1)} %fusion.15), kind=kCustom, calls=%fused_computation.1 | custom fusion | bytes 12288 | tf_op jit(solution)/shard_map/jit(_take)/gather | solution.py:178
  14.4 7.7 %gather_fusion = bf16[1024,1024]{1,0:T(8,128)(2,1)S(1)} fusion(bf16[2048,1024]{1,0:T(8,128)(2,1)} %param.9, s32[1024]{0:T(1024)S(1)} %fusion.15), kind=kCustom, calls=%fused_computation | custom fusion | bytes 4198400 | tf_op jit(solution)/shard_map/jit(_take)/gather | solution.py:177
  22.1 0.1 select_reduce_fusion.1
  22.2 0.1 select_reduce_fusion
  22.4 1.6 broadcast_select_fusion
  24.0 25.6 %all-gather.2.cloned.1.call-done = bf16[2048,1024]{0,1:T(8,128)(2,1)} async-done(((bf16[2048,64]{0,1:T(8,128)(2,1)}), bf16[2048,1024]{0,1:T(8,128)(2,1)}) %all-gather.2.cloned.1.call-update) | async-done | bytes 4194320 | tf_op jit(solution)/shard_map/all_gather | solution.py:175
  49.6 5.0 %fusion.4 = f32[512,2048]{1,0:T(8,128)S(1)} fusion(bf16[2048,1024]{0,1:T(8,128)(2,1)} %all-gather.2.cloned.1.call-done, bf16[1024,1024]{1,0:T(8,128)(2,1)} %broadcast_select_fusion), kind=kOutput, calls=%fused_computation.22 | convolution fusion | flops 2147483648 | bytes 9437184 | tf_op jit(solution)/shard_map/dot_general | solution.py:27
  54.6 3.3 %fusion = (f32[512]{0:T(512)S(1)}, f32[512]{0:T(512)S(1)}, f32[512,2048]{1,0:T(8,128)S(1)}) fusion(f32[512]{0:T(512)S(1)} %get-tuple-element.17, f32[2048]{0:T(1024)S(1)} %broadcast_divide_fusion, f32[512]{0:T(512)S(1)} %get-tuple-element.16, f32[512,2048]{1,0:T(8,128)S(1)} %fusion.4, bf16[2048,1024]{0,1:T(8,128)(2,1)S(1)} %copy-done.10, ...), kind=kOutput, calls=%fused_computation.7 | convolution fusion | flops 2153774080 | bytes 13647872 | tf_op jit(solution)/shard_map/dot_general | solution.py:27
  57.9 1.5 collective-permute-start
  59.4 0.6 collective-permute-start.3
  60.0 1.6 collective-permute-done
  61.5 2.8 collective-permute-start.1
  64.3 1.4 collective-permute-start.4
  65.7 0.9 collective-permute-done.1
  66.6 3.0 collective-permute-start.2
  69.6 2.8 collective-permute-start.5
  72.4 2.3 collective-permute-done.5
  74.7 1.8 fusion.2
  76.5 1.3 fusion.27
  77.8 0.0 copy-done.4
  77.8 0.6 copy-done.5
  78.4 18.1 %all_to_all.50 = f32[8,128,256]{2,1,0:T(8,128)S(1)} all-to-all(f32[8,128,256]{2,1,0:T(8,128)S(1)} %bitcast.78), channel_id=1, replica_groups=mesh['sample'=8,'landmark'=16] {'sample'}, dimensions={0} | all-to-all | bytes 2097152 | tf_op jit(solution)/shard_map/all_to_all | solution.py:105
  96.6 0.1 reduce_sum.134
  96.7 1.1 broadcast_in_dim.76
  97.7 3.7 %all-to-all-start.1 = ((f32[8,128,256]{2,1,0:T(8,128)}), f32[8,128,256]{2,1,0:T(8,128)S(1)}, u32[]{:S(2)}, u32[]{:S(2)}) async-start(f32[8,128,256]{2,1,0:T(8,128)} %broadcast_in_dim.76), calls=%async_computation.1 | async-start | bytes 2097152 | tf_op jit(solution)/shard_map/all_to_all | solution.py:115
  101.5 4.7 %pad_maximum_fusion = bf16[2048,1024]{0,1:T(8,128)(2,1)} fusion(bf16[2048,512]{0,1:T(8,128)(2,1)} %copy-done.5, bf16[2048,512]{0,1:T(8,128)(2,1)} %copy-done.4), kind=kLoop, calls=%fused_computation.2 | loop fusion | flops 8388608 | bytes 8388608 | tf_op jit(solution)/shard_map/concatenate | solution.py:187
  106.2 6.4 %copy.15 = bf16[2048,1024]{1,0:T(8,128)(2,1)} copy(bf16[2048,1024]{0,1:T(8,128)(2,1)} %pad_maximum_fusion) | data formatting | bytes 8388608 | tf_op jit(solution)/shard_map/dot_general | solution.py:136
  112.6 0.9 all-to-all-done.1
  113.5 0.2 multiply_convert_fusion
  113.8 3.4 %convolution_convert_fusion.1 = bf16[16,128,256]{2,1,0:T(8,128)(2,1)S(1)} fusion(bf16[16,128,1024]{2,1,0:T(8,128)(2,1)} %bitcast.74, bf16[1024,256,1]{1,0,2:T(8,128)(2,1)S(1)} %bitcast.79), kind=kOutput, calls=%fused_computation.17 | convolution fusion | flops 1074266112 | bytes 5767168 | tf_op jit(solution)/shard_map/dot_general | solution.py:136
  117.3 0.1 pad_maximum_fusion.1
  117.4 20.8 %all_to_all.51 = bf16[16,134,256]{2,1,0:T(8,128)(2,1)S(1)} all-to-all(bf16[16,134,256]{2,1,0:T(8,128)(2,1)S(1)} %pad_maximum_fusion.1), channel_id=1, replica_groups=mesh['sample'=8,'landmark'=16] {'landmark'}, dimensions={0} | all-to-all | bytes 2195456 | tf_op jit(solution)/shard_map/all_to_all | solution.py:105
  138.2 0.2 convert_reduce_fusion.1
  138.3 0.1 broadcast_in_dim.78
  138.4 19.1 %all_to_all.52 = bf16[16,128,256]{2,1,0:T(8,128)(2,1)S(1)} all-to-all(bf16[16,128,256]{2,1,0:T(8,128)(2,1)S(1)} %broadcast_in_dim.78), channel_id=1, replica_groups=mesh['sample'=8,'landmark'=16] {'landmark'}, dimensions={0} | all-to-all | bytes 2097152 | tf_op jit(solution)/shard_map/all_to_all | solution.py:115
  157.5 1.3 fusion.29
  158.8 0.3 multiply_reduce_fusion.1
  159.1 0.1 pad_maximum_fusion.2
  159.2 23.8 %all_to_all.53 = f32[8,129,256]{2,1,0:T(8,128)S(1)} all-to-all(f32[8,129,256]{2,1,0:T(8,128)S(1)} %pad_maximum_fusion.2), channel_id=1, replica_groups=mesh['sample'=8,'landmark'=16] {'sample'}, dimensions={0} | all-to-all | bytes 2113536 | tf_op jit(solution)/shard_map/all_to_all | solution.py:105
  183.0 0.1 reduce_sum.138
  183.1 1.1 broadcast_in_dim.80
  184.1 3.6 %all-to-all-start.5 = ((f32[8,128,256]{2,1,0:T(8,128)}), f32[8,128,256]{2,1,0:T(8,128)S(1)}, u32[]{:S(2)}, u32[]{:S(2)}) async-start(f32[8,128,256]{2,1,0:T(8,128)} %broadcast_in_dim.80), calls=%async_computation.5 | async-start | bytes 2097152 | tf_op jit(solution)/shard_map/all_to_all | solution.py:115
  187.7 14.2 %all-to-all-done.5 = f32[8,128,256]{2,1,0:T(8,128)S(1)} async-done(((f32[8,128,256]{2,1,0:T(8,128)}), f32[8,128,256]{2,1,0:T(8,128)S(1)}, u32[]{:S(2)}, u32[]{:S(2)}) %all-to-all-start.5) | async-done | bytes 1048608 | tf_op jit(solution)/shard_map/all_to_all | solution.py:115
  201.9 1.4 multiply_reduce_fusion.3
  203.3 3.4 %convolution_convert_fusion = bf16[16,128,256]{2,1,0:T(8,128)(2,1)S(1)} fusion(bf16[16,128,1024]{2,1,0:T(8,128)(2,1)} %bitcast.75, bf16[1024,256,1]{1,0,2:T(8,128)(2,1)S(1)} %bitcast.80), kind=kOutput, calls=%fused_computation.16 | convolution fusion | flops 1074266112 | bytes 5767168 | tf_op jit(solution)/shard_map/dot_general | solution.py:144
  206.9 0.1 pad_maximum_fusion.3
  207.0 21.0 %all_to_all.54 = bf16[16,134,256]{2,1,0:T(8,128)(2,1)S(1)} all-to-all(bf16[16,134,256]{2,1,0:T(8,128)(2,1)S(1)} %pad_maximum_fusion.3), channel_id=1, replica_groups=mesh['sample'=8,'landmark'=16] {'landmark'}, dimensions={0} | all-to-all | bytes 2195456 | tf_op jit(solution)/shard_map/all_to_all | solution.py:105
  227.9 0.2 convert_reduce_fusion
  228.2 0.1 broadcast_in_dim.82
  228.3 19.1 %all_to_all.55 = bf16[16,128,256]{2,1,0:T(8,128)(2,1)S(1)} all-to-all(bf16[16,128,256]{2,1,0:T(8,128)(2,1)S(1)} %broadcast_in_dim.82), channel_id=1, replica_groups=mesh['sample'=8,'landmark'=16] {'landmark'}, dimensions={0} | all-to-all | bytes 2097152 | tf_op jit(solution)/shard_map/all_to_all | solution.py:115
  247.3 1.3 fusion.30
  248.6 0.3 multiply_reduce_fusion
  248.9 0.1 pad_maximum_fusion.4
  249.0 21.9 %all_to_all.56 = f32[8,129,256]{2,1,0:T(8,128)S(1)} all-to-all(f32[8,129,256]{2,1,0:T(8,128)S(1)} %pad_maximum_fusion.4), channel_id=1, replica_groups=mesh['sample'=8,'landmark'=16] {'sample'}, dimensions={0} | all-to-all | bytes 2113536 | tf_op jit(solution)/shard_map/all_to_all | solution.py:105
  270.9 0.1 reduce_sum.143
  271.0 1.1 broadcast_in_dim.84
  272.1 3.6 %all-to-all-start.9 = ((f32[8,128,256]{2,1,0:T(8,128)}), f32[8,128,256]{2,1,0:T(8,128)S(1)}, u32[]{:S(2)}, u32[]{:S(2)}) async-start(f32[8,128,256]{2,1,0:T(8,128)} %broadcast_in_dim.84), calls=%async_computation.9 | async-start | bytes 2097152 | tf_op jit(solution)/shard_map/all_to_all | solution.py:115
  275.7 14.2 %all-to-all-done.9 = f32[8,128,256]{2,1,0:T(8,128)S(1)} async-done(((f32[8,128,256]{2,1,0:T(8,128)}), f32[8,128,256]{2,1,0:T(8,128)S(1)}, u32[]{:S(2)}, u32[]{:S(2)}) %all-to-all-start.9) | async-done | bytes 1048608 | tf_op jit(solution)/shard_map/all_to_all | solution.py:115
  289.9 0.1 broadcast_multiply_fusion
  290.0 3.2 %fusion.9 = (f32[1024,256]{1,0:T(8,128)}, f32[1024,256]{1,0:T(8,128)}) fusion(f32[8,128,256]{2,1,0:T(8,128)S(1)} %broadcast_multiply_fusion, f32[256]{0:T(256)S(1)} %broadcast_multiply_fusion.2, f32[8,128,256]{2,1,0:T(8,128)S(1)} %all-to-all-done.1, f32[8,128,256]{2,1,0:T(8,128)} %get-tuple-element.11, f32[256]{0:T(256)S(1)} %bitcast.85, ...), kind=kLoop, calls=%fused_computation.28 | loop fusion | flops 3670016 | bytes 5246976 | tf_op jit(solution)/shard_map/sub | solution.py:166
  (55 shorter events, 0.3 us)
Async XLA Ops:
  7.2 69.3 %copy-start = (bf16[2048,256]{1,0:T(8,128)(2,1)S(1)}, bf16[2048,256]{1,0:T(8,128)(2,1)}, u32[]{:S(2)}) copy-start(bf16[2048,256]{1,0:T(8,128)(2,1)} %param.13) | copy-start | bytes 3145732
  7.2 42.4 %all-gather.2.cloned.1.call-start = ((), (), s32[]{:S(2)}) async-start(), calls=%async_computation.10 | async-start | bytes 4456448 | tf_op jit(solution)/shard_map/all_gather | solution.py:175
  14.3 7.8 %copy-start.7 = (s32[1024]{0:T(1024)S(1)}, s32[1024]{0:T(1024)}, u32[]{:S(2)}) copy-start(s32[1024]{0:T(1024)} %param.11) | copy-start | bytes 12292
  14.4 7.8 %copy-start.9 = (f32[4]{0:T(128)S(1)}, f32[4]{0:T(128)}, u32[]{:S(2)}) copy-start(f32[4]{0:T(128)} %param.12) | copy-start | bytes 52
  14.4 7.9 %copy-start.8 = (s32[2048]{0:T(1024)S(1)}, s32[2048]{0:T(1024)}, u32[]{:S(2)}) copy-start(s32[2048]{0:T(1024)} %param.8) | copy-start | bytes 24580
  24.0 30.6 %copy-start.6 = (bf16[1024,1024]{1,0:T(8,128)(2,1)S(1)}, bf16[1024,1024]{1,0:T(8,128)(2,1)}, u32[]{:S(2)}) copy-start(bf16[1024,1024]{1,0:T(8,128)(2,1)} %broadcast_select_fusion) | copy-start | bytes 6291460
  49.6 5.0 %copy-start.10 = (bf16[2048,1024]{0,1:T(8,128)(2,1)S(1)}, bf16[2048,1024]{0,1:T(8,128)(2,1)}, u32[]{:S(2)}) copy-start(bf16[2048,1024]{0,1:T(8,128)(2,1)} %all-gather.2.cloned.1.call-done) | copy-start | bytes 12582916
  57.9 3.7 %collective-permute-start = (f32[512]{0:T(512)S(1)}, f32[512]{0:T(512)S(1)}, u32[]{:S(2)}, u32[]{:S(2)}) collective-permute-start(f32[512]{0:T(512)S(1)} %get-tuple-element.4), channel_id=1, source_target_pairs={{0,32},{16,48},{32,0},{48,16},{64,96},{80,112},{96,64},{112,80},{1... | collective-permute-start | bytes 6152 | tf_op jit(solution)/shard_map/ppermute | solution.py:41
  59.4 4.9 %collective-permute-start.3 = (f32[512]{0:T(512)S(1)}, f32[512]{0:T(512)S(1)}, u32[]{:S(2)}, u32[]{:S(2)}) collective-permute-start(f32[512]{0:T(512)S(1)} %get-tuple-element.5), channel_id=1, source_target_pairs={{0,32},{16,48},{32,0},{48,16},{64,96},{80,112},{96,64},{112,80},{1... | collective-permute-start | bytes 6152 | tf_op jit(solution)/shard_map/ppermute | solution.py:41
  61.5 5.1 %collective-permute-start.1 = (f32[512]{0:T(512)S(1)}, f32[512]{0:T(512)S(1)}, u32[]{:S(2)}, u32[]{:S(2)}) collective-permute-start(f32[512]{0:T(512)S(1)} %add.80), channel_id=1, source_target_pairs={{0,16},{16,0},{32,48},{48,32},{64,80},{80,64},{96,112},{112,96},{1... | collective-permute-start | bytes 6152 | tf_op jit(solution)/shard_map/ppermute | solution.py:41
  64.3 5.3 %collective-permute-start.4 = (f32[512]{0:T(512)S(1)}, f32[512]{0:T(512)S(1)}, u32[]{:S(2)}, u32[]{:S(2)}) collective-permute-start(f32[512]{0:T(512)S(1)} %add.83), channel_id=1, source_target_pairs={{0,16},{16,0},{32,48},{48,32},{64,80},{80,64},{96,112},{112,96},{1... | collective-permute-start | bytes 6152 | tf_op jit(solution)/shard_map/ppermute | solution.py:41
  66.6 5.8 %collective-permute-start.2 = (f32[512]{0:T(512)S(1)}, f32[512]{0:T(512)S(1)}, u32[]{:S(2)}, u32[]{:S(2)}) collective-permute-start(f32[512]{0:T(512)S(1)} %add.81), channel_id=1, source_target_pairs={{0,64},{16,80},{32,96},{48,112},{64,0},{80,16},{96,32},{112,48},{1... | collective-permute-start | bytes 6152 | tf_op jit(solution)/shard_map/ppermute | solution.py:41
  69.6 5.1 %collective-permute-start.5 = (f32[512]{0:T(512)S(1)}, f32[512]{0:T(512)S(1)}, u32[]{:S(2)}, u32[]{:S(2)}) collective-permute-start(f32[512]{0:T(512)S(1)} %add.84), channel_id=1, source_target_pairs={{0,64},{16,80},{32,96},{48,112},{64,0},{80,16},{96,32},{112,48},{1... | collective-permute-start | bytes 6152 | tf_op jit(solution)/shard_map/ppermute | solution.py:41
  76.5 1.3 copy-start.4
  76.5 2.0 copy-start.5
  97.7 15.8 %all-to-all-start.1 = ((f32[8,128,256]{2,1,0:T(8,128)}), f32[8,128,256]{2,1,0:T(8,128)S(1)}, u32[]{:S(2)}, u32[]{:S(2)}) async-start(f32[8,128,256]{2,1,0:T(8,128)} %broadcast_in_dim.76), calls=%async_computation.1 | async-start | bytes 2097152 | tf_op jit(solution)/shard_map/all_to_all | solution.py:115
  117.3 40.2 %copy-start.2 = (bf16[2048,1024]{0,1:T(8,128)(2,1)S(1)}, bf16[2048,1024]{0,1:T(8,128)(2,1)}, u32[]{:S(2)}) copy-start(bf16[2048,1024]{0,1:T(8,128)(2,1)} %pad_maximum_fusion) | copy-start | bytes 12582916
  184.1 17.8 %all-to-all-start.5 = ((f32[8,128,256]{2,1,0:T(8,128)}), f32[8,128,256]{2,1,0:T(8,128)S(1)}, u32[]{:S(2)}, u32[]{:S(2)}) async-start(f32[8,128,256]{2,1,0:T(8,128)} %broadcast_in_dim.80), calls=%async_computation.5 | async-start | bytes 2097152 | tf_op jit(solution)/shard_map/all_to_all | solution.py:115
  206.9 40.5 %copy-start.3 = (bf16[2048,1024]{0,1:T(8,128)(2,1)S(1)}, bf16[2048,1024]{0,1:T(8,128)(2,1)}, u32[]{:S(2)}) copy-start(bf16[2048,1024]{0,1:T(8,128)(2,1)} %pad_maximum_fusion) | copy-start | bytes 12582916
  272.1 17.8 %all-to-all-start.9 = ((f32[8,128,256]{2,1,0:T(8,128)}), f32[8,128,256]{2,1,0:T(8,128)S(1)}, u32[]{:S(2)}, u32[]{:S(2)}) async-start(f32[8,128,256]{2,1,0:T(8,128)} %broadcast_in_dim.84), calls=%async_computation.9 | async-start | bytes 2097152 | tf_op jit(solution)/shard_map/all_to_all | solution.py:115
  275.6 17.6 %copy-start.1 = (bf16[2048,256]{1,0:T(8,128)(2,1)S(1)}, bf16[2048,256]{1,0:T(8,128)(2,1)}, u32[]{:S(2)}) copy-start(bf16[2048,256]{1,0:T(8,128)(2,1)} %param.13) | copy-start | bytes 3145732
Sparse Core Ops, SparseCore 0:
  9.7 39.8 all-gather.1

commit v8 on v4

--- a/solution.py
+++ b/solution.py
@@ -167,6 +167,21 @@
     return weights, residual
 
 
+def gather_sum(x, axis):
+    size = lax.axis_size(axis)
+    index = lax.axis_index(axis)
+    copies = [x] + [
+        lax.ppermute(x, axis, [(i, (i + shift) % size) for i in range(size)])
+        for shift in range(1, size)
+    ]
+    stacked = jnp.stack(copies)
+    ordered = jnp.take(stacked, (index - jnp.arange(size)) % size, axis=0)
+    total = ordered[0]
+    for j in range(1, size):
+        total = total + ordered[j]
+    return total
+
+
 def on_device(summaries, row_level, pool, pool_level, landmark_index, level_scale, targets):
     sample_bits = partner_bits(lax.axis_size("sample"), (2, 1, 4, 8, 16, 32, 64))
     landmark_bits = partner_bits(lax.axis_size("landmark"), (1, 2, 4, 8, 16, 32, 64))
@@ -179,7 +194,7 @@
     row_factor = 1.0 / math.sqrt(feature_count) / level_values(row_level, level_scale)
     anchor_factor = 1.0 / level_values(anchor_level, level_scale)
     raw = raw_block(gathered, row_factor, anchors, anchor_factor)
-    column_mean = butterfly_sum(jnp.sum(raw, axis=0), "sample", sample_bits) / n_rows
+    column_mean = gather_sum(jnp.sum(raw, axis=0), "sample") / n_rows
     kernel = (raw - column_mean[None, :]).astype(jnp.bfloat16)
     column_count = targets.shape[1]
     group_width = column_count // GROUPS

time: 300 us -> 310 us (1.033)
  starting transfers between devices: 18.1 us -> 24.7 us
    ppermute x3 -> x7, starting transfers between devices: 7.36 us -> 13.9 us  [gather_sum(): lax.ppermute(x, axis, [(i, (i + shift) % size) for i in range(size)])]
    ppermute x3 -> x7, waiting for transfers between devices: 6.55 us -> 5.57 us  [gather_sum(): lax.ppermute(x, axis, [(i, (i + shift) % size) for i in range(size)])]
  transfers between devices with their start and end apart: 7 -> 11, of which waited for: 7 -> 6; matrix products, arithmetic and copies ran while one was open for 9% -> 9% of each run, Pallas kernels for 0% -> 0%
where the time goes in v8:
time: 310 us; the launch traced here: 309 us
  blocking collectives  144 us (46%)
  waiting for transfers between devices  62.5 us (20%)
  local copies, waits for them, and re-layouts  25.9 us (8%)
  starting transfers between devices  24.7 us (8%)
  matrix products  20.3 us (7%)
  other arithmetic  17.5 us (6%)
  between operations  14.4 us (5%)
    all_to_all x5, blocking collectives, exchange_scatter(): got = lax.all_to_all(chunks, axis, 0, 0, tiled=False)  106 us
    all_to_all x2, blocking collectives, exchange_gather(): lax.all_to_all(jnp.broadcast_to(part[None], (size,) + part.shape), axis,...  38.1 us
    all_to_all x3, waiting for transfers between devices, exchange_gather(): lax.all_to_all(jnp.broadcast_to(part[None], (size,) + part.shape), axis,...  29 us
    all_gather x1, waiting for transfers between devices, on_device(): gathered = lax.all_gather(summaries, 'landmark', axis=1, tiled=True)  27.2 us
    ppermute x7, starting transfers between devices, gather_sum(): lax.ppermute(x, axis, [(i, (i + shift) % size) for i in range(size)])  13.9 us
    all_to_all x3, starting transfers between devices, exchange_gather(): lax.all_to_all(jnp.broadcast_to(part[None], (size,) + part.shape), axis,...  10.9 us
    dot_general x1, matrix products, raw_block(): jnp.dot(summary_rows, anchors.T, preferred_element_type=jnp.float32)  9.64 us
    gather x1, local copies, waits for them, and re-layouts, on_device(): anchors = jnp.take(pool, landmark_index, axis=0)  7.72 us
  transfers between devices with their start and end apart: 11, of which 6 were waited for; matrix products, arithmetic and copies ran while one was open for 9% of the time, Pallas kernels for 0%

profile of v8, /device:TPU:0, one launch (start us, length us, event | category | flops | bytes accessed | tf_op | source)
XLA Modules:
  0.0 309.3 jit_solution(2836302127939180047)
XLA Ops:
  7.2 0.0 copy-start
  7.2 0.0 all-gather.2.cloned.1.call-start
  7.2 0.7 all-gather.2.cloned.1.call-update
  7.9 0.7 fusion.13
  8.6 5.7 %gather_fusion.1 = s32[1024]{0:T(1024)S(1)} fusion(s32[2048]{0:T(1024)} %param.10, s32[1024]{0:T(1024)S(1)} %fusion.13), kind=kCustom, calls=%fused_computation.1 | custom fusion | bytes 12288 | tf_op jit(solution)/shard_map/jit(_take)/gather | solution.py:193
  14.4 7.7 %gather_fusion = bf16[1024,1024]{1,0:T(8,128)(2,1)S(1)} fusion(bf16[2048,1024]{1,0:T(8,128)(2,1)} %param.9, s32[1024]{0:T(1024)S(1)} %fusion.13), kind=kCustom, calls=%fused_computation | custom fusion | bytes 4198400 | tf_op jit(solution)/shard_map/jit(_take)/gather | solution.py:192
  22.2 0.1 select_reduce_fusion.1
  22.3 0.1 select_reduce_fusion
  22.4 27.2 %all-gather.2.cloned.1.call-done = bf16[2048,1024]{0,1:T(8,128)(2,1)} async-done(((bf16[2048,64]{0,1:T(8,128)(2,1)}), bf16[2048,1024]{0,1:T(8,128)(2,1)}) %all-gather.2.cloned.1.call-update) | async-done | bytes 4194320 | tf_op jit(solution)/shard_map/all_gather | solution.py:190
  49.6 9.6 %fusion = (f32[1024]{0:T(1024)S(1)}, f32[1024,2048]{1,0:T(8,128)}) fusion(f32[1024]{0:T(1024)S(1)} %broadcast_divide_fusion.1, f32[2048]{0:T(1024)S(1)} %broadcast_divide_fusion, bf16[2048,1024]{0,1:T(8,128)(2,1)} %all-gather.2.cloned.1.call-done, bf16[1024,1024]{1,0:T(8,128)(2,1)S(1)} %gather_fusion, pred[1024]{0:T(1024)(128)(4,1)S(1)} %get-tuple-element.5), kind=kOutput, calls=%fused_computation.5 | convolution fusion | flops 4302306304 | bytes 14697472 | tf_op jit(solution)/shard_map/dot_general | solution.py:27
  59.2 4.9 %collective-permute-start.6 = (f32[1024]{0:T(1024)S(1)}, f32[1024]{0:T(1024)S(1)}, u32[]{:S(2)}, u32[]{:S(2)}) collective-permute-start(f32[1024]{0:T(1024)S(1)} %get-tuple-element.18), channel_id=1, source_target_pairs={{0,112},{16,0},{32,16},{48,32},{64,48},{80,64},{96,80},{112,96},{1... | collective-permute-start | bytes 12296 | tf_op jit(solution)/shard_map/ppermute | solution.py:174
  64.1 0.9 collective-permute-start.5
  65.0 0.7 collective-permute-start.4
  65.7 2.7 collective-permute-start.3
  68.4 1.1 collective-permute-start.2
  69.4 2.0 collective-permute-start.1
  71.5 1.6 collective-permute-start
  73.1 2.8 collective-permute-done.2
  75.9 2.8 collective-permute-done
  78.7 0.1 stack.35
  78.7 0.6 gather_fusion.2
  79.3 0.1 broadcast_select_fusion
  79.4 4.3 %subtract_convert_fusion = bf16[1024,2048]{1,0:T(8,128)(2,1)S(1)} fusion(f32[1024,2048]{1,0:T(8,128)} %get-tuple-element.19, f32[1024]{0:T(1024)S(1)} %bitcast.88, f32[1024]{0:T(1024)S(1)} %broadcast_divide_fusion.1, f32[2048]{0:T(1024)S(1)} %broadcast_divide_fusion), kind=kLoop, calls=%fused_computation.3 | loop fusion | flops 8388608 | bytes 12599296 | tf_op jit(solution)/shard_map/convert.6
  83.8 2.0 copy-done.1
  85.7 1.3 fusion.29
  87.0 18.2 %all_to_all.50 = f32[8,128,256]{2,1,0:T(8,128)S(1)} all-to-all(f32[8,128,256]{2,1,0:T(8,128)S(1)} %bitcast.85), channel_id=1, replica_groups=mesh['sample'=8,'landmark'=16] {'sample'}, dimensions={0} | all-to-all | bytes 2097152 | tf_op jit(solution)/shard_map/all_to_all | solution.py:105
  105.2 0.1 reduce_sum.124
  105.2 1.1 broadcast_in_dim.88
  106.3 3.7 %all-to-all-start.1 = ((f32[8,128,256]{2,1,0:T(8,128)}), f32[8,128,256]{2,1,0:T(8,128)S(1)}, u32[]{:S(2)}, u32[]{:S(2)}) async-start(f32[8,128,256]{2,1,0:T(8,128)} %broadcast_in_dim.88), calls=%async_computation.1 | async-start | bytes 2097152 | tf_op jit(solution)/shard_map/all_to_all | solution.py:115
  110.0 5.6 %fusion.43 = bf16[2048,1024]{0,1:T(8,128)(2,1)} fusion(f32[1024]{0:T(1024)S(1)} %bitcast.89, f32[1024]{0:T(1024)S(1)} %broadcast_divide_fusion.1, f32[1024,2048]{1,0:T(8,128)} %get-tuple-element.19, f32[2048]{0:T(1024)S(1)} %broadcast_divide_fusion), kind=kLoop, calls=%fused_computation.111 | loop fusion | flops 8388608 | bytes 12599296 | tf_op jit(solution)/shard_map/sub | solution.py:198
  115.7 6.4 %copy.15 = bf16[2048,1024]{1,0:T(8,128)(2,1)} copy(bf16[2048,1024]{0,1:T(8,128)(2,1)} %fusion.43) | data formatting | bytes 8388608 | tf_op jit(solution)/shard_map/dot_general | solution.py:136
  122.1 0.6 all-to-all-done.1
  122.7 0.2 multiply_convert_fusion
  123.0 3.4 %convolution_convert_fusion.1 = bf16[16,128,256]{2,1,0:T(8,128)(2,1)S(1)} fusion(bf16[16,128,1024]{2,1,0:T(8,128)(2,1)} %bitcast.81, bf16[1024,256,1]{1,0,2:T(8,128)(2,1)S(1)} %bitcast.86), kind=kOutput, calls=%fused_computation.14 | convolution fusion | flops 1074266112 | bytes 5767168 | tf_op jit(solution)/shard_map/dot_general | solution.py:136
  126.4 0.1 pad_maximum_fusion
  126.5 20.8 %all_to_all.51 = bf16[16,134,256]{2,1,0:T(8,128)(2,1)S(1)} all-to-all(bf16[16,134,256]{2,1,0:T(8,128)(2,1)S(1)} %pad_maximum_fusion), channel_id=1, replica_groups=mesh['sample'=8,'landmark'=16] {'landmark'}, dimensions={0} | all-to-all | bytes 2195456 | tf_op jit(solution)/shard_map/all_to_all | solution.py:105
  147.3 0.2 convert_reduce_fusion.1
  147.5 0.1 broadcast_in_dim.139
  147.6 19.1 %all_to_all.52 = bf16[16,128,256]{2,1,0:T(8,128)(2,1)S(1)} all-to-all(bf16[16,128,256]{2,1,0:T(8,128)(2,1)S(1)} %broadcast_in_dim.139), channel_id=1, replica_groups=mesh['sample'=8,'landmark'=16] {'landmark'}, dimensions={0} | all-to-all | bytes 2097152 | tf_op jit(solution)/shard_map/all_to_all | solution.py:115
  166.6 1.3 fusion.30
  167.9 0.3 multiply_reduce_fusion.1
  168.2 0.1 pad_maximum_fusion.1
  168.3 24.0 %all_to_all.53 = f32[8,129,256]{2,1,0:T(8,128)S(1)} all-to-all(f32[8,129,256]{2,1,0:T(8,128)S(1)} %pad_maximum_fusion.1), channel_id=1, replica_groups=mesh['sample'=8,'landmark'=16] {'sample'}, dimensions={0} | all-to-all | bytes 2113536 | tf_op jit(solution)/shard_map/all_to_all | solution.py:105
  192.3 0.1 reduce_sum.128
  192.4 1.1 broadcast_in_dim.141
  193.5 3.6 %all-to-all-start.5 = ((f32[8,128,256]{2,1,0:T(8,128)}), f32[8,128,256]{2,1,0:T(8,128)S(1)}, u32[]{:S(2)}, u32[]{:S(2)}) async-start(f32[8,128,256]{2,1,0:T(8,128)} %broadcast_in_dim.141), calls=%async_computation.5 | async-start | bytes 2097152 | tf_op jit(solution)/shard_map/all_to_all | solution.py:115
  197.1 14.2 %all-to-all-done.5 = f32[8,128,256]{2,1,0:T(8,128)S(1)} async-done(((f32[8,128,256]{2,1,0:T(8,128)}), f32[8,128,256]{2,1,0:T(8,128)S(1)}, u32[]{:S(2)}, u32[]{:S(2)}) %all-to-all-start.5) | async-done | bytes 1048608 | tf_op jit(solution)/shard_map/all_to_all | solution.py:115
  211.3 1.3 multiply_reduce_fusion.3
  212.6 3.4 %convolution_convert_fusion = bf16[16,128,256]{2,1,0:T(8,128)(2,1)S(1)} fusion(bf16[16,128,1024]{2,1,0:T(8,128)(2,1)} %bitcast.82, bf16[1024,256,1]{1,0,2:T(8,128)(2,1)S(1)} %bitcast.87), kind=kOutput, calls=%fused_computation.13 | convolution fusion | flops 1074266112 | bytes 5767168 | tf_op jit(solution)/shard_map/dot_general | solution.py:144
  216.2 0.1 pad_maximum_fusion.2
  216.2 21.0 %all_to_all.54 = bf16[16,134,256]{2,1,0:T(8,128)(2,1)S(1)} all-to-all(bf16[16,134,256]{2,1,0:T(8,128)(2,1)S(1)} %pad_maximum_fusion.2), channel_id=1, replica_groups=mesh['sample'=8,'landmark'=16] {'landmark'}, dimensions={0} | all-to-all | bytes 2195456 | tf_op jit(solution)/shard_map/all_to_all | solution.py:105
  237.2 0.2 convert_reduce_fusion
  237.4 0.1 broadcast_in_dim.143
  237.5 19.1 %all_to_all.55 = bf16[16,128,256]{2,1,0:T(8,128)(2,1)S(1)} all-to-all(bf16[16,128,256]{2,1,0:T(8,128)(2,1)S(1)} %broadcast_in_dim.143), channel_id=1, replica_groups=mesh['sample'=8,'landmark'=16] {'landmark'}, dimensions={0} | all-to-all | bytes 2097152 | tf_op jit(solution)/shard_map/all_to_all | solution.py:115
  256.6 1.3 fusion.31
  257.9 0.3 multiply_reduce_fusion
  258.2 0.1 pad_maximum_fusion.3
  258.3 21.9 %all_to_all.56 = f32[8,129,256]{2,1,0:T(8,128)S(1)} all-to-all(f32[8,129,256]{2,1,0:T(8,128)S(1)} %pad_maximum_fusion.3), channel_id=1, replica_groups=mesh['sample'=8,'landmark'=16] {'sample'}, dimensions={0} | all-to-all | bytes 2113536 | tf_op jit(solution)/shard_map/all_to_all | solution.py:105
  280.2 0.1 reduce_sum.133
  280.3 1.1 broadcast_in_dim.145
  281.3 3.6 %all-to-all-start.9 = ((f32[8,128,256]{2,1,0:T(8,128)}), f32[8,128,256]{2,1,0:T(8,128)S(1)}, u32[]{:S(2)}, u32[]{:S(2)}) async-start(f32[8,128,256]{2,1,0:T(8,128)} %broadcast_in_dim.145), calls=%async_computation.9 | async-start | bytes 2097152 | tf_op jit(solution)/shard_map/all_to_all | solution.py:115
  284.9 14.2 %all-to-all-done.9 = f32[8,128,256]{2,1,0:T(8,128)S(1)} async-done(((f32[8,128,256]{2,1,0:T(8,128)}), f32[8,128,256]{2,1,0:T(8,128)S(1)}, u32[]{:S(2)}, u32[]{:S(2)}) %all-to-all-start.9) | async-done | bytes 1048608 | tf_op jit(solution)/shard_map/all_to_all | solution.py:115
  299.1 0.1 broadcast_multiply_fusion
  299.2 3.2 %fusion.5 = (f32[1024,256]{1,0:T(8,128)}, f32[1024,256]{1,0:T(8,128)}) fusion(f32[8,128,256]{2,1,0:T(8,128)S(1)} %broadcast_multiply_fusion, f32[256]{0:T(256)S(1)} %broadcast_multiply_fusion.2, f32[8,128,256]{2,1,0:T(8,128)S(1)} %all-to-all-done.1, f32[8,128,256]{2,1,0:T(8,128)} %get-tuple-element.9, f32[256]{0:T(256)S(1)} %bitcast.94, f32[256]{0:T(256)S(1)} %bitcast.95, ...), kind=kLoop, calls=%fused_computation.21 | loop fusion | flops 3670016 | bytes 5246976 | tf_op jit(solution)/shard_map/sub | solution.py:166
  (47 shorter events, 0.4 us)
Async XLA Ops:
  7.2 78.6 %copy-start = (bf16[2048,256]{1,0:T(8,128)(2,1)S(1)}, bf16[2048,256]{1,0:T(8,128)(2,1)}, u32[]{:S(2)}) copy-start(bf16[2048,256]{1,0:T(8,128)(2,1)} %param.13) | copy-start | bytes 3145732
  7.2 42.4 %all-gather.2.cloned.1.call-start = ((), (), s32[]{:S(2)}) async-start(), calls=%async_computation.10 | async-start | bytes 4456448 | tf_op jit(solution)/shard_map/all_gather | solution.py:190
  14.3 7.8 %copy-start.4 = (s32[1024]{0:T(1024)S(1)}, s32[1024]{0:T(1024)}, u32[]{:S(2)}) copy-start(s32[1024]{0:T(1024)} %param.11) | copy-start | bytes 12292
  14.4 7.8 %copy-start.6 = (f32[4]{0:T(128)S(1)}, f32[4]{0:T(128)}, u32[]{:S(2)}) copy-start(f32[4]{0:T(128)} %param.12) | copy-start | bytes 52
  14.4 7.9 %copy-start.5 = (s32[2048]{0:T(1024)S(1)}, s32[2048]{0:T(1024)}, u32[]{:S(2)}) copy-start(s32[2048]{0:T(1024)} %param.8) | copy-start | bytes 24580
  59.2 10.2 %collective-permute-start.6 = (f32[1024]{0:T(1024)S(1)}, f32[1024]{0:T(1024)S(1)}, u32[]{:S(2)}, u32[]{:S(2)}) collective-permute-start(f32[1024]{0:T(1024)S(1)} %get-tuple-element.18), channel_id=1, source_target_pairs={{0,112},{16,0},{32,16},{48,32},{64,48},{80,64},{96,80},{112,96},{1... | collective-permute-start | bytes 12296 | tf_op jit(solution)/shard_map/ppermute | solution.py:174
  64.1 7.3 %collective-permute-start.5 = (f32[1024]{0:T(1024)S(1)}, f32[1024]{0:T(1024)S(1)}, u32[]{:S(2)}, u32[]{:S(2)}) collective-permute-start(f32[1024]{0:T(1024)S(1)} %get-tuple-element.18), channel_id=1, source_target_pairs={{0,96},{16,112},{32,0},{48,16},{64,32},{80,48},{96,64},{112,80},{1... | collective-permute-start | bytes 12296 | tf_op jit(solution)/shard_map/ppermute | solution.py:174
  65.0 8.1 %collective-permute-start.4 = (f32[1024]{0:T(1024)S(1)}, f32[1024]{0:T(1024)S(1)}, u32[]{:S(2)}, u32[]{:S(2)}) collective-permute-start(f32[1024]{0:T(1024)S(1)} %get-tuple-element.18), channel_id=1, source_target_pairs={{0,80},{16,96},{32,112},{48,0},{64,16},{80,32},{96,48},{112,64},{1... | collective-permute-start | bytes 12296 | tf_op jit(solution)/shard_map/ppermute | solution.py:174
  65.7 7.4 %collective-permute-start.3 = (f32[1024]{0:T(1024)S(1)}, f32[1024]{0:T(1024)S(1)}, u32[]{:S(2)}, u32[]{:S(2)}) collective-permute-start(f32[1024]{0:T(1024)S(1)} %get-tuple-element.18), channel_id=1, source_target_pairs={{0,64},{16,80},{32,96},{48,112},{64,0},{80,16},{96,32},{112,48},{1... | collective-permute-start | bytes 12296 | tf_op jit(solution)/shard_map/ppermute | solution.py:174
  68.4 7.5 %collective-permute-start.2 = (f32[1024]{0:T(1024)S(1)}, f32[1024]{0:T(1024)S(1)}, u32[]{:S(2)}, u32[]{:S(2)}) collective-permute-start(f32[1024]{0:T(1024)S(1)} %get-tuple-element.18), channel_id=1, source_target_pairs={{0,48},{16,64},{32,80},{48,96},{64,112},{80,0},{96,16},{112,32},{1... | collective-permute-start | bytes 12296 | tf_op jit(solution)/shard_map/ppermute | solution.py:174
  69.4 6.5 %collective-permute-start.1 = (f32[1024]{0:T(1024)S(1)}, f32[1024]{0:T(1024)S(1)}, u32[]{:S(2)}, u32[]{:S(2)}) collective-permute-start(f32[1024]{0:T(1024)S(1)} %get-tuple-element.18), channel_id=1, source_target_pairs={{0,32},{16,48},{32,64},{48,80},{64,96},{80,112},{96,0},{112,16},{1... | collective-permute-start | bytes 12296 | tf_op jit(solution)/shard_map/ppermute | solution.py:174
  71.5 7.2 %collective-permute-start = (f32[1024]{0:T(1024)S(1)}, f32[1024]{0:T(1024)S(1)}, u32[]{:S(2)}, u32[]{:S(2)}) collective-permute-start(f32[1024]{0:T(1024)S(1)} %get-tuple-element.18), channel_id=1, source_target_pairs={{0,16},{16,32},{32,48},{48,64},{64,80},{80,96},{96,112},{112,0},{1... | collective-permute-start | bytes 12296 | tf_op jit(solution)/shard_map/ppermute | solution.py:174
  83.8 2.0 copy-start.1
  106.3 16.4 %all-to-all-start.1 = ((f32[8,128,256]{2,1,0:T(8,128)}), f32[8,128,256]{2,1,0:T(8,128)S(1)}, u32[]{:S(2)}, u32[]{:S(2)}) async-start(f32[8,128,256]{2,1,0:T(8,128)} %broadcast_in_dim.88), calls=%async_computation.1 | async-start | bytes 2097152 | tf_op jit(solution)/shard_map/all_to_all | solution.py:115
  126.4 40.2 %copy-start.2 = (bf16[1024,2048]{1,0:T(8,128)(2,1)S(1)}, bf16[1024,2048]{1,0:T(8,128)(2,1)}, u32[]{:S(2)}) copy-start(bf16[1024,2048]{1,0:T(8,128)(2,1)} %copy-done.1) | copy-start | bytes 12582916
  193.5 17.8 %all-to-all-start.5 = ((f32[8,128,256]{2,1,0:T(8,128)}), f32[8,128,256]{2,1,0:T(8,128)S(1)}, u32[]{:S(2)}, u32[]{:S(2)}) async-start(f32[8,128,256]{2,1,0:T(8,128)} %broadcast_in_dim.141), calls=%async_computation.5 | async-start | bytes 2097152 | tf_op jit(solution)/shard_map/all_to_all | solution.py:115
  216.1 40.5 %copy-start.3 = (bf16[1024,2048]{1,0:T(8,128)(2,1)S(1)}, bf16[1024,2048]{1,0:T(8,128)(2,1)}, u32[]{:S(2)}) copy-start(bf16[1024,2048]{1,0:T(8,128)(2,1)} %copy-done.1) | copy-start | bytes 12582916
  281.3 17.8 %all-to-all-start.9 = ((f32[8,128,256]{2,1,0:T(8,128)}), f32[8,128,256]{2,1,0:T(8,128)S(1)}, u32[]{:S(2)}, u32[]{:S(2)}) async-start(f32[8,128,256]{2,1,0:T(8,128)} %broadcast_in_dim.145), calls=%async_computation.9 | async-start | bytes 2097152 | tf_op jit(solution)/shard_map/all_to_all | solution.py:115
Sparse Core Ops, SparseCore 0:
  9.7 39.8 all-gather.1

commit v9 on v4

--- a/solution.py
+++ b/solution.py
@@ -156,14 +156,15 @@
         row_half = exchange_gather(row_chunk.astype(jnp.bfloat16), "landmark")
         row_square = jnp.sum(jnp.square(row_half.astype(jnp.float32)), axis=0)
         column_part = jnp.dot(kernel.T, row_half, preferred_element_type=jnp.float32)
-        column_total, row_square_total = exchange_sum(
-            column_part, row_square, "sample", jnp.float32, jnp.float32
+        column_chunk, row_square_total = exchange_scatter(
+            column_part, row_square, "sample", jnp.float32
         )
-        image = column_total / n_rows + ridge * direction
         curvature = row_square_total / n_rows + ridge * direction_square
         step_size = norm_now / curvature
         weights = weights + step_size * direction
-        residual = residual - step_size * image
+        residual = residual - (step_size * ridge) * direction
+        column_total = exchange_gather(column_chunk, "sample")
+        residual = residual - (step_size / n_rows) * column_total
     return weights, residual
 
 

time: 300 us -> 303 us (1.010)
  no operation moved by 1% of the time
where the time goes in v9:
time: 303 us; the launch traced here: 302 us
  blocking collectives  146 us (48%)
  waiting for transfers between devices  62.1 us (20%)
  local copies, waits for them, and re-layouts  25.1 us (8%)
  matrix products  19.5 us (6%)
  starting transfers between devices  18.8 us (6%)
  other arithmetic  16.2 us (5%)
  between operations  14.4 us (5%)
    all_to_all x5, blocking collectives, exchange_scatter(): got = lax.all_to_all(chunks, axis, 0, 0, tiled=False)  108 us
    all_to_all x2, blocking collectives, exchange_gather(): lax.all_to_all(jnp.broadcast_to(part[None], (size,) + part.shape), axis,...  38.1 us
    all_to_all x3, waiting for transfers between devices, exchange_gather(): lax.all_to_all(jnp.broadcast_to(part[None], (size,) + part.shape), axis,...  28.7 us
    all_gather x1, waiting for transfers between devices, on_device(): gathered = lax.all_gather(summaries, 'landmark', axis=1, tiled=True)  26.2 us
    all_to_all x3, starting transfers between devices, exchange_gather(): lax.all_to_all(jnp.broadcast_to(part[None], (size,) + part.shape), axis,...  11.3 us
    gather x1, local copies, waits for them, and re-layouts, on_device(): anchors = jnp.take(pool, landmark_index, axis=0)  8.79 us
    dot_general x1, matrix products, raw_block(): jnp.dot(summary_rows, anchors.T, preferred_element_type=jnp.float32)  7.88 us
    ppermute x3, starting transfers between devices, butterfly_sum(): x = x + lax.ppermute(x, axis, perm)  7.36 us
  transfers between devices with their start and end apart: 7, of which 7 were waited for; matrix products, arithmetic and copies ran while one was open for 9% of the time, Pallas kernels for 0%

profile of v9, /device:TPU:0, one launch (start us, length us, event | category | flops | bytes accessed | tf_op | source)
XLA Modules:
  0.0 302.4 jit_solution(1293117966038914707)
XLA Ops:
  7.2 0.0 copy-start
  7.2 0.0 all-gather.2.cloned.1.call-start
  7.2 0.7 all-gather.2.cloned.1.call-update
  7.9 0.7 fusion.11
  8.6 5.7 %gather_fusion.1 = s32[1024]{0:T(1024)S(1)} fusion(s32[2048]{0:T(1024)} %param.10, s32[1024]{0:T(1024)S(1)} %fusion.11), kind=kCustom, calls=%fused_computation.1 | custom fusion | bytes 12288 | tf_op jit(solution)/shard_map/jit(_take)/gather | solution.py:179
  14.3 0.0 copy-start.5
  14.4 0.0 copy-start.7
  14.4 0.0 copy-start.6
  14.4 8.8 %gather_fusion = bf16[1024,1024]{1,0:T(8,128)(2,1)} fusion(bf16[2048,1024]{1,0:T(8,128)(2,1)} %param.9, s32[1024]{0:T(1024)S(1)} %fusion.11), kind=kCustom, calls=%fused_computation | custom fusion | bytes 4198400 | tf_op jit(solution)/shard_map/jit(_take)/gather | solution.py:178
  23.2 0.1 select_reduce_fusion.1
  23.3 0.1 select_reduce_fusion
  23.4 26.2 %all-gather.2.cloned.1.call-done = bf16[2048,1024]{0,1:T(8,128)(2,1)} async-done(((bf16[2048,64]{0,1:T(8,128)(2,1)}), bf16[2048,1024]{0,1:T(8,128)(2,1)}) %all-gather.2.cloned.1.call-update) | async-done | bytes 4194320 | tf_op jit(solution)/shard_map/all_gather | solution.py:176
  49.6 7.9 %fusion = (f32[1024]{0:T(1024)S(1)}, f32[1024,2048]{1,0:T(8,128)S(1)}) fusion(f32[1024]{0:T(1024)S(1)} %broadcast_divide_fusion.1, f32[2048]{0:T(1024)S(1)} %broadcast_divide_fusion, bf16[2048,1024]{0,1:T(8,128)(2,1)} %all-gather.2.cloned.1.call-done, bf16[1024,1024]{1,0:T(8,128)(2,1)} %gather_fusion, pred[1024]{0:T(1024)(128)(4,1)S(1)} %get-tuple-element.9), kind=kOutput, calls=%fused_computation.4 | convolution fusion | flops 4302306304 | bytes 14697472 | tf_op jit(solution)/shard_map/dot_general | solution.py:27
  57.5 0.0 copy-start.1
  57.5 1.6 collective-permute-start
  59.1 2.1 collective-permute-done
  61.2 2.8 collective-permute-start.1
  64.0 2.3 collective-permute-done.1
  66.3 3.0 collective-permute-start.2
  69.3 2.1 collective-permute-done.2
  71.4 1.8 subtract_convert_fusion
  73.2 0.0 copy-done.1
  73.2 0.0 copy-done
  73.2 0.0 copy-start.2
  73.3 1.3 fusion.26
  74.5 0.7 copy-done.2
  75.2 20.1 %all_to_all.50 = f32[8,128,256]{2,1,0:T(8,128)S(1)} all-to-all(f32[8,128,256]{2,1,0:T(8,128)S(1)} %bitcast.76), channel_id=1, replica_groups=mesh['sample'=8,'landmark'=16] {'sample'}, dimensions={0} | all-to-all | bytes 2097152 | tf_op jit(solution)/shard_map/all_to_all | solution.py:105
  95.3 0.1 reduce_sum.124
  95.4 1.1 broadcast_in_dim.76
  96.4 3.6 %all-to-all-start.1 = ((f32[8,128,256]{2,1,0:T(8,128)}), f32[8,128,256]{2,1,0:T(8,128)S(1)}, u32[]{:S(2)}, u32[]{:S(2)}) async-start(f32[8,128,256]{2,1,0:T(8,128)} %broadcast_in_dim.76), calls=%async_computation.1 | async-start | bytes 2097152 | tf_op jit(solution)/shard_map/all_to_all | solution.py:115
  100.0 5.6 %fusion.40 = bf16[2048,1024]{0,1:T(8,128)(2,1)} fusion(f32[1024]{0:T(1024)S(1)} %add_multiply_fusion, f32[1024]{0:T(1024)S(1)} %broadcast_divide_fusion.1, f32[1024,2048]{1,0:T(8,128)} %copy-done.1, f32[2048]{0:T(1024)S(1)} %broadcast_divide_fusion), kind=kLoop, calls=%fused_computation.90 | loop fusion | flops 8388608 | bytes 12599296 | tf_op jit(solution)/shard_map/sub | solution.py:184
  105.6 6.4 %copy.15 = bf16[2048,1024]{1,0:T(8,128)(2,1)} copy(bf16[2048,1024]{0,1:T(8,128)(2,1)} %fusion.40) | data formatting | bytes 8388608 | tf_op jit(solution)/shard_map/dot_general | solution.py:136
  112.0 0.2 all-to-all-done.1
  112.2 0.2 multiply_convert_fusion
  112.5 3.4 %convolution_convert_fusion.1 = bf16[16,128,256]{2,1,0:T(8,128)(2,1)S(1)} fusion(bf16[16,128,1024]{2,1,0:T(8,128)(2,1)} %bitcast.72, bf16[1024,256,1]{1,0,2:T(8,128)(2,1)S(1)} %bitcast.78), kind=kOutput, calls=%fused_computation.13 | convolution fusion | flops 1074266112 | bytes 5767168 | tf_op jit(solution)/shard_map/dot_general | solution.py:136
  116.0 0.1 pad_maximum_fusion
  116.1 20.7 %all_to_all.51 = bf16[16,134,256]{2,1,0:T(8,128)(2,1)S(1)} all-to-all(bf16[16,134,256]{2,1,0:T(8,128)(2,1)S(1)} %pad_maximum_fusion), channel_id=1, replica_groups=mesh['sample'=8,'landmark'=16] {'landmark'}, dimensions={0} | all-to-all | bytes 2195456 | tf_op jit(solution)/shard_map/all_to_all | solution.py:105
  136.8 0.2 convert_reduce_fusion.1
  136.9 0.1 broadcast_in_dim.78
  137.0 19.1 %all_to_all.52 = bf16[16,128,256]{2,1,0:T(8,128)(2,1)S(1)} all-to-all(bf16[16,128,256]{2,1,0:T(8,128)(2,1)S(1)} %broadcast_in_dim.78), channel_id=1, replica_groups=mesh['sample'=8,'landmark'=16] {'landmark'}, dimensions={0} | all-to-all | bytes 2097152 | tf_op jit(solution)/shard_map/all_to_all | solution.py:115
  156.1 1.2 fusion.27
  157.4 0.3 multiply_reduce_fusion.1
  157.7 0.1 pad_maximum_fusion.1
  157.8 24.7 %all_to_all.53 = f32[8,129,256]{2,1,0:T(8,128)S(1)} all-to-all(f32[8,129,256]{2,1,0:T(8,128)S(1)} %pad_maximum_fusion.1), channel_id=1, replica_groups=mesh['sample'=8,'landmark'=16] {'sample'}, dimensions={0} | all-to-all | bytes 2113536 | tf_op jit(solution)/shard_map/all_to_all | solution.py:105
  182.4 0.1 reduce_sum.128
  182.5 1.1 broadcast_in_dim.80
  183.6 3.6 %all-to-all-start.5 = ((f32[8,128,256]{2,1,0:T(8,128)}), f32[8,128,256]{2,1,0:T(8,128)S(1)}, u32[]{:S(2)}, u32[]{:S(2)}) async-start(f32[8,128,256]{2,1,0:T(8,128)} %broadcast_in_dim.80), calls=%async_computation.5 | async-start | bytes 2097152 | tf_op jit(solution)/shard_map/all_to_all | solution.py:115
  187.2 14.2 %all-to-all-done.5 = f32[8,128,256]{2,1,0:T(8,128)S(1)} async-done(((f32[8,128,256]{2,1,0:T(8,128)}), f32[8,128,256]{2,1,0:T(8,128)S(1)}, u32[]{:S(2)}, u32[]{:S(2)}) %all-to-all-start.5) | async-done | bytes 1048608 | tf_op jit(solution)/shard_map/all_to_all | solution.py:115
  201.4 0.3 multiply_reduce_fusion.3
  201.7 4.4 %convolution_convert_fusion = bf16[16,128,256]{2,1,0:T(8,128)(2,1)} fusion(bf16[16,128,1024]{2,1,0:T(8,128)(2,1)} %bitcast.73, bf16[1024,256,1]{1,0,2:T(8,128)(2,1)S(1)} %bitcast.77), kind=kOutput, calls=%fused_computation.12 | convolution fusion | flops 1074266112 | bytes 5767168 | tf_op jit(solution)/shard_map/dot_general | solution.py:144
  206.2 1.5 pad_maximum_fusion.2
  207.7 20.9 %all_to_all.54 = bf16[16,134,256]{2,1,0:T(8,128)(2,1)S(1)} all-to-all(bf16[16,134,256]{2,1,0:T(8,128)(2,1)S(1)} %pad_maximum_fusion.2), channel_id=1, replica_groups=mesh['sample'=8,'landmark'=16] {'landmark'}, dimensions={0} | all-to-all | bytes 2195456 | tf_op jit(solution)/shard_map/all_to_all | solution.py:105
  228.5 0.2 convert_reduce_fusion
  228.7 0.1 broadcast_in_dim.82
  228.8 19.1 %all_to_all.55 = bf16[16,128,256]{2,1,0:T(8,128)(2,1)S(1)} all-to-all(bf16[16,128,256]{2,1,0:T(8,128)(2,1)S(1)} %broadcast_in_dim.82), channel_id=1, replica_groups=mesh['sample'=8,'landmark'=16] {'landmark'}, dimensions={0} | all-to-all | bytes 2097152 | tf_op jit(solution)/shard_map/all_to_all | solution.py:115
  247.9 1.3 fusion.28
  249.2 0.3 multiply_reduce_fusion
  249.5 0.1 pad_maximum_fusion.3
  249.6 22.0 %all_to_all.56 = f32[8,129,256]{2,1,0:T(8,128)} all-to-all(f32[8,129,256]{2,1,0:T(8,128)S(1)} %pad_maximum_fusion.3), channel_id=1, replica_groups=mesh['sample'=8,'landmark'=16] {'sample'}, dimensions={0} | all-to-all | bytes 2113536 | tf_op jit(solution)/shard_map/all_to_all | solution.py:105
  271.6 1.3 reduce_sum.133
  273.0 1.1 broadcast_in_dim.84
  274.0 4.2 %all-to-all-start.9 = ((f32[8,128,256]{2,1,0:T(8,128)}), f32[8,128,256]{2,1,0:T(8,128)}, u32[]{:S(2)}, u32[]{:S(2)}) async-start(f32[8,128,256]{2,1,0:T(8,128)} %broadcast_in_dim.84), calls=%async_computation.9 | async-start | bytes 2097152 | tf_op jit(solution)/shard_map/all_to_all | solution.py:115
  278.3 14.3 %all-to-all-done.9 = f32[8,128,256]{2,1,0:T(8,128)} async-done(((f32[8,128,256]{2,1,0:T(8,128)}), f32[8,128,256]{2,1,0:T(8,128)}, u32[]{:S(2)}, u32[]{:S(2)}) %all-to-all-start.9) | async-done | bytes 1048608 | tf_op jit(solution)/shard_map/all_to_all | solution.py:115
  292.6 3.0 fusion.4
  (37 shorter events, 0.3 us)
Async XLA Ops:
  7.2 66.1 %copy-start = (bf16[2048,256]{1,0:T(8,128)(2,1)S(1)}, bf16[2048,256]{1,0:T(8,128)(2,1)}, u32[]{:S(2)}) copy-start(bf16[2048,256]{1,0:T(8,128)(2,1)} %param.13) | copy-start | bytes 3145732
  7.2 42.4 %all-gather.2.cloned.1.call-start = ((), (), s32[]{:S(2)}) async-start(), calls=%async_computation.10 | async-start | bytes 4456448 | tf_op jit(solution)/shard_map/all_gather | solution.py:176
  14.3 8.8 %copy-start.5 = (s32[1024]{0:T(1024)S(1)}, s32[1024]{0:T(1024)}, u32[]{:S(2)}) copy-start(s32[1024]{0:T(1024)} %param.11) | copy-start | bytes 12292
  14.4 8.8 %copy-start.7 = (f32[4]{0:T(128)S(1)}, f32[4]{0:T(128)}, u32[]{:S(2)}) copy-start(f32[4]{0:T(128)} %param.12) | copy-start | bytes 52
  14.4 8.9 %copy-start.6 = (s32[2048]{0:T(1024)S(1)}, s32[2048]{0:T(1024)}, u32[]{:S(2)}) copy-start(s32[2048]{0:T(1024)} %param.8) | copy-start | bytes 24580
  57.5 15.8 %copy-start.1 = (f32[1024,2048]{1,0:T(8,128)}, f32[1024,2048]{1,0:T(8,128)S(1)}, u32[]{:S(2)}) copy-start(f32[1024,2048]{1,0:T(8,128)S(1)} %get-tuple-element.24) | copy-start | bytes 25165828
  57.5 3.7 %collective-permute-start = (f32[1024]{0:T(1024)S(1)}, f32[1024]{0:T(1024)S(1)}, u32[]{:S(2)}, u32[]{:S(2)}) collective-permute-start(f32[1024]{0:T(1024)S(1)} %get-tuple-element.23), channel_id=1, source_target_pairs={{0,32},{16,48},{32,0},{48,16},{64,96},{80,112},{96,64},{112,80},{1... | collective-permute-start | bytes 12296 | tf_op jit(solution)/shard_map/ppermute | solution.py:41
  61.2 5.1 %collective-permute-start.1 = (f32[1024]{0:T(1024)S(1)}, f32[1024]{0:T(1024)S(1)}, u32[]{:S(2)}, u32[]{:S(2)}) collective-permute-start(f32[1024]{0:T(1024)S(1)} %add.68), channel_id=1, source_target_pairs={{0,16},{16,0},{32,48},{48,32},{64,80},{80,64},{96,112},{112,96},{1... | collective-permute-start | bytes 12296 | tf_op jit(solution)/shard_map/ppermute | solution.py:41
  66.3 5.1 %collective-permute-start.2 = (f32[1024]{0:T(1024)S(1)}, f32[1024]{0:T(1024)S(1)}, u32[]{:S(2)}, u32[]{:S(2)}) collective-permute-start(f32[1024]{0:T(1024)S(1)} %add.69), channel_id=1, source_target_pairs={{0,64},{16,80},{32,96},{48,112},{64,0},{80,16},{96,32},{112,48},{1... | collective-permute-start | bytes 12296 | tf_op jit(solution)/shard_map/ppermute | solution.py:41
  73.2 2.0 copy-start.2
  96.4 15.8 %all-to-all-start.1 = ((f32[8,128,256]{2,1,0:T(8,128)}), f32[8,128,256]{2,1,0:T(8,128)S(1)}, u32[]{:S(2)}, u32[]{:S(2)}) async-start(f32[8,128,256]{2,1,0:T(8,128)} %broadcast_in_dim.76), calls=%async_computation.1 | async-start | bytes 2097152 | tf_op jit(solution)/shard_map/all_to_all | solution.py:115
  116.0 40.1 %copy-start.3 = (bf16[1024,2048]{1,0:T(8,128)(2,1)S(1)}, bf16[1024,2048]{1,0:T(8,128)(2,1)}, u32[]{:S(2)}) copy-start(bf16[1024,2048]{1,0:T(8,128)(2,1)} %copy-done.2) | copy-start | bytes 12582916
  183.6 17.8 %all-to-all-start.5 = ((f32[8,128,256]{2,1,0:T(8,128)}), f32[8,128,256]{2,1,0:T(8,128)S(1)}, u32[]{:S(2)}, u32[]{:S(2)}) async-start(f32[8,128,256]{2,1,0:T(8,128)} %broadcast_in_dim.80), calls=%async_computation.5 | async-start | bytes 2097152 | tf_op jit(solution)/shard_map/all_to_all | solution.py:115
  206.2 41.7 %copy-start.4 = (bf16[1024,2048]{1,0:T(8,128)(2,1)S(1)}, bf16[1024,2048]{1,0:T(8,128)(2,1)}, u32[]{:S(2)}) copy-start(bf16[1024,2048]{1,0:T(8,128)(2,1)} %copy-done.2) | copy-start | bytes 12582916
  274.0 18.6 %all-to-all-start.9 = ((f32[8,128,256]{2,1,0:T(8,128)}), f32[8,128,256]{2,1,0:T(8,128)}, u32[]{:S(2)}, u32[]{:S(2)}) async-start(f32[8,128,256]{2,1,0:T(8,128)} %broadcast_in_dim.84), calls=%async_computation.9 | async-start | bytes 2097152 | tf_op jit(solution)/shard_map/all_to_all | solution.py:115
Sparse Core Ops, SparseCore 0:
  9.7 39.8 all-gather.1

commit v10 on v4

--- a/solution.py
+++ b/solution.py
@@ -153,7 +153,7 @@
             direction = residual + beta * direction
             direction_square = norm_next + 2.0 * beta * cross + beta * beta * direction_square
             norm_now = norm_next
-        row_half = exchange_gather(row_chunk.astype(jnp.bfloat16), "landmark")
+        row_half = lax.all_gather(row_chunk.astype(jnp.bfloat16), "landmark", axis=0, tiled=True)
         row_square = jnp.sum(jnp.square(row_half.astype(jnp.float32)), axis=0)
         column_part = jnp.dot(kernel.T, row_half, preferred_element_type=jnp.float32)
         column_total, row_square_total = exchange_sum(

time: 300 us -> 335 us (1.12)
  waiting for transfers between devices: 62 us -> 126 us
  blocking collectives: 146 us -> 110 us
  matrix products: 18.5 us -> 23.6 us
    all_gather x0 -> x2, waiting for transfers between devices: none -> 62.3 us  [conjugate_gradients(): lax.all_gather(row_chunk.astype(jnp.bfloat16), 'landmark', axis=0, tiled=...]
    all_to_all x2 -> x0, blocking collectives: 38.1 us -> none  [exchange_gather(): lax.all_to_all(jnp.broadcast_to(part[None], (size,) + part.shape), axis,...]
    dot_general x2, matrix products: 2.5 us -> 7.57 us  [conjugate_gradients(): jnp.dot(kernel.T, row_half, preferred_element_type=jnp.float32)]
  transfers between devices with their start and end apart: 7 -> 9, of which waited for: 7 -> 9; matrix products, arithmetic and copies ran while one was open for 9% -> 8% of each run, Pallas kernels for 0% -> 0%
where the time goes in v10:
time: 335 us; the launch traced here: 334 us
  waiting for transfers between devices  126 us (38%)
  blocking collectives  110 us (33%)
  local copies, waits for them, and re-layouts  25.5 us (8%)
  matrix products  23.6 us (7%)
  starting transfers between devices  18.2 us (5%)
  other arithmetic  16.7 us (5%)
  between operations  14.1 us (4%)
    all_to_all x5, blocking collectives, exchange_scatter(): got = lax.all_to_all(chunks, axis, 0, 0, tiled=False)  110 us
    all_gather x2, waiting for transfers between devices, conjugate_gradients(): lax.all_gather(row_chunk.astype(jnp.bfloat16), 'landmark', axis=0, tiled=...  62.3 us
    all_to_all x3, waiting for transfers between devices, exchange_gather(): lax.all_to_all(jnp.broadcast_to(part[None], (size,) + part.shape), axis,...  30 us
    all_gather x1, waiting for transfers between devices, on_device(): gathered = lax.all_gather(summaries, 'landmark', axis=1, tiled=True)  26.2 us
    all_to_all x3, starting transfers between devices, exchange_gather(): lax.all_to_all(jnp.broadcast_to(part[None], (size,) + part.shape), axis,...  10.7 us
    gather x1, local copies, waits for them, and re-layouts, on_device(): anchors = jnp.take(pool, landmark_index, axis=0)  8.79 us
    dot_general x1, matrix products, raw_block(): jnp.dot(summary_rows, anchors.T, preferred_element_type=jnp.float32)  7.88 us
    dot_general x2, matrix products, conjugate_gradients(): jnp.dot(kernel.T, row_half, preferred_element_type=jnp.float32)  7.57 us
  transfers between devices with their start and end apart: 9, of which 9 were waited for; matrix products, arithmetic and copies ran while one was open for 8% of the time, Pallas kernels for 0%

profile of v10, /device:TPU:0, one launch (start us, length us, event | category | flops | bytes accessed | tf_op | source)
XLA Modules:
  0.0 334.1 jit_solution(675963857444919960)
XLA Ops:
  7.2 0.0 copy-start
  7.2 0.0 all-gather.4.cloned.1.call-start
  7.2 0.7 all-gather.4.cloned.1.call-update
  7.9 0.7 fusion.12
  8.6 5.7 %gather_fusion.1 = s32[1024]{0:T(1024)S(1)} fusion(s32[2048]{0:T(1024)} %param.10, s32[1024]{0:T(1024)S(1)} %fusion.12), kind=kCustom, calls=%fused_computation.1 | custom fusion | bytes 12288 | tf_op jit(solution)/shard_map/jit(_take)/gather | solution.py:178
  14.4 0.0 copy-start.6
  14.4 0.0 copy-start.5
  14.4 8.8 %gather_fusion = bf16[1024,1024]{1,0:T(8,128)(2,1)} fusion(bf16[2048,1024]{1,0:T(8,128)(2,1)} %param.9, s32[1024]{0:T(1024)S(1)} %fusion.12), kind=kCustom, calls=%fused_computation | custom fusion | bytes 4198400 | tf_op jit(solution)/shard_map/jit(_take)/gather | solution.py:177
  23.2 0.1 select_reduce_fusion.1
  23.3 0.1 select_reduce_fusion
  23.4 26.2 %all-gather.4.cloned.1.call-done = bf16[2048,1024]{0,1:T(8,128)(2,1)} async-done(((bf16[2048,64]{0,1:T(8,128)(2,1)}), bf16[2048,1024]{0,1:T(8,128)(2,1)}) %all-gather.4.cloned.1.call-update) | async-done | bytes 4194320 | tf_op jit(solution)/shard_map/all_gather | solution.py:175
  49.6 7.9 %fusion = (f32[1024]{0:T(1024)S(1)}, f32[1024,2048]{1,0:T(8,128)S(1)}) fusion(f32[1024]{0:T(1024)S(1)} %broadcast_divide_fusion.1, f32[2048]{0:T(1024)S(1)} %broadcast_divide_fusion, bf16[2048,1024]{0,1:T(8,128)(2,1)} %all-gather.4.cloned.1.call-done, bf16[1024,1024]{1,0:T(8,128)(2,1)} %gather_fusion, pred[1024]{0:T(1024)(128)(4,1)S(1)} %get-tuple-element.5), kind=kOutput, calls=%fused_computation.4 | convolution fusion | flops 4302306304 | bytes 14697472 | tf_op jit(solution)/shard_map/dot_general | solution.py:27
  57.5 1.6 collective-permute-start
  59.1 2.1 collective-permute-done
  61.2 2.8 collective-permute-start.1
  64.0 2.3 collective-permute-done.1
  66.3 3.0 collective-permute-start.2
  69.3 2.1 collective-permute-done.2
  71.4 1.8 subtract_convert_fusion
  73.3 1.3 fusion.25
  74.5 0.7 copy-done.2
  75.2 20.1 %all_to_all.40 = f32[8,128,256]{2,1,0:T(8,128)S(1)} all-to-all(f32[8,128,256]{2,1,0:T(8,128)S(1)} %bitcast.67), channel_id=1, replica_groups=mesh['sample'=8,'landmark'=16] {'sample'}, dimensions={0} | all-to-all | bytes 2097152 | tf_op jit(solution)/shard_map/all_to_all | solution.py:105
  95.3 0.1 reduce_sum.124
  95.4 1.1 broadcast_in_dim.72
  96.4 3.6 %all-to-all-start.1 = ((f32[8,128,256]{2,1,0:T(8,128)}), f32[8,128,256]{2,1,0:T(8,128)S(1)}, u32[]{:S(2)}, u32[]{:S(2)}) async-start(f32[8,128,256]{2,1,0:T(8,128)} %broadcast_in_dim.72), calls=%async_computation.1 | async-start | bytes 2097152 | tf_op jit(solution)/shard_map/all_to_all | solution.py:115
  100.0 0.0 all-gather.6.cloned.1.call-start
  100.0 5.6 %fusion.39 = bf16[2048,1024]{0,1:T(8,128)(2,1)} fusion(f32[1024]{0:T(1024)S(1)} %add_multiply_fusion, f32[1024]{0:T(1024)S(1)} %broadcast_divide_fusion.1, f32[1024,2048]{1,0:T(8,128)} %copy-done.1, f32[2048]{0:T(1024)S(1)} %broadcast_divide_fusion), kind=kLoop, calls=%fused_computation.89 | loop fusion | flops 8388608 | bytes 12599296 | tf_op jit(solution)/shard_map/sub | solution.py:183
  105.7 6.4 %copy.15 = bf16[2048,1024]{1,0:T(8,128)(2,1)} copy(bf16[2048,1024]{0,1:T(8,128)(2,1)} %fusion.39) | data formatting | bytes 8388608 | tf_op jit(solution)/shard_map/dot_general | solution.py:136
  112.1 0.2 all-to-all-done.1
  112.2 0.2 multiply_convert_fusion
  112.5 3.4 %convolution_convert_fusion.1 = bf16[16,128,256]{2,1,0:T(8,128)(2,1)S(1)} fusion(bf16[16,128,1024]{2,1,0:T(8,128)(2,1)} %bitcast.63, bf16[1024,256,1]{1,0,2:T(8,128)(2,1)S(1)} %bitcast.68), kind=kOutput, calls=%fused_computation.13 | convolution fusion | flops 1074266112 | bytes 5767168 | tf_op jit(solution)/shard_map/dot_general | solution.py:136
  116.0 0.1 pad_maximum_fusion
  116.1 20.6 %all_to_all.41 = bf16[16,134,256]{2,1,0:T(8,128)(2,1)S(1)} all-to-all(bf16[16,134,256]{2,1,0:T(8,128)(2,1)S(1)} %pad_maximum_fusion), channel_id=1, replica_groups=mesh['sample'=8,'landmark'=16] {'landmark'}, dimensions={0} | all-to-all | bytes 2195456 | tf_op jit(solution)/shard_map/all_to_all | solution.py:105
  136.7 0.2 convert_reduce_fusion.1
  136.8 0.6 slice.140
  137.5 0.0 all-gather.6.cloned.1.call-update
  137.5 32.6 %all-gather.6.cloned.1.call-done = bf16[2048,256]{1,0:T(8,128)(2,1)} async-done(((bf16[128,256]{1,0:T(8,128)(2,1)}), bf16[2048,256]{1,0:T(8,128)(2,1)}) %all-gather.6.cloned.1.call-update) | async-done | bytes 1048592 | tf_op jit(solution)/shard_map/all_gather | solution.py:156
  170.1 1.5 multiply_reduce_fusion.1
  171.7 3.7 %fusion.26 = f32[1024,256]{1,0:T(8,128)S(1)} fusion(bf16[1024,2048]{1,0:T(8,128)(2,1)} %copy-done.2, bf16[2048,256]{1,0:T(8,128)(2,1)} %all-gather.6.cloned.1.call-done), kind=kOutput, calls=%fused_computation.87 | convolution fusion | flops 1073741824 | bytes 6291456 | tf_op jit(solution)/shard_map/dot_general | solution.py:158
  175.4 0.1 pad_maximum_fusion.1
  175.5 24.5 %all_to_all.42 = f32[8,129,256]{2,1,0:T(8,128)S(1)} all-to-all(f32[8,129,256]{2,1,0:T(8,128)S(1)} %pad_maximum_fusion.1), channel_id=1, replica_groups=mesh['sample'=8,'landmark'=16] {'sample'}, dimensions={0} | all-to-all | bytes 2113536 | tf_op jit(solution)/shard_map/all_to_all | solution.py:105
  200.0 0.1 reduce_sum.128
  200.1 1.1 broadcast_in_dim.116
  201.2 3.6 %all-to-all-start.4 = ((f32[8,128,256]{2,1,0:T(8,128)}), f32[8,128,256]{2,1,0:T(8,128)S(1)}, u32[]{:S(2)}, u32[]{:S(2)}) async-start(f32[8,128,256]{2,1,0:T(8,128)} %broadcast_in_dim.116), calls=%async_computation.4 | async-start | bytes 2097152 | tf_op jit(solution)/shard_map/all_to_all | solution.py:115
  204.8 0.0 all-gather.8.cloned.1.call-start
  204.8 14.9 %all-to-all-done.4 = f32[8,128,256]{2,1,0:T(8,128)S(1)} async-done(((f32[8,128,256]{2,1,0:T(8,128)}), f32[8,128,256]{2,1,0:T(8,128)S(1)}, u32[]{:S(2)}, u32[]{:S(2)}) %all-to-all-start.4) | async-done | bytes 1048608 | tf_op jit(solution)/shard_map/all_to_all | solution.py:115
  219.8 1.3 multiply_reduce_fusion.3
  221.1 3.4 %convolution_convert_fusion = bf16[16,128,256]{2,1,0:T(8,128)(2,1)S(1)} fusion(bf16[16,128,1024]{2,1,0:T(8,128)(2,1)} %bitcast.64, bf16[1024,256,1]{1,0,2:T(8,128)(2,1)S(1)} %bitcast.69), kind=kOutput, calls=%fused_computation.12 | convolution fusion | flops 1074266112 | bytes 5767168 | tf_op jit(solution)/shard_map/dot_general | solution.py:144
  224.6 0.1 pad_maximum_fusion.2
  224.7 20.5 %all_to_all.43 = bf16[16,134,256]{2,1,0:T(8,128)(2,1)S(1)} all-to-all(bf16[16,134,256]{2,1,0:T(8,128)(2,1)S(1)} %pad_maximum_fusion.2), channel_id=1, replica_groups=mesh['sample'=8,'landmark'=16] {'landmark'}, dimensions={0} | all-to-all | bytes 2195456 | tf_op jit(solution)/shard_map/all_to_all | solution.py:105
  245.2 0.2 convert_reduce_fusion
  245.4 0.7 fusion.11
  246.1 0.0 all-gather.8.cloned.1.call-update
  246.1 29.7 %all-gather.8.cloned.1.call-done = bf16[2048,256]{1,0:T(8,128)(2,1)} async-done(((bf16[128,256]{1,0:T(8,128)(2,1)}), bf16[2048,256]{1,0:T(8,128)(2,1)}) %all-gather.8.cloned.1.call-update) | async-done | bytes 1048592 | tf_op jit(solution)/shard_map/all_gather | solution.py:156
  275.7 3.8 %fusion.27 = f32[1024,256]{1,0:T(8,128)S(1)} fusion(bf16[1024,2048]{1,0:T(8,128)(2,1)} %copy-done.2, bf16[2048,256]{1,0:T(8,128)(2,1)} %all-gather.8.cloned.1.call-done), kind=kOutput, calls=%fused_computation.88 | convolution fusion | flops 1073741824 | bytes 6291456 | tf_op jit(solution)/shard_map/dot_general | solution.py:158
  279.6 0.3 multiply_reduce_fusion
  279.9 0.1 pad_maximum_fusion.3
  280.0 24.5 %all_to_all.44 = f32[8,129,256]{2,1,0:T(8,128)S(1)} all-to-all(f32[8,129,256]{2,1,0:T(8,128)S(1)} %pad_maximum_fusion.3), channel_id=1, replica_groups=mesh['sample'=8,'landmark'=16] {'sample'}, dimensions={0} | all-to-all | bytes 2113536 | tf_op jit(solution)/shard_map/all_to_all | solution.py:105
  304.5 0.1 reduce_sum.133
  304.6 1.1 broadcast_in_dim.119
  305.7 3.6 %all-to-all-start.7 = ((f32[8,128,256]{2,1,0:T(8,128)}), f32[8,128,256]{2,1,0:T(8,128)S(1)}, u32[]{:S(2)}, u32[]{:S(2)}) async-start(f32[8,128,256]{2,1,0:T(8,128)} %broadcast_in_dim.119), calls=%async_computation.7 | async-start | bytes 2097152 | tf_op jit(solution)/shard_map/all_to_all | solution.py:115
  309.3 15.0 %all-to-all-done.7 = f32[8,128,256]{2,1,0:T(8,128)S(1)} async-done(((f32[8,128,256]{2,1,0:T(8,128)}), f32[8,128,256]{2,1,0:T(8,128)S(1)}, u32[]{:S(2)}, u32[]{:S(2)}) %all-to-all-start.7) | async-done | bytes 1048608 | tf_op jit(solution)/shard_map/all_to_all | solution.py:115
  324.2 0.1 broadcast_multiply_fusion
  324.3 3.2 fusion.5
  (37 shorter events, 0.2 us)
Async XLA Ops:
  7.2 66.1 %copy-start = (bf16[2048,256]{1,0:T(8,128)(2,1)S(1)}, bf16[2048,256]{1,0:T(8,128)(2,1)}, u32[]{:S(2)}) copy-start(bf16[2048,256]{1,0:T(8,128)(2,1)} %param.13) | copy-start | bytes 3145732
  7.2 42.4 %all-gather.4.cloned.1.call-start = ((), (), s32[]{:S(2)}) async-start(), calls=%async_computation.8 | async-start | bytes 4456448 | tf_op jit(solution)/shard_map/all_gather | solution.py:175
  14.3 8.8 %copy-start.4 = (s32[1024]{0:T(1024)S(1)}, s32[1024]{0:T(1024)}, u32[]{:S(2)}) copy-start(s32[1024]{0:T(1024)} %param.11) | copy-start | bytes 12292
  14.4 8.8 %copy-start.6 = (f32[4]{0:T(128)S(1)}, f32[4]{0:T(128)}, u32[]{:S(2)}) copy-start(f32[4]{0:T(128)} %param.12) | copy-start | bytes 52
  14.4 8.9 %copy-start.5 = (s32[2048]{0:T(1024)S(1)}, s32[2048]{0:T(1024)}, u32[]{:S(2)}) copy-start(s32[2048]{0:T(1024)} %param.8) | copy-start | bytes 24580
  57.5 15.8 %copy-start.1 = (f32[1024,2048]{1,0:T(8,128)}, f32[1024,2048]{1,0:T(8,128)S(1)}, u32[]{:S(2)}) copy-start(f32[1024,2048]{1,0:T(8,128)S(1)} %get-tuple-element.19) | copy-start | bytes 25165828
  57.5 3.7 %collective-permute-start = (f32[1024]{0:T(1024)S(1)}, f32[1024]{0:T(1024)S(1)}, u32[]{:S(2)}, u32[]{:S(2)}) collective-permute-start(f32[1024]{0:T(1024)S(1)} %get-tuple-element.18), channel_id=1, source_target_pairs={{0,32},{16,48},{32,0},{48,16},{64,96},{80,112},{96,64},{112,80},{1... | collective-permute-start | bytes 12296 | tf_op jit(solution)/shard_map/ppermute | solution.py:41
  61.2 5.1 %collective-permute-start.1 = (f32[1024]{0:T(1024)S(1)}, f32[1024]{0:T(1024)S(1)}, u32[]{:S(2)}, u32[]{:S(2)}) collective-permute-start(f32[1024]{0:T(1024)S(1)} %add.71), channel_id=1, source_target_pairs={{0,16},{16,0},{32,48},{48,32},{64,80},{80,64},{96,112},{112,96},{1... | collective-permute-start | bytes 12296 | tf_op jit(solution)/shard_map/ppermute | solution.py:41
  66.3 5.1 %collective-permute-start.2 = (f32[1024]{0:T(1024)S(1)}, f32[1024]{0:T(1024)S(1)}, u32[]{:S(2)}, u32[]{:S(2)}) collective-permute-start(f32[1024]{0:T(1024)S(1)} %add.72), channel_id=1, source_target_pairs={{0,64},{16,80},{32,96},{48,112},{64,0},{80,16},{96,32},{112,48},{1... | collective-permute-start | bytes 12296 | tf_op jit(solution)/shard_map/ppermute | solution.py:41
  73.2 2.0 copy-start.2
  96.4 15.8 %all-to-all-start.1 = ((f32[8,128,256]{2,1,0:T(8,128)}), f32[8,128,256]{2,1,0:T(8,128)S(1)}, u32[]{:S(2)}, u32[]{:S(2)}) async-start(f32[8,128,256]{2,1,0:T(8,128)} %broadcast_in_dim.72), calls=%async_computation.1 | async-start | bytes 2097152 | tf_op jit(solution)/shard_map/all_to_all | solution.py:115
  100.0 70.1 %all-gather.6.cloned.1.call-start = ((), (), s32[]{:S(2)}) async-start(), calls=%async_computation.9 | async-start | bytes 1114112 | tf_op jit(solution)/shard_map/all_gather | solution.py:156
  201.2 18.6 %all-to-all-start.4 = ((f32[8,128,256]{2,1,0:T(8,128)}), f32[8,128,256]{2,1,0:T(8,128)S(1)}, u32[]{:S(2)}, u32[]{:S(2)}) async-start(f32[8,128,256]{2,1,0:T(8,128)} %broadcast_in_dim.116), calls=%async_computation.4 | async-start | bytes 2097152 | tf_op jit(solution)/shard_map/all_to_all | solution.py:115
  204.8 71.0 %all-gather.8.cloned.1.call-start = ((), (), s32[]{:S(2)}) async-start(), calls=%async_computation.10 | async-start | bytes 1114112 | tf_op jit(solution)/shard_map/all_gather | solution.py:156
  275.7 3.8 %copy-start.3 = (bf16[2048,256]{1,0:T(8,128)(2,1)S(1)}, bf16[2048,256]{1,0:T(8,128)(2,1)}, u32[]{:S(2)}) copy-start(bf16[2048,256]{1,0:T(8,128)(2,1)} %all-gather.8.cloned.1.call-done) | copy-start | bytes 3145732
  305.7 18.6 %all-to-all-start.7 = ((f32[8,128,256]{2,1,0:T(8,128)}), f32[8,128,256]{2,1,0:T(8,128)S(1)}, u32[]{:S(2)}, u32[]{:S(2)}) async-start(f32[8,128,256]{2,1,0:T(8,128)} %broadcast_in_dim.119), calls=%async_computation.7 | async-start | bytes 2097152 | tf_op jit(solution)/shard_map/all_to_all | solution.py:115
Sparse Core Ops, SparseCore 0:
  9.7 39.8 all-gather.3
  137.6 32.4 all-gather.5
  246.2 29.4 all-gather.7

commit v11 on v4

--- a/solution.py
+++ b/solution.py
@@ -53,12 +53,14 @@
             term = lax.reduce_precision(rest, exponent_bits=8, mantissa_bits=7)
             parts.append(term)
             rest = rest - term
-    return jnp.concatenate(parts, axis=0).astype(wire_dtype)
+    packed = jnp.concatenate(parts, axis=0).astype(wire_dtype)
+    tile = 8 if wire_dtype == jnp.float32 else 16
+    return jnp.pad(packed, ((0, -packed.shape[0] % tile), (0, 0)))
 
 
 def unpack_rows(packed, count, wire_dtype):
     terms = 1 if wire_dtype == jnp.float32 else 3
-    packed = packed.astype(jnp.float32).reshape(terms, count, -1)
+    packed = packed[: terms * count].astype(jnp.float32).reshape(terms, count, -1)
     total = packed[0]
     for t in range(1, terms):
         total = total + packed[t]

time: 300 us -> 302 us (level)
  no operation moved by 1% of the time
where the time goes in v11:
time: 302 us; the launch traced here: 301 us
  blocking collectives  148 us (49%)
  waiting for transfers between devices  62 us (21%)
  local copies, waits for them, and re-layouts  25.1 us (8%)
  matrix products  18.5 us (6%)
  starting transfers between devices  18.1 us (6%)
  other arithmetic  14.8 us (5%)
  between operations  14.4 us (5%)
    all_to_all x5, blocking collectives, exchange_scatter(): got = lax.all_to_all(chunks, axis, 0, 0, tiled=False)  110 us
    all_to_all x2, blocking collectives, exchange_gather(): lax.all_to_all(jnp.broadcast_to(part[None], (size,) + part.shape), axis,...  38.1 us
    all_to_all x3, waiting for transfers between devices, exchange_gather(): lax.all_to_all(jnp.broadcast_to(part[None], (size,) + part.shape), axis,...  28.6 us
    all_gather x1, waiting for transfers between devices, on_device(): gathered = lax.all_gather(summaries, 'landmark', axis=1, tiled=True)  26.2 us
    all_to_all x3, starting transfers between devices, exchange_gather(): lax.all_to_all(jnp.broadcast_to(part[None], (size,) + part.shape), axis,...  10.7 us
    gather x1, local copies, waits for them, and re-layouts, on_device(): anchors = jnp.take(pool, landmark_index, axis=0)  8.79 us
    dot_general x1, matrix products, raw_block(): jnp.dot(summary_rows, anchors.T, preferred_element_type=jnp.float32)  7.88 us
    ppermute x3, starting transfers between devices, butterfly_sum(): x = x + lax.ppermute(x, axis, perm)  7.36 us
  transfers between devices with their start and end apart: 7, of which 7 were waited for; matrix products, arithmetic and copies ran while one was open for 9% of the time, Pallas kernels for 0%

profile of v11, /device:TPU:0, one launch (start us, length us, event | category | flops | bytes accessed | tf_op | source)
XLA Modules:
  0.0 300.9 jit_solution(10350655231106981196)
XLA Ops:
  7.2 0.0 copy-start
  7.2 0.0 all-gather.2.cloned.1.call-start
  7.2 0.7 all-gather.2.cloned.1.call-update
  7.9 0.7 fusion.22
  8.6 5.7 %gather_fusion.1 = s32[1024]{0:T(1024)S(1)} fusion(s32[2048]{0:T(1024)} %param.10, s32[1024]{0:T(1024)S(1)} %fusion.22), kind=kCustom, calls=%fused_computation.1 | custom fusion | bytes 12288 | tf_op jit(solution)/shard_map/jit(_take)/gather | solution.py:180
  14.3 0.0 copy-start.5
  14.4 0.0 copy-start.7
  14.4 0.0 copy-start.6
  14.4 8.8 %gather_fusion = bf16[1024,1024]{1,0:T(8,128)(2,1)} fusion(bf16[2048,1024]{1,0:T(8,128)(2,1)} %param.9, s32[1024]{0:T(1024)S(1)} %fusion.22), kind=kCustom, calls=%fused_computation | custom fusion | bytes 4198400 | tf_op jit(solution)/shard_map/jit(_take)/gather | solution.py:179
  23.2 0.0 copy-done.5
  23.2 0.0 copy-done.7
  23.2 0.1 select_reduce_fusion.1
  23.3 0.1 select_reduce_fusion
  23.4 26.2 %all-gather.2.cloned.1.call-done = bf16[2048,1024]{0,1:T(8,128)(2,1)} async-done(((bf16[2048,64]{0,1:T(8,128)(2,1)}), bf16[2048,1024]{0,1:T(8,128)(2,1)}) %all-gather.2.cloned.1.call-update) | async-done | bytes 4194320 | tf_op jit(solution)/shard_map/all_gather | solution.py:177
  49.6 7.9 %fusion = (f32[1024]{0:T(1024)S(1)}, f32[1024,2048]{1,0:T(8,128)S(1)}) fusion(f32[1024]{0:T(1024)S(1)} %broadcast_divide_fusion.1, f32[2048]{0:T(1024)S(1)} %broadcast_divide_fusion, bf16[2048,1024]{0,1:T(8,128)(2,1)} %all-gather.2.cloned.1.call-done, bf16[1024,1024]{1,0:T(8,128)(2,1)} %gather_fusion, pred[1024]{0:T(1024)(128)(4,1)S(1)} %get-tuple-element.5), kind=kOutput, calls=%fused_computation.4 | convolution fusion | flops 4302306304 | bytes 14697472 | tf_op jit(solution)/shard_map/dot_general | solution.py:27
  57.5 0.0 copy-start.1
  57.5 1.6 collective-permute-start
  59.1 2.1 collective-permute-done
  61.2 2.8 collective-permute-start.1
  64.0 2.3 collective-permute-done.1
  66.3 3.0 collective-permute-start.2
  69.3 2.1 collective-permute-done.2
  71.4 1.8 subtract_convert_fusion
  73.3 1.3 fusion.35
  74.5 0.7 copy-done.2
  75.2 20.1 %all_to_all.50 = f32[8,128,256]{2,1,0:T(8,128)S(1)} all-to-all(f32[8,128,256]{2,1,0:T(8,128)S(1)} %bitcast.76), channel_id=1, replica_groups=mesh['sample'=8,'landmark'=16] {'sample'}, dimensions={0} | all-to-all | bytes 2097152 | tf_op jit(solution)/shard_map/all_to_all | solution.py:107
  95.3 0.1 reduce_sum.124
  95.4 1.1 broadcast_in_dim.76
  96.4 3.6 %all-to-all-start.1 = ((f32[8,128,256]{2,1,0:T(8,128)}), f32[8,128,256]{2,1,0:T(8,128)S(1)}, u32[]{:S(2)}, u32[]{:S(2)}) async-start(f32[8,128,256]{2,1,0:T(8,128)} %broadcast_in_dim.76), calls=%async_computation.1 | async-start | bytes 2097152 | tf_op jit(solution)/shard_map/all_to_all | solution.py:117
  100.0 5.6 %fusion.49 = bf16[2048,1024]{0,1:T(8,128)(2,1)} fusion(f32[1024]{0:T(1024)S(1)} %add_multiply_fusion, f32[1024]{0:T(1024)S(1)} %broadcast_divide_fusion.1, f32[1024,2048]{1,0:T(8,128)} %copy-done.1, f32[2048]{0:T(1024)S(1)} %broadcast_divide_fusion), kind=kLoop, calls=%fused_computation.98 | loop fusion | flops 8388608 | bytes 12599296 | tf_op jit(solution)/shard_map/sub | solution.py:185
  105.6 6.4 %copy.15 = bf16[2048,1024]{1,0:T(8,128)(2,1)} copy(bf16[2048,1024]{0,1:T(8,128)(2,1)} %fusion.49) | data formatting | bytes 8388608 | tf_op jit(solution)/shard_map/dot_general | solution.py:138
  112.0 0.2 all-to-all-done.1
  112.2 0.2 multiply_convert_fusion
  112.5 3.4 %convolution_convert_fusion.1 = bf16[16,128,256]{2,1,0:T(8,128)(2,1)S(1)} fusion(bf16[16,128,1024]{2,1,0:T(8,128)(2,1)} %bitcast.72, bf16[1024,256,1]{1,0,2:T(8,128)(2,1)S(1)} %bitcast.77), kind=kOutput, calls=%fused_computation.13 | convolution fusion | flops 1074266112 | bytes 5767168 | tf_op jit(solution)/shard_map/dot_general | solution.py:138
  116.0 0.1 pad_maximum_fusion
  116.1 21.4 %all_to_all.51 = bf16[16,144,256]{2,1,0:T(8,128)(2,1)S(1)} all-to-all(bf16[16,144,256]{2,1,0:T(8,128)(2,1)S(1)} %pad_maximum_fusion), channel_id=1, replica_groups=mesh['sample'=8,'landmark'=16] {'landmark'}, dimensions={0} | all-to-all | bytes 2359296 | tf_op jit(solution)/shard_map/all_to_all | solution.py:107
  137.5 0.2 convert_reduce_fusion.1
  137.7 0.1 broadcast_in_dim.78
  137.8 19.1 %all_to_all.52 = bf16[16,128,256]{2,1,0:T(8,128)(2,1)S(1)} all-to-all(bf16[16,128,256]{2,1,0:T(8,128)(2,1)S(1)} %broadcast_in_dim.78), channel_id=1, replica_groups=mesh['sample'=8,'landmark'=16] {'landmark'}, dimensions={0} | all-to-all | bytes 2097152 | tf_op jit(solution)/shard_map/all_to_all | solution.py:117
  156.8 0.3 multiply_reduce_fusion.1
  157.2 1.3 fusion.36
  158.4 0.1 pad_maximum_fusion.2
  158.5 24.7 %all_to_all.53 = f32[8,136,256]{2,1,0:T(8,128)S(1)} all-to-all(f32[8,136,256]{2,1,0:T(8,128)S(1)} %pad_maximum_fusion.2), channel_id=1, replica_groups=mesh['sample'=8,'landmark'=16] {'sample'}, dimensions={0} | all-to-all | bytes 2228224 | tf_op jit(solution)/shard_map/all_to_all | solution.py:107
  183.2 0.1 reduce_sum.128
  183.3 1.1 broadcast_in_dim.80
  184.3 3.6 %all-to-all-start.5 = ((f32[8,128,256]{2,1,0:T(8,128)}), f32[8,128,256]{2,1,0:T(8,128)S(1)}, u32[]{:S(2)}, u32[]{:S(2)}) async-start(f32[8,128,256]{2,1,0:T(8,128)} %broadcast_in_dim.80), calls=%async_computation.5 | async-start | bytes 2097152 | tf_op jit(solution)/shard_map/all_to_all | solution.py:117
  187.9 14.2 %all-to-all-done.5 = f32[8,128,256]{2,1,0:T(8,128)S(1)} async-done(((f32[8,128,256]{2,1,0:T(8,128)}), f32[8,128,256]{2,1,0:T(8,128)S(1)}, u32[]{:S(2)}, u32[]{:S(2)}) %all-to-all-start.5) | async-done | bytes 1048608 | tf_op jit(solution)/shard_map/all_to_all | solution.py:117
  202.1 1.3 multiply_reduce_fusion.3
  203.5 3.4 %convolution_convert_fusion = bf16[16,128,256]{2,1,0:T(8,128)(2,1)S(1)} fusion(bf16[16,128,1024]{2,1,0:T(8,128)(2,1)} %bitcast.73, bf16[1024,256,1]{1,0,2:T(8,128)(2,1)S(1)} %bitcast.78), kind=kOutput, calls=%fused_computation.12 | convolution fusion | flops 1074266112 | bytes 5767168 | tf_op jit(solution)/shard_map/dot_general | solution.py:146
  207.0 0.1 pad_maximum_fusion.1
  207.1 21.7 %all_to_all.54 = bf16[16,144,256]{2,1,0:T(8,128)(2,1)S(1)} all-to-all(bf16[16,144,256]{2,1,0:T(8,128)(2,1)S(1)} %pad_maximum_fusion.1), channel_id=1, replica_groups=mesh['sample'=8,'landmark'=16] {'landmark'}, dimensions={0} | all-to-all | bytes 2359296 | tf_op jit(solution)/shard_map/all_to_all | solution.py:107
  228.8 0.2 convert_reduce_fusion
  229.0 0.1 broadcast_in_dim.82
  229.1 19.1 %all_to_all.55 = bf16[16,128,256]{2,1,0:T(8,128)(2,1)S(1)} all-to-all(bf16[16,128,256]{2,1,0:T(8,128)(2,1)S(1)} %broadcast_in_dim.82), channel_id=1, replica_groups=mesh['sample'=8,'landmark'=16] {'landmark'}, dimensions={0} | all-to-all | bytes 2097152 | tf_op jit(solution)/shard_map/all_to_all | solution.py:117
  248.2 1.3 fusion.37
  249.5 0.3 multiply_reduce_fusion
  249.8 0.1 pad_maximum_fusion.3
  249.9 21.9 %all_to_all.56 = f32[8,136,256]{2,1,0:T(8,128)S(1)} all-to-all(f32[8,136,256]{2,1,0:T(8,128)S(1)} %pad_maximum_fusion.3), channel_id=1, replica_groups=mesh['sample'=8,'landmark'=16] {'sample'}, dimensions={0} | all-to-all | bytes 2228224 | tf_op jit(solution)/shard_map/all_to_all | solution.py:107
  271.8 0.1 reduce_sum.133
  271.9 1.1 broadcast_in_dim.84
  272.9 3.6 %all-to-all-start.9 = ((f32[8,128,256]{2,1,0:T(8,128)}), f32[8,128,256]{2,1,0:T(8,128)S(1)}, u32[]{:S(2)}, u32[]{:S(2)}) async-start(f32[8,128,256]{2,1,0:T(8,128)} %broadcast_in_dim.84), calls=%async_computation.9 | async-start | bytes 2097152 | tf_op jit(solution)/shard_map/all_to_all | solution.py:117
  276.5 14.2 %all-to-all-done.9 = f32[8,128,256]{2,1,0:T(8,128)S(1)} async-done(((f32[8,128,256]{2,1,0:T(8,128)}), f32[8,128,256]{2,1,0:T(8,128)S(1)}, u32[]{:S(2)}, u32[]{:S(2)}) %all-to-all-start.9) | async-done | bytes 1048608 | tf_op jit(solution)/shard_map/all_to_all | solution.py:117
  290.7 0.1 broadcast_multiply_fusion
  290.8 3.2 %fusion.5 = (f32[1024,256]{1,0:T(8,128)}, f32[1024,256]{1,0:T(8,128)}) fusion(f32[8,128,256]{2,1,0:T(8,128)S(1)} %broadcast_multiply_fusion, f32[256]{0:T(256)S(1)} %broadcast_multiply_fusion.2, f32[8,128,256]{2,1,0:T(8,128)S(1)} %all-to-all-done.1, f32[8,128,256]{2,1,0:T(8,128)} %get-tuple-element.9, f32[256]{0:T(256)S(1)} %bitcast.83, f32[256]{0:T(256)S(1)} %bitcast.86, ...), kind=kLoop, calls=%fused_computation.20 | loop fusion | flops 3670016 | bytes 5246976 | tf_op jit(solution)/shard_map/sub | solution.py:168
  (39 shorter events, 0.3 us)
Async XLA Ops:
  7.2 66.1 %copy-start = (bf16[2048,256]{1,0:T(8,128)(2,1)S(1)}, bf16[2048,256]{1,0:T(8,128)(2,1)}, u32[]{:S(2)}) copy-start(bf16[2048,256]{1,0:T(8,128)(2,1)} %param.13) | copy-start | bytes 3145732
  7.2 42.4 %all-gather.2.cloned.1.call-start = ((), (), s32[]{:S(2)}) async-start(), calls=%async_computation.10 | async-start | bytes 4456448 | tf_op jit(solution)/shard_map/all_gather | solution.py:177
  14.3 8.8 %copy-start.5 = (s32[1024]{0:T(1024)S(1)}, s32[1024]{0:T(1024)}, u32[]{:S(2)}) copy-start(s32[1024]{0:T(1024)} %param.11) | copy-start | bytes 12292
  14.4 8.8 %copy-start.7 = (f32[4]{0:T(128)S(1)}, f32[4]{0:T(128)}, u32[]{:S(2)}) copy-start(f32[4]{0:T(128)} %param.12) | copy-start | bytes 52
  14.4 8.9 %copy-start.6 = (s32[2048]{0:T(1024)S(1)}, s32[2048]{0:T(1024)}, u32[]{:S(2)}) copy-start(s32[2048]{0:T(1024)} %param.8) | copy-start | bytes 24580
  57.5 15.8 %copy-start.1 = (f32[1024,2048]{1,0:T(8,128)}, f32[1024,2048]{1,0:T(8,128)S(1)}, u32[]{:S(2)}) copy-start(f32[1024,2048]{1,0:T(8,128)S(1)} %get-tuple-element.19) | copy-start | bytes 25165828
  57.5 3.7 %collective-permute-start = (f32[1024]{0:T(1024)S(1)}, f32[1024]{0:T(1024)S(1)}, u32[]{:S(2)}, u32[]{:S(2)}) collective-permute-start(f32[1024]{0:T(1024)S(1)} %get-tuple-element.18), channel_id=1, source_target_pairs={{0,32},{16,48},{32,0},{48,16},{64,96},{80,112},{96,64},{112,80},{1... | collective-permute-start | bytes 12296 | tf_op jit(solution)/shard_map/ppermute | solution.py:41
  61.2 5.1 %collective-permute-start.1 = (f32[1024]{0:T(1024)S(1)}, f32[1024]{0:T(1024)S(1)}, u32[]{:S(2)}, u32[]{:S(2)}) collective-permute-start(f32[1024]{0:T(1024)S(1)} %add.79), channel_id=1, source_target_pairs={{0,16},{16,0},{32,48},{48,32},{64,80},{80,64},{96,112},{112,96},{1... | collective-permute-start | bytes 12296 | tf_op jit(solution)/shard_map/ppermute | solution.py:41
  66.3 5.1 %collective-permute-start.2 = (f32[1024]{0:T(1024)S(1)}, f32[1024]{0:T(1024)S(1)}, u32[]{:S(2)}, u32[]{:S(2)}) collective-permute-start(f32[1024]{0:T(1024)S(1)} %add.80), channel_id=1, source_target_pairs={{0,64},{16,80},{32,96},{48,112},{64,0},{80,16},{96,32},{112,48},{1... | collective-permute-start | bytes 12296 | tf_op jit(solution)/shard_map/ppermute | solution.py:41
  73.2 2.0 copy-start.2
  96.4 15.8 %all-to-all-start.1 = ((f32[8,128,256]{2,1,0:T(8,128)}), f32[8,128,256]{2,1,0:T(8,128)S(1)}, u32[]{:S(2)}, u32[]{:S(2)}) async-start(f32[8,128,256]{2,1,0:T(8,128)} %broadcast_in_dim.76), calls=%async_computation.1 | async-start | bytes 2097152 | tf_op jit(solution)/shard_map/all_to_all | solution.py:117
  116.1 41.1 %copy-start.3 = (bf16[1024,2048]{1,0:T(8,128)(2,1)S(1)}, bf16[1024,2048]{1,0:T(8,128)(2,1)}, u32[]{:S(2)}) copy-start(bf16[1024,2048]{1,0:T(8,128)(2,1)} %copy-done.2) | copy-start | bytes 12582916
  184.3 17.8 %all-to-all-start.5 = ((f32[8,128,256]{2,1,0:T(8,128)}), f32[8,128,256]{2,1,0:T(8,128)S(1)}, u32[]{:S(2)}, u32[]{:S(2)}) async-start(f32[8,128,256]{2,1,0:T(8,128)} %broadcast_in_dim.80), calls=%async_computation.5 | async-start | bytes 2097152 | tf_op jit(solution)/shard_map/all_to_all | solution.py:117
  207.1 41.1 %copy-start.4 = (bf16[1024,2048]{1,0:T(8,128)(2,1)S(1)}, bf16[1024,2048]{1,0:T(8,128)(2,1)}, u32[]{:S(2)}) copy-start(bf16[1024,2048]{1,0:T(8,128)(2,1)} %copy-done.2) | copy-start | bytes 12582916
  272.9 17.8 %all-to-all-start.9 = ((f32[8,128,256]{2,1,0:T(8,128)}), f32[8,128,256]{2,1,0:T(8,128)S(1)}, u32[]{:S(2)}, u32[]{:S(2)}) async-start(f32[8,128,256]{2,1,0:T(8,128)} %broadcast_in_dim.84), calls=%async_computation.9 | async-start | bytes 2097152 | tf_op jit(solution)/shard_map/all_to_all | solution.py:117
Sparse Core Ops, SparseCore 0:
  9.7 39.8 all-gather.1

commit v12 on v4

--- a/solution.py
+++ b/solution.py
@@ -168,7 +168,7 @@
 
 
 def on_device(summaries, row_level, pool, pool_level, landmark_index, level_scale, targets):
-    sample_bits = partner_bits(lax.axis_size("sample"), (2, 1, 4, 8, 16, 32, 64))
+    sample_bits = partner_bits(lax.axis_size("sample"), (1, 2, 4, 8, 16, 32, 64))
     landmark_bits = partner_bits(lax.axis_size("landmark"), (1, 2, 4, 8, 16, 32, 64))
     row_count = summaries.shape[0]
     n_rows = row_count * lax.axis_size("sample")

time: 300 us -> 300 us (level)
  no operation moved by 1% of the time
where the time goes in v12:
time: 300 us; the launch traced here: 299 us
  blocking collectives  146 us (49%)
  waiting for transfers between devices  62 us (21%)
  local copies, waits for them, and re-layouts  25.1 us (8%)
  matrix products  18.5 us (6%)
  starting transfers between devices  18.1 us (6%)
  other arithmetic  14.8 us (5%)
  between operations  14.4 us (5%)
    all_to_all x5, blocking collectives, exchange_scatter(): got = lax.all_to_all(chunks, axis, 0, 0, tiled=False)  108 us
    all_to_all x2, blocking collectives, exchange_gather(): lax.all_to_all(jnp.broadcast_to(part[None], (size,) + part.shape), axis,...  38.1 us
    all_to_all x3, waiting for transfers between devices, exchange_gather(): lax.all_to_all(jnp.broadcast_to(part[None], (size,) + part.shape), axis,...  28.6 us
    all_gather x1, waiting for transfers between devices, on_device(): gathered = lax.all_gather(summaries, 'landmark', axis=1, tiled=True)  26.2 us
    all_to_all x3, starting transfers between devices, exchange_gather(): lax.all_to_all(jnp.broadcast_to(part[None], (size,) + part.shape), axis,...  10.7 us
    gather x1, local copies, waits for them, and re-layouts, on_device(): anchors = jnp.take(pool, landmark_index, axis=0)  8.79 us
    dot_general x1, matrix products, raw_block(): jnp.dot(summary_rows, anchors.T, preferred_element_type=jnp.float32)  7.88 us
    ppermute x3, starting transfers between devices, butterfly_sum(): x = x + lax.ppermute(x, axis, perm)  7.36 us
  transfers between devices with their start and end apart: 7, of which 7 were waited for; matrix products, arithmetic and copies ran while one was open for 9% of the time, Pallas kernels for 0%

profile of v12, /device:TPU:0, one launch (start us, length us, event | category | flops | bytes accessed | tf_op | source)
XLA Modules:
  0.0 299.4 jit_solution(3121421850026870584)
XLA Ops:
  7.2 0.0 copy-start
  7.2 0.0 all-gather.2.cloned.1.call-start
  7.2 0.7 all-gather.2.cloned.1.call-update
  7.9 0.7 fusion.12
  8.6 5.7 %gather_fusion.1 = s32[1024]{0:T(1024)S(1)} fusion(s32[2048]{0:T(1024)} %param.10, s32[1024]{0:T(1024)S(1)} %fusion.12), kind=kCustom, calls=%fused_computation.1 | custom fusion | bytes 12288 | tf_op jit(solution)/shard_map/jit(_take)/gather | solution.py:178
  14.3 0.0 copy-start.5
  14.4 0.0 copy-start.7
  14.4 0.0 copy-start.6
  14.4 8.8 %gather_fusion = bf16[1024,1024]{1,0:T(8,128)(2,1)} fusion(bf16[2048,1024]{1,0:T(8,128)(2,1)} %param.9, s32[1024]{0:T(1024)S(1)} %fusion.12), kind=kCustom, calls=%fused_computation | custom fusion | bytes 4198400 | tf_op jit(solution)/shard_map/jit(_take)/gather | solution.py:177
  23.2 0.0 copy-done.5
  23.2 0.0 copy-done.7
  23.2 0.1 select_reduce_fusion.1
  23.3 0.1 select_reduce_fusion
  23.4 26.2 %all-gather.2.cloned.1.call-done = bf16[2048,1024]{0,1:T(8,128)(2,1)} async-done(((bf16[2048,64]{0,1:T(8,128)(2,1)}), bf16[2048,1024]{0,1:T(8,128)(2,1)}) %all-gather.2.cloned.1.call-update) | async-done | bytes 4194320 | tf_op jit(solution)/shard_map/all_gather | solution.py:175
  49.6 7.9 %fusion = (f32[1024]{0:T(1024)S(1)}, f32[1024,2048]{1,0:T(8,128)S(1)}) fusion(f32[1024]{0:T(1024)S(1)} %broadcast_divide_fusion.1, f32[2048]{0:T(1024)S(1)} %broadcast_divide_fusion, bf16[2048,1024]{0,1:T(8,128)(2,1)} %all-gather.2.cloned.1.call-done, bf16[1024,1024]{1,0:T(8,128)(2,1)} %gather_fusion, pred[1024]{0:T(1024)(128)(4,1)S(1)} %get-tuple-element.5), kind=kOutput, calls=%fused_computation.4 | convolution fusion | flops 4302306304 | bytes 14697472 | tf_op jit(solution)/shard_map/dot_general | solution.py:27
  57.5 0.0 copy-start.1
  57.5 2.9 collective-permute-start
  60.4 2.3 collective-permute-done
  62.7 1.5 collective-permute-start.1
  64.2 2.1 collective-permute-done.1
  66.3 3.0 collective-permute-start.2
  69.3 2.1 collective-permute-done.2
  71.4 1.8 subtract_convert_fusion
  73.3 1.3 fusion.25
  74.5 0.7 copy-done.2
  75.2 20.1 %all_to_all.50 = f32[8,128,256]{2,1,0:T(8,128)S(1)} all-to-all(f32[8,128,256]{2,1,0:T(8,128)S(1)} %bitcast.74), channel_id=1, replica_groups=mesh['sample'=8,'landmark'=16] {'sample'}, dimensions={0} | all-to-all | bytes 2097152 | tf_op jit(solution)/shard_map/all_to_all | solution.py:105
  95.3 0.1 reduce_sum.124
  95.4 1.1 broadcast_in_dim.76
  96.4 3.6 %all-to-all-start.1 = ((f32[8,128,256]{2,1,0:T(8,128)}), f32[8,128,256]{2,1,0:T(8,128)S(1)}, u32[]{:S(2)}, u32[]{:S(2)}) async-start(f32[8,128,256]{2,1,0:T(8,128)} %broadcast_in_dim.76), calls=%async_computation.1 | async-start | bytes 2097152 | tf_op jit(solution)/shard_map/all_to_all | solution.py:115
  100.0 5.6 %fusion.39 = bf16[2048,1024]{0,1:T(8,128)(2,1)} fusion(f32[1024]{0:T(1024)S(1)} %add_multiply_fusion, f32[1024]{0:T(1024)S(1)} %broadcast_divide_fusion.1, f32[1024,2048]{1,0:T(8,128)} %copy-done.1, f32[2048]{0:T(1024)S(1)} %broadcast_divide_fusion), kind=kLoop, calls=%fused_computation.89 | loop fusion | flops 8388608 | bytes 12599296 | tf_op jit(solution)/shard_map/sub | solution.py:183
  105.6 6.4 %copy.15 = bf16[2048,1024]{1,0:T(8,128)(2,1)} copy(bf16[2048,1024]{0,1:T(8,128)(2,1)} %fusion.39) | data formatting | bytes 8388608 | tf_op jit(solution)/shard_map/dot_general | solution.py:136
  112.0 0.2 all-to-all-done.1
  112.2 0.2 multiply_convert_fusion
  112.5 3.4 %convolution_convert_fusion.1 = bf16[16,128,256]{2,1,0:T(8,128)(2,1)S(1)} fusion(bf16[16,128,1024]{2,1,0:T(8,128)(2,1)} %bitcast.70, bf16[1024,256,1]{1,0,2:T(8,128)(2,1)S(1)} %bitcast.75), kind=kOutput, calls=%fused_computation.13 | convolution fusion | flops 1074266112 | bytes 5767168 | tf_op jit(solution)/shard_map/dot_general | solution.py:136
  116.0 0.1 pad_maximum_fusion
  116.1 20.7 %all_to_all.51 = bf16[16,134,256]{2,1,0:T(8,128)(2,1)S(1)} all-to-all(bf16[16,134,256]{2,1,0:T(8,128)(2,1)S(1)} %pad_maximum_fusion), channel_id=1, replica_groups=mesh['sample'=8,'landmark'=16] {'landmark'}, dimensions={0} | all-to-all | bytes 2195456 | tf_op jit(solution)/shard_map/all_to_all | solution.py:105
  136.8 0.2 convert_reduce_fusion.1
  136.9 0.1 broadcast_in_dim.78
  137.0 19.1 %all_to_all.52 = bf16[16,128,256]{2,1,0:T(8,128)(2,1)S(1)} all-to-all(bf16[16,128,256]{2,1,0:T(8,128)(2,1)S(1)} %broadcast_in_dim.78), channel_id=1, replica_groups=mesh['sample'=8,'landmark'=16] {'landmark'}, dimensions={0} | all-to-all | bytes 2097152 | tf_op jit(solution)/shard_map/all_to_all | solution.py:115
  156.1 1.2 fusion.26
  157.4 0.3 multiply_reduce_fusion.1
  157.7 0.1 pad_maximum_fusion.1
  157.8 24.7 %all_to_all.53 = f32[8,129,256]{2,1,0:T(8,128)S(1)} all-to-all(f32[8,129,256]{2,1,0:T(8,128)S(1)} %pad_maximum_fusion.1), channel_id=1, replica_groups=mesh['sample'=8,'landmark'=16] {'sample'}, dimensions={0} | all-to-all | bytes 2113536 | tf_op jit(solution)/shard_map/all_to_all | solution.py:105
  182.4 0.1 reduce_sum.128
  182.5 1.1 broadcast_in_dim.80
  183.6 3.6 %all-to-all-start.5 = ((f32[8,128,256]{2,1,0:T(8,128)}), f32[8,128,256]{2,1,0:T(8,128)S(1)}, u32[]{:S(2)}, u32[]{:S(2)}) async-start(f32[8,128,256]{2,1,0:T(8,128)} %broadcast_in_dim.80), calls=%async_computation.5 | async-start | bytes 2097152 | tf_op jit(solution)/shard_map/all_to_all | solution.py:115
  187.2 14.2 %all-to-all-done.5 = f32[8,128,256]{2,1,0:T(8,128)S(1)} async-done(((f32[8,128,256]{2,1,0:T(8,128)}), f32[8,128,256]{2,1,0:T(8,128)S(1)}, u32[]{:S(2)}, u32[]{:S(2)}) %all-to-all-start.5) | async-done | bytes 1048608 | tf_op jit(solution)/shard_map/all_to_all | solution.py:115
  201.4 1.3 multiply_reduce_fusion.3
  202.7 3.4 %convolution_convert_fusion = bf16[16,128,256]{2,1,0:T(8,128)(2,1)S(1)} fusion(bf16[16,128,1024]{2,1,0:T(8,128)(2,1)} %bitcast.71, bf16[1024,256,1]{1,0,2:T(8,128)(2,1)S(1)} %bitcast.76), kind=kOutput, calls=%fused_computation.12 | convolution fusion | flops 1074266112 | bytes 5767168 | tf_op jit(solution)/shard_map/dot_general | solution.py:144
  206.3 0.1 pad_maximum_fusion.2
  206.3 21.0 %all_to_all.54 = bf16[16,134,256]{2,1,0:T(8,128)(2,1)S(1)} all-to-all(bf16[16,134,256]{2,1,0:T(8,128)(2,1)S(1)} %pad_maximum_fusion.2), channel_id=1, replica_groups=mesh['sample'=8,'landmark'=16] {'landmark'}, dimensions={0} | all-to-all | bytes 2195456 | tf_op jit(solution)/shard_map/all_to_all | solution.py:105
  227.3 0.2 convert_reduce_fusion
  227.5 0.1 broadcast_in_dim.82
  227.6 19.1 %all_to_all.55 = bf16[16,128,256]{2,1,0:T(8,128)(2,1)S(1)} all-to-all(bf16[16,128,256]{2,1,0:T(8,128)(2,1)S(1)} %broadcast_in_dim.82), channel_id=1, replica_groups=mesh['sample'=8,'landmark'=16] {'landmark'}, dimensions={0} | all-to-all | bytes 2097152 | tf_op jit(solution)/shard_map/all_to_all | solution.py:115
  246.7 1.3 fusion.27
  248.0 0.3 multiply_reduce_fusion
  248.3 0.1 pad_maximum_fusion.3
  248.4 21.9 %all_to_all.56 = f32[8,129,256]{2,1,0:T(8,128)S(1)} all-to-all(f32[8,129,256]{2,1,0:T(8,128)S(1)} %pad_maximum_fusion.3), channel_id=1, replica_groups=mesh['sample'=8,'landmark'=16] {'sample'}, dimensions={0} | all-to-all | bytes 2113536 | tf_op jit(solution)/shard_map/all_to_all | solution.py:105
  270.3 0.1 reduce_sum.133
  270.4 1.1 broadcast_in_dim.133
  271.4 3.6 %all-to-all-start.9 = ((f32[8,128,256]{2,1,0:T(8,128)}), f32[8,128,256]{2,1,0:T(8,128)S(1)}, u32[]{:S(2)}, u32[]{:S(2)}) async-start(f32[8,128,256]{2,1,0:T(8,128)} %broadcast_in_dim.133), calls=%async_computation.9 | async-start | bytes 2097152 | tf_op jit(solution)/shard_map/all_to_all | solution.py:115
  275.1 14.2 %all-to-all-done.9 = f32[8,128,256]{2,1,0:T(8,128)S(1)} async-done(((f32[8,128,256]{2,1,0:T(8,128)}), f32[8,128,256]{2,1,0:T(8,128)S(1)}, u32[]{:S(2)}, u32[]{:S(2)}) %all-to-all-start.9) | async-done | bytes 1048608 | tf_op jit(solution)/shard_map/all_to_all | solution.py:115
  289.3 0.1 broadcast_multiply_fusion
  289.3 3.2 %fusion.5 = (f32[1024,256]{1,0:T(8,128)}, f32[1024,256]{1,0:T(8,128)}) fusion(f32[8,128,256]{2,1,0:T(8,128)S(1)} %broadcast_multiply_fusion, f32[256]{0:T(256)S(1)} %broadcast_multiply_fusion.2, f32[8,128,256]{2,1,0:T(8,128)S(1)} %all-to-all-done.1, f32[8,128,256]{2,1,0:T(8,128)} %get-tuple-element.9, f32[256]{0:T(256)S(1)} %bitcast.81, f32[256]{0:T(256)S(1)} %bitcast.82, ...), kind=kLoop, calls=%fused_computation.20 | loop fusion | flops 3670016 | bytes 5246976 | tf_op jit(solution)/shard_map/sub | solution.py:166
  (37 shorter events, 0.3 us)
Async XLA Ops:
  7.2 66.1 %copy-start = (bf16[2048,256]{1,0:T(8,128)(2,1)S(1)}, bf16[2048,256]{1,0:T(8,128)(2,1)}, u32[]{:S(2)}) copy-start(bf16[2048,256]{1,0:T(8,128)(2,1)} %param.13) | copy-start | bytes 3145732
  7.2 42.4 %all-gather.2.cloned.1.call-start = ((), (), s32[]{:S(2)}) async-start(), calls=%async_computation.10 | async-start | bytes 4456448 | tf_op jit(solution)/shard_map/all_gather | solution.py:175
  14.3 8.8 %copy-start.5 = (s32[1024]{0:T(1024)S(1)}, s32[1024]{0:T(1024)}, u32[]{:S(2)}) copy-start(s32[1024]{0:T(1024)} %param.11) | copy-start | bytes 12292
  14.4 8.8 %copy-start.7 = (f32[4]{0:T(128)S(1)}, f32[4]{0:T(128)}, u32[]{:S(2)}) copy-start(f32[4]{0:T(128)} %param.12) | copy-start | bytes 52
  14.4 8.9 %copy-start.6 = (s32[2048]{0:T(1024)S(1)}, s32[2048]{0:T(1024)}, u32[]{:S(2)}) copy-start(s32[2048]{0:T(1024)} %param.8) | copy-start | bytes 24580
  57.5 15.8 %copy-start.1 = (f32[1024,2048]{1,0:T(8,128)}, f32[1024,2048]{1,0:T(8,128)S(1)}, u32[]{:S(2)}) copy-start(f32[1024,2048]{1,0:T(8,128)S(1)} %get-tuple-element.19) | copy-start | bytes 25165828
  57.5 5.2 %collective-permute-start = (f32[1024]{0:T(1024)S(1)}, f32[1024]{0:T(1024)S(1)}, u32[]{:S(2)}, u32[]{:S(2)}) collective-permute-start(f32[1024]{0:T(1024)S(1)} %get-tuple-element.18), channel_id=1, source_target_pairs={{0,16},{16,0},{32,48},{48,32},{64,80},{80,64},{96,112},{112,96},{1... | collective-permute-start | bytes 12296 | tf_op jit(solution)/shard_map/ppermute | solution.py:41
  62.7 3.6 %collective-permute-start.1 = (f32[1024]{0:T(1024)S(1)}, f32[1024]{0:T(1024)S(1)}, u32[]{:S(2)}, u32[]{:S(2)}) collective-permute-start(f32[1024]{0:T(1024)S(1)} %add.71), channel_id=1, source_target_pairs={{0,32},{16,48},{32,0},{48,16},{64,96},{80,112},{96,64},{112,80},{1... | collective-permute-start | bytes 12296 | tf_op jit(solution)/shard_map/ppermute | solution.py:41
  66.3 5.1 %collective-permute-start.2 = (f32[1024]{0:T(1024)S(1)}, f32[1024]{0:T(1024)S(1)}, u32[]{:S(2)}, u32[]{:S(2)}) collective-permute-start(f32[1024]{0:T(1024)S(1)} %add.72), channel_id=1, source_target_pairs={{0,64},{16,80},{32,96},{48,112},{64,0},{80,16},{96,32},{112,48},{1... | collective-permute-start | bytes 12296 | tf_op jit(solution)/shard_map/ppermute | solution.py:41
  73.2 2.0 copy-start.2
  96.4 15.8 %all-to-all-start.1 = ((f32[8,128,256]{2,1,0:T(8,128)}), f32[8,128,256]{2,1,0:T(8,128)S(1)}, u32[]{:S(2)}, u32[]{:S(2)}) async-start(f32[8,128,256]{2,1,0:T(8,128)} %broadcast_in_dim.76), calls=%async_computation.1 | async-start | bytes 2097152 | tf_op jit(solution)/shard_map/all_to_all | solution.py:115
  116.0 40.1 %copy-start.3 = (bf16[1024,2048]{1,0:T(8,128)(2,1)S(1)}, bf16[1024,2048]{1,0:T(8,128)(2,1)}, u32[]{:S(2)}) copy-start(bf16[1024,2048]{1,0:T(8,128)(2,1)} %copy-done.2) | copy-start | bytes 12582916
  183.6 17.8 %all-to-all-start.5 = ((f32[8,128,256]{2,1,0:T(8,128)}), f32[8,128,256]{2,1,0:T(8,128)S(1)}, u32[]{:S(2)}, u32[]{:S(2)}) async-start(f32[8,128,256]{2,1,0:T(8,128)} %broadcast_in_dim.80), calls=%async_computation.5 | async-start | bytes 2097152 | tf_op jit(solution)/shard_map/all_to_all | solution.py:115
  206.2 40.5 %copy-start.4 = (bf16[1024,2048]{1,0:T(8,128)(2,1)S(1)}, bf16[1024,2048]{1,0:T(8,128)(2,1)}, u32[]{:S(2)}) copy-start(bf16[1024,2048]{1,0:T(8,128)(2,1)} %copy-done.2) | copy-start | bytes 12582916
  271.4 17.8 %all-to-all-start.9 = ((f32[8,128,256]{2,1,0:T(8,128)}), f32[8,128,256]{2,1,0:T(8,128)S(1)}, u32[]{:S(2)}, u32[]{:S(2)}) async-start(f32[8,128,256]{2,1,0:T(8,128)} %broadcast_in_dim.133), calls=%async_computation.9 | async-start | bytes 2097152 | tf_op jit(solution)/shard_map/all_to_all | solution.py:115
Sparse Core Ops, SparseCore 0:
  9.7 39.8 all-gather.1
